TPU v7x, 128 devices: a whole 4x4x4 slice. The times are simulated.
128 devices in a mesh: head: 4 (over y), tile: 32 (over x, z, core).
Axes of the slice: x: 4, y: 4, z: 4, core: 2. Of those that a mesh axis runs over, the one named last changes fastest.
Arguments:
- hidden: bfloat16 [32, 384, 1536], P(None, ('head', 'tile')), may hold values from -6 to 6
- latent: float32 [32, 384, 64], P(None, ('head', 'tile')), may hold values from -6 to 6
- cell_map: int32 [32, 384], P(None, ('head', 'tile')), may hold values from 0 to 383, each once within a row
- text_lengths: int32 [32], P('tile'), may hold values from 64 to 512, as said below
- block_modulation: float32 [32, 3, 1536], replicated, may hold values from -3 to 3
- head_modulation: float32 [32, 2, 1536], replicated, may hold values from -3 to 3
- step_sizes: float32 [32], replicated, may hold values from -0.5 to -0.1
- w_qkv: bfloat16 [1536, 4608], replicated, may hold values from -0.15625 to 0.15625
- self_q_gain: float32 [1536], replicated, may hold values from 0.5 to 2
- self_k_gain: float32 [1536], replicated, may hold values from 0.5 to 2
- w_out: bfloat16 [1536, 1536], replicated, may hold values from -0.15625 to 0.15625
- cross_gain: float32 [1536], replicated, may hold values from 0.1 to 1.9
- cross_wq: bfloat16 [1536, 1536], P(None, 'head'), may hold values from -0.15625 to 0.15625
- cross_q_gain: float32 [1536], P('head'), may hold values from 0.5 to 2
- text_keys: bfloat16 [32, 512, 1536], P('tile', None, 'head'), may hold values from -2.5 to 2.5
- text_values: bfloat16 [32, 512, 1536], P('tile', None, 'head'), may hold values from -4 to 4
- cross_wo: bfloat16 [1536, 1536], P('head'), may hold values from -0.15625 to 0.15625
- head_w: bfloat16 [1536, 64], replicated, may hold values from -0.15625 to 0.15625
Outputs:
- hidden_next: bfloat16 [32, 384, 1536], P(None, ('head', 'tile'))
- latent_next: float32 [32, 384, 64], P(None, ('head', 'tile'))
Inputs may be any that keep to these rules, and one draw needn't show every extreme that they name: Each row cell_map[v] names every cell of video v once. Text positions from text_lengths[v] on are padding of video v.
All inputs are finite; a program needn't handle non-finite values.
Results may differ from a plain program's by a relative error of at most 0.007.
Values may be sent and summed in bfloat16 or wider, within the bound.
No kernel may reach another device: no remote copies, remote signals or barrier semaphores. Data moves between devices by JAX's collectives and lax.ppermute only.
A program may use at most 128 MiB of HBM per device.

v0:
```python
import math

import jax
import jax.numpy as jnp
from jax import lax
from jax.sharding import PartitionSpec as P

HEADS = 12
HEAD_DIM = 128
GRID_H = 24
GRID_W = 8


EPSILON = 1e-06


def layer_norm(inputs):
    average = jnp.mean(inputs, axis=-1, keepdims=True)
    centred = inputs - average
    variance = jnp.mean(centred * centred, axis=-1, keepdims=True)
    return centred * lax.rsqrt(variance + EPSILON)


def head_norm(inputs, gain_table):
    mean_square = jnp.mean(inputs * inputs, axis=-1, keepdims=True)
    return inputs * lax.rsqrt(mean_square + EPSILON) * gain_table


def frequencies(pair_count):
    return jnp.power(10000.0, -jnp.arange(pair_count, dtype=jnp.float32) / pair_count)


def rope_angles(cell_ids):
    sixth_part = HEAD_DIM // 6
    time_pairs = HEAD_DIM // 2 - 2 * sixth_part
    plane_cells = GRID_H * GRID_W
    frame_index = (cell_ids // plane_cells).astype(jnp.float32)
    row_index = (cell_ids // GRID_W % GRID_H).astype(jnp.float32)
    column = (cell_ids % GRID_W).astype(jnp.float32)
    return jnp.concatenate(
        [
            frame_index[..., None] * frequencies(time_pairs),
            row_index[..., None] * frequencies(sixth_part),
            column[..., None] * frequencies(sixth_part),
        ],
        axis=-1,
    )


def rotate(inputs, angles):
    half_dim = inputs.shape[-1] // 2
    cosine = jnp.cos(angles)[..., None, :]
    sine_part = jnp.sin(angles)[..., None, :]
    lower_half = inputs[..., :half_dim]
    upper_half = inputs[..., half_dim:]
    return jnp.concatenate(
        [
            lower_half * cosine - upper_half * sine_part,
            lower_half * sine_part + upper_half * cosine,
        ],
        axis=-1,
    )


def attend_self(queries, keys_own, values_own):
    factor = 1.0 / math.sqrt(queries.shape[-1])
    token_total = queries.shape[0]

    def one_block(block_queries):
        scores = (
            jnp.einsum("qhd,khd->hqk", block_queries, keys_own, preferred_element_type=jnp.float32)
            * factor
        )
        weights = jnp.exp(scores)
        totals = jnp.sum(weights, axis=-1)
        mixture = jnp.einsum(
            "hqk,khd->qhd",
            weights.astype(jnp.bfloat16),
            values_own,
            preferred_element_type=jnp.float32,
        )
        return (mixture / jnp.transpose(totals)[:, :, None]).astype(jnp.bfloat16)

    blocked = queries.reshape((token_total // token_total, token_total) + queries.shape[1:])
    return lax.map(one_block, blocked).reshape(queries.shape)


def attend_text(queries, keys_own, values_own, length):
    factor = 1.0 / math.sqrt(queries.shape[-1])
    live_mask = (jnp.arange(keys_own.shape[0]) < length).astype(jnp.float32)
    scores = (
        jnp.einsum("qhd,khd->hqk", queries, keys_own, preferred_element_type=jnp.float32) * factor
    )
    weights = jnp.exp(scores) * live_mask
    totals = jnp.sum(weights, axis=-1)
    mixture = jnp.einsum(
        "hqk,khd->qhd", weights.astype(jnp.bfloat16), values_own, preferred_element_type=jnp.float32
    )
    return (mixture / jnp.transpose(totals)[:, :, None]).astype(jnp.bfloat16)


def pack_projected(block_in, cell_map, w_qkv, self_q_gain, self_k_gain, head_count):
    videos, per_video, model_width = block_in.shape
    projected = jnp.dot(
        block_in.reshape(-1, model_width), w_qkv, preferred_element_type=jnp.float32
    )
    projected = projected.reshape(videos, per_video, 3, HEADS, HEAD_DIM)
    angles = rope_angles(cell_map)
    queries = rotate(
        head_norm(projected[:, :, 0], self_q_gain.reshape(HEADS, HEAD_DIM)), angles
    ).astype(jnp.bfloat16)
    keys_all = rotate(
        head_norm(projected[:, :, 1], self_k_gain.reshape(HEADS, HEAD_DIM)), angles
    ).astype(jnp.bfloat16)
    values_all = projected[:, :, 2].astype(jnp.bfloat16)
    packed = jnp.stack([queries, keys_all, values_all], axis=2)
    group_width = model_width // head_count
    packed = packed.reshape(videos, per_video, 3, head_count, group_width).transpose(3, 0, 1, 2, 4)
    return packed.reshape(head_count, videos, per_video, 3 * group_width)


def local(
    hidden,
    latent,
    cell_map,
    text_lengths,
    block_modulation,
    head_modulation,
    step_sizes,
    w_qkv,
    self_q_gain,
    self_k_gain,
    w_out,
    cross_gain,
    cross_wq,
    cross_q_gain,
    text_keys,
    text_values,
    cross_wo,
    head_w,
):
    head_count = lax.axis_size("head")
    tile_count = lax.axis_size("tile")
    videos, per_video, model_width = hidden.shape
    group_heads = HEADS // head_count
    group_width = group_heads * HEAD_DIM
    stream = hidden.astype(jnp.float32)
    block_shift = block_modulation[:, 0][:, None, :]
    block_scale = block_modulation[:, 1][:, None, :]
    block_gate = block_modulation[:, 2][:, None, :]
    block_in = (layer_norm(stream) * (1.0 + block_scale) + block_shift).astype(jnp.bfloat16)
    packed = pack_projected(block_in, cell_map, w_qkv, self_q_gain, self_k_gain, head_count)
    arrived = lax.all_to_all(
        packed.reshape(head_count * videos, per_video, 3 * group_width),
        ("head", "tile"),
        split_axis=0,
        concat_axis=0,
        tiled=True,
    )
    arrived = arrived.reshape(-1, 3, group_heads, HEAD_DIM)
    own_queries = arrived[:, 0]
    own_keys = arrived[:, 1]
    own_values = arrived[:, 2]
    own_mixture = attend_self(own_queries, own_keys, own_values)
    returned = lax.all_to_all(
        own_mixture.reshape(head_count * tile_count, per_video, group_width),
        ("head", "tile"),
        split_axis=0,
        concat_axis=0,
        tiled=True,
    )
    attended = (
        returned.reshape(head_count, videos, per_video, group_width)
        .transpose(1, 2, 0, 3)
        .reshape(videos * per_video, model_width)
    )
    self_update = jnp.dot(attended, w_out, preferred_element_type=jnp.float32).reshape(
        videos, per_video, model_width
    )
    after_self = stream + block_gate * self_update
    cross_in = (layer_norm(after_self) * cross_gain).astype(jnp.bfloat16)
    copies = jnp.broadcast_to(cross_in[None], (head_count,) + cross_in.shape).reshape(
        head_count * videos, per_video, model_width
    )
    owner_cross = lax.all_to_all(copies, ("head", "tile"), split_axis=0, concat_axis=0, tiled=True)
    owner_cross = owner_cross.reshape(-1, model_width)
    cross_queries = jnp.dot(owner_cross, cross_wq, preferred_element_type=jnp.float32).reshape(
        -1, group_heads, HEAD_DIM
    )
    cross_queries = head_norm(cross_queries, cross_q_gain.reshape(group_heads, HEAD_DIM)).astype(
        jnp.bfloat16
    )
    own_text_keys = text_keys[0].reshape(-1, group_heads, HEAD_DIM)
    own_text_values = text_values[0].reshape(-1, group_heads, HEAD_DIM)
    cross_mixture = attend_text(
        cross_queries, own_text_keys, own_text_values, text_lengths[0]
    ).reshape(-1, group_width)
    summed = lax.psum_scatter(
        jnp.dot(cross_mixture, cross_wo, preferred_element_type=jnp.float32).astype(jnp.bfloat16),
        "head",
        scatter_dimension=0,
        tiled=True,
    )
    cross_out = summed.reshape(tile_count, per_video, model_width)
    returned_cross = lax.all_to_all(cross_out, "tile", split_axis=0, concat_axis=0, tiled=True)
    after_cross = after_self + returned_cross.astype(jnp.float32)
    hidden_next = after_cross.astype(jnp.bfloat16)
    head_shift = head_modulation[:, 0][:, None, :]
    head_scale = head_modulation[:, 1][:, None, :]
    head_in = (layer_norm(after_cross) * (1.0 + head_scale) + head_shift).astype(jnp.bfloat16)
    velocity = jnp.dot(
        head_in.reshape(-1, model_width), head_w, preferred_element_type=jnp.float32
    ).reshape(videos, per_video, -1)
    latent_next = latent + step_sizes[:, None, None] * velocity
    return (hidden_next, latent_next)


def solution(mesh):
    return jax.shard_map(
        local,
        mesh=mesh,
        in_specs=(
            P(None, ("head", "tile"), None),
            P(None, ("head", "tile"), None),
            P(None, ("head", "tile")),
            P("tile"),
            P(),
            P(),
            P(),
            P(),
            P(),
            P(),
            P(),
            P(),
            P(None, "head"),
            P("head"),
            P("tile", None, "head"),
            P("tile", None, "head"),
            P("head", None),
            P(),
        ),
        out_specs=(P(None, ("head", "tile"), None), P(None, ("head", "tile"), None)),
        check_vma=False,
    )
```

profile of v0, /device:TPU:1, one launch (start us, length us, event | category | flops | bytes accessed | tf_op | source)
XLA Modules:
  0.0 187.5 jit_solution(6854522850857029256)
XLA Ops:
  7.2 1.9 %slice_bitcast_fusion.3 = (f32[32,1536]{1,0:T(8,128)}, f32[32,1536]{1,0:T(8,128)S(1)}, f32[32,1536]{1,0:T(8,128)S(1)}) fusion(f32[32,3,1536]{2,0,1:T(8,128)} %param.22), kind=kLoop, calls=%fused_computation.79 | loop fusion | flops 49152 | bytes 1179648 | tf_op jit(solution)/shard_map/mul | solution.py:180
  9.1 1.1 convert_reduce_fusion
  10.2 1.2 fusion.24
  11.4 18.6 %copy.53 = bf16[1536,4608]{0,1:T(8,128)(2,1)} copy(bf16[1536,4608]{1,0:T(8,128)(2,1)} %param.25) | data formatting | bytes 28311552 | tf_op args[7]
  30.1 7.6 %fusion.34 = f32[32,3,3,12,128]{4,0,3,2,1:T(8,128)S(1)} fusion(bf16[3,12,128,1536,1]{3,2,1,0,4:T(8,128)(2,1)} %bitcast.115, bf16[32,3,1536]{2,0,1:T(8,128)(2,1)S(1)} %copy-done.1, f32[32,1536]{1,0:T(8,128)S(1)} %get-tuple-element.31, f32[32,1536]{1,0:T(8,128)S(1)} %get-tuple-element.32, f32[32,3]{0,1:T(4,128)S(1)} %add_rsqrt_fusion.5, ...), kind=kOutput, calls=%fused_computation.55 | convolution fusion | flops 1359839232 | bytes 16614144 | tf_op jit(solution)/shard_map/dot_general | solution.py:104
  39.3 0.5 fusion.28
  41.2 0.7 maximum_bitcast_fusion
  42.0 0.8 copy.79
  42.7 0.8 reshape.204
  43.6 31.9 %all_to_all.20 = bf16[128,3,1152]{2,1,0:T(4,128)(2,1)S(1)} all-to-all(bf16[128,3,1152]{2,1,0:T(4,128)(2,1)S(1)} %reshape.204), channel_id=1, replica_groups=mesh['head'=4,'tile'=32] {'head','tile'}, dimensions={0} | all-to-all | bytes 1769472 | tf_op jit(solution)/shard_map/all_to_all | solution.py:153
  75.4 0.8 reshape.193
  77.0 0.4 fusion.10
  77.4 0.4 fusion.15
  78.4 16.4 %all_to_all.21 = bf16[128,3,384]{2,1,0:T(4,128)(2,1)S(1)} all-to-all(bf16[128,3,384]{2,1,0:T(4,128)(2,1)S(1)} %reshape_reshape.7), channel_id=1, replica_groups=mesh['head'=4,'tile'=32] {'head','tile'}, dimensions={0} | all-to-all | bytes 589824 | tf_op jit(solution)/shard_map/all_to_all | solution.py:165
  95.2 3.3 %fusion.64 = (f32[32,3]{0,1:T(4,128)S(1)}, f32[32,3,1536]{2,0,1:T(8,128)S(1)}) fusion(bf16[32,3,1536]{2,0,1:T(8,128)(2,1)S(1)} %dot_general.44, bf16[1536,1536]{1,0:T(8,128)(2,1)} %param.28, f32[32,1536]{1,0:T(8,128)S(1)} %copy-done.4, bf16[32,3,1536]{2,0,1:T(8,128)(2,1)S(1)} %copy-done.2), kind=kOutput, calls=%fused_computation.120 | convolution fusion | flops 453574560 | bytes 6095232 | tf_op jit(solution)/shard_map/dot_general | solution.py:177
  99.2 1.6 broadcast_in_dim.5
  100.8 4.6 %all-to-all-start.2 = ((bf16[128,3,1536]{2,1,0:T(4,128)(2,1)}), bf16[128,3,1536]{2,1,0:T(4,128)(2,1)S(1)}, u32[]{:S(2)}, u32[]{:S(2)}) async-start(bf16[128,3,1536]{2,1,0:T(4,128)(2,1)} %bitcast.116), calls=%async_computation.2 | async-start | bytes 3145728 | tf_op jit(solution)/shard_map/all_to_all | solution.py:185
  105.5 2.4 %copy.67 = bf16[1536,384]{0,1:T(8,128)(2,1)} copy(bf16[1536,384]{1,0:T(8,128)(2,1)} %param.30) | data formatting | bytes 2359296 | tf_op args[12]
  108.5 1.9 %copy.68 = bf16[1,512,384]{1,2,0:T(8,128)(2,1)} copy(bf16[1,512,384]{2,1,0:T(8,128)(2,1)} %param.32) | data formatting | bytes 786432 | tf_op args[14]
  110.4 1.9 %copy.71 = bf16[1,512,384]{1,2,0:T(8,128)(2,1)} copy(bf16[1,512,384]{2,1,0:T(8,128)(2,1)} %param.33) | data formatting | bytes 786432 | tf_op args[15]
  112.4 17.9 %all-to-all-done.2 = bf16[128,3,1536]{2,1,0:T(4,128)(2,1)S(1)} async-done(((bf16[128,3,1536]{2,1,0:T(4,128)(2,1)}), bf16[128,3,1536]{2,1,0:T(4,128)(2,1)S(1)}, u32[]{:S(2)}, u32[]{:S(2)}) %all-to-all-start.2) | async-done | bytes 1179680 | tf_op jit(solution)/shard_map/all_to_all | solution.py:185
  130.3 2.2 %reshape.202 = bf16[384,1536,1]{1,0,2:T(8,128)(2,1)} reshape(bf16[128,3,1536]{2,1,0:T(4,128)(2,1)S(1)} %all-to-all-done.2) | data formatting | bytes 2359296 | tf_op jit(solution)/shard_map/reshape | solution.py:186
  132.4 2.5 %multiply_reduce_fusion.1 = (f32[384,3]{0,1:T(4,128)S(1)}, f32[384,3,128]{0,2,1:T(8,128)S(1)}) fusion(bf16[384,1536,1]{1,0,2:T(8,128)(2,1)} %reshape.202, bf16[3,128,1536]{2,1,0:T(8,128)(2,1)} %bitcast.119), kind=kOutput, calls=%fused_computation.38 | convolution fusion | flops 453278592 | bytes 2953728 | tf_op jit(solution)/shard_map/dot_general | solution.py:187
  135.0 0.8 fusion.8
  135.9 0.6 fusion.14
  136.5 1.8 convolution_convert_fusion
  138.7 18.7 %reduce-scatter.2.cloned.1.call-done = bf16[96,1536]{1,0:T(8,128)(2,1)} async-done(((bf16[384,1536]{1,0:T(8,128)(2,1)}), bf16[96,1536]{1,0:T(8,128)(2,1)}) %reduce-scatter.2.cloned.1.call-update) | async-done | bytes 294928 | tf_op jit(solution)/shard_map/reduce_scatter | solution.py:198
  157.4 1.9 %reshape.198 = bf16[32,3,1536]{2,1,0:T(4,128)(2,1)} reshape(bf16[96,1536]{1,0:T(8,128)(2,1)} %reduce-scatter.2.cloned.1.call-done) | data formatting | bytes 589824 | tf_op jit(solution)/shard_map/reshape | solution.py:204
  159.3 9.1 %all-to-all-start.3 = ((bf16[32,3,1536]{2,1,0:T(4,128)(2,1)}), bf16[32,3,1536]{2,1,0:T(4,128)(2,1)S(1)}, u32[]{:S(2)}, u32[]{:S(2)}) async-start(bf16[32,3,1536]{2,1,0:T(4,128)(2,1)} %reshape.198), calls=%async_computation.4 | async-start | bytes 786432 | tf_op jit(solution)/shard_map/all_to_all | solution.py:205
  168.4 10.3 %all-to-all-done.3 = bf16[32,3,1536]{2,1,0:T(4,128)(2,1)S(1)} async-done(((bf16[32,3,1536]{2,1,0:T(4,128)(2,1)}), bf16[32,3,1536]{2,1,0:T(4,128)(2,1)S(1)}, u32[]{:S(2)}, u32[]{:S(2)}) %all-to-all-start.3) | async-done | bytes 294944 | tf_op jit(solution)/shard_map/all_to_all | solution.py:205
  178.8 0.9 multiply_reduce_fusion
  179.7 0.9 fusion.19
  (70 shorter events, 5.9 us)
Async XLA Ops:
  7.2 129.3 %copy-start = (bf16[384,1536]{1,0:T(8,128)(2,1)S(1)}, bf16[384,1536]{1,0:T(8,128)(2,1)}, u32[]{:S(2)}) copy-start(bf16[384,1536]{1,0:T(8,128)(2,1)} %param.34) | copy-start | bytes 3538948
  11.4 18.7 %copy-start.1 = (bf16[32,3,1536]{2,0,1:T(8,128)(2,1)S(1)}, bf16[32,3,1536]{2,0,1:T(8,128)(2,1)}, u32[]{:S(2)}) copy-start(bf16[32,3,1536]{2,0,1:T(8,128)(2,1)} %param.18) | copy-start | bytes 884740
  37.7 0.7 copy-start.13
  37.7 1.2 copy-start.9
  37.7 1.2 copy-start.10
  77.9 17.3 %copy-start.2 = (bf16[32,3,1536]{2,0,1:T(8,128)(2,1)S(1)}, bf16[32,3,1536]{2,0,1:T(8,128)(2,1)}, u32[]{:S(2)}) copy-start(bf16[32,3,1536]{2,0,1:T(8,128)(2,1)} %param.18) | copy-start | bytes 884740
  77.9 17.3 %copy-start.4 = (f32[32,1536]{1,0:T(8,128)S(1)}, f32[32,1536]{1,0:T(8,128)}, u32[]{:S(2)}) copy-start(f32[32,1536]{1,0:T(8,128)} %get-tuple-element.30) | copy-start | bytes 589828
  95.2 3.6 %copy-start.11 = (f32[1536]{0:T(1024)S(1)}, f32[1536]{0:T(1024)}, u32[]{:S(2)}) copy-start(f32[1536]{0:T(1024)} %param.29) | copy-start | bytes 18436
  100.8 29.5 %all-to-all-start.2 = ((bf16[128,3,1536]{2,1,0:T(4,128)(2,1)}), bf16[128,3,1536]{2,1,0:T(4,128)(2,1)S(1)}, u32[]{:S(2)}, u32[]{:S(2)}) async-start(bf16[128,3,1536]{2,1,0:T(4,128)(2,1)} %bitcast.116), calls=%async_computation.2 | async-start | bytes 3145728 | tf_op jit(solution)/shard_map/all_to_all | solution.py:185
  105.4 52.0 %reduce-scatter.2.cloned.1.call-start = ((), (), s32[]{:S(2)}) async-start(), calls=%async_computation.5 | async-start | bytes 1474560 | tf_op jit(solution)/shard_map/reduce_scatter | solution.py:198
  132.4 2.5 %copy-start.3 = (bf16[1,512,384]{1,2,0:T(8,128)(2,1)S(1)}, bf16[1,512,384]{1,2,0:T(8,128)(2,1)}, u32[]{:S(2)}) copy-start(bf16[1,512,384]{1,2,0:T(8,128)(2,1)} %copy.68) | copy-start | bytes 1179652
  132.4 2.5 %copy-start.12 = (f32[384]{0:T(512)S(1)}, f32[384]{0:T(512)}, u32[]{:S(2)}) copy-start(f32[384]{0:T(512)} %param.31) | copy-start | bytes 4612
  134.9 1.0 copy-start.6
  136.5 1.9 copy-start.5
  159.3 20.5 %copy-start.7 = (bf16[1536,64]{0,1:T(8,128)(2,1)S(1)}, bf16[1536,64]{0,1:T(8,128)(2,1)}, u32[]{:S(2)}) copy-start(bf16[1536,64]{0,1:T(8,128)(2,1)} %param.35) | copy-start | bytes 589828
  159.3 20.5 %copy-start.8 = (f32[32,3,64]{2,0,1:T(8,128)S(1)}, f32[32,3,64]{2,0,1:T(8,128)}, u32[]{:S(2)}) copy-start(f32[32,3,64]{2,0,1:T(8,128)} %param.19) | copy-start | bytes 73732
  159.3 20.5 %copy-start.14 = (f32[32]{0:T(128)S(1)}, f32[32]{0:T(128)}, u32[]{:S(2)}) copy-start(f32[32]{0:T(128)} %param.24) | copy-start | bytes 388
  159.3 19.4 %all-to-all-start.3 = ((bf16[32,3,1536]{2,1,0:T(4,128)(2,1)}), bf16[32,3,1536]{2,1,0:T(4,128)(2,1)S(1)}, u32[]{:S(2)}, u32[]{:S(2)}) async-start(bf16[32,3,1536]{2,1,0:T(4,128)(2,1)} %reshape.198), calls=%async_computation.4 | async-start | bytes 786432 | tf_op jit(solution)/shard_map/all_to_all | solution.py:205
Sparse Core Ops, SparseCore 0:
  138.5 18.8 reduce-scatter.1
where the time goes:
time: 189 us; the launch traced here: 188 us
  blocking collectives  48.2 us (26%)
  waiting for transfers between devices  46.9 us (25%)
  local copies, waits for them, and re-layouts  36.6 us (19%)
  matrix products  18.5 us (10%)
  between operations  15.1 us (8%)
  starting transfers between devices  13.8 us (7%)
  other arithmetic  8.48 us (4%)
    all_to_all x1, blocking collectives, local(): lax.all_to_all(packed.reshape(head_count * videos, per_video, 3 * group_w...  31.9 us
    unnamed x35, local copies, waits for them, and re-layouts  25.6 us
    reduce_scatter x1, waiting for transfers between devices, local(): lax.psum_scatter(jnp.dot(cross_mixture, cross_wo, preferred_element_type=...  18.7 us
    all_to_all x1, waiting for transfers between devices, local(): lax.all_to_all(copies, ('head', 'tile'), split_axis=0, concat_axis=0, til...  17.9 us
    all_to_all x1, blocking collectives, local(): lax.all_to_all(own_mixture.reshape(head_count * tile_count, per_video, gr...  16.4 us
    all_to_all x1, waiting for transfers between devices, local(): lax.all_to_all(cross_out, 'tile', split_axis=0, concat_axis=0, tiled=True)  10.3 us
    all_to_all x1, starting transfers between devices, local(): lax.all_to_all(cross_out, 'tile', split_axis=0, concat_axis=0, tiled=True)  9.08 us
    dot_general x1, matrix products, pack_projected(): jnp.dot(block_in.reshape(-1, model_width), w_qkv, preferred_element_type=...  7.61 us
  transfers between devices with their start and end apart: 3, of which 3 were waited for; matrix products, arithmetic and copies ran while one was open for 4% of the time, Pallas kernels for 0%

commit v1 on v0

--- a/solution.py
+++ b/solution.py
@@ -3,6 +3,8 @@
 import jax
 import jax.numpy as jnp
 from jax import lax
+from jax.experimental import pallas as pl
+from jax.experimental.pallas import tpu as pltpu
 from jax.sharding import PartitionSpec as P
 
 HEADS = 12
@@ -99,11 +101,33 @@
     return (mixture / jnp.transpose(totals)[:, :, None]).astype(jnp.bfloat16)
 
 
+def _matmul_kernel(x_ref, w_ref, o_ref):
+    o_ref[...] = jnp.dot(x_ref[...], w_ref[...], preferred_element_type=jnp.float32)
+
+
+def stream_matmul(rows, weight, column_block):
+    row_count, inner = rows.shape
+    columns = weight.shape[1]
+    return pl.pallas_call(
+        _matmul_kernel,
+        grid=(columns // column_block,),
+        in_specs=[
+            pl.BlockSpec((row_count, inner), lambda j: (0, 0)),
+            pl.BlockSpec((inner, column_block), lambda j: (0, j)),
+        ],
+        out_specs=pl.BlockSpec((row_count, column_block), lambda j: (0, j)),
+        out_shape=jax.ShapeDtypeStruct((row_count, columns), jnp.float32),
+        cost_estimate=pl.CostEstimate(
+            flops=2 * row_count * inner * columns,
+            bytes_accessed=2 * inner * columns + 2 * row_count * inner + 4 * row_count * columns,
+            transcendentals=0,
+        ),
+    )(rows, weight)
+
+
 def pack_projected(block_in, cell_map, w_qkv, self_q_gain, self_k_gain, head_count):
     videos, per_video, model_width = block_in.shape
-    projected = jnp.dot(
-        block_in.reshape(-1, model_width), w_qkv, preferred_element_type=jnp.float32
-    )
+    projected = stream_matmul(block_in.reshape(-1, model_width), w_qkv, 768)
     projected = projected.reshape(videos, per_video, 3, HEADS, HEAD_DIM)
     angles = rope_angles(cell_map)
     queries = rotate(

time: 189 us -> 194 us (1.026)
  Pallas kernels: 0 us -> 8.63 us
  other arithmetic: 8.48 us -> 17 us
  matrix products: 18.5 us -> 10.8 us
  local copies, waits for them, and re-layouts: 36.6 us -> 32 us
    unnamed x35 -> x32, local copies, waits for them, and re-layouts: 25.6 us -> 6.75 us
    pallas_call x0 -> x1, Pallas kernels: none -> 8.63 us  [stream_matmul(): pl.pallas_call(_matmul_kernel, grid=(columns // column_block,), in_specs=...]
    dot_general x1 -> x0, matrix products: 7.61 us -> none  [pack_projected(): jnp.dot(block_in.reshape(-1, model_width), w_qkv, preferred_element_type=...]
    convert_element_type x0 -> x4, local copies, waits for them, and re-layouts: none -> 3.7 us  [the longest x1 1.34 us: rope_angles(): frame_index = (cell_ids // plane_cells).astype(jnp.float32)]
    reduce_sum x0 -> x2, local copies, waits for them, and re-layouts: none -> 3.07 us  [head_norm(): mean_square = jnp.mean(inputs * inputs, axis=-1, keepdims=True)]
    rsqrt x0 -> x2, local copies, waits for them, and re-layouts: none -> 2.89 us  [head_norm(): return inputs * lax.rsqrt(mean_square + EPSILON) * gain_table]
    rsqrt x2 -> x3, other arithmetic: 0.02 us -> 2.72 us  [head_norm(): return inputs * lax.rsqrt(mean_square + EPSILON) * gain_table]
    reshape x0 -> x2, local copies, waits for them, and re-layouts: none -> 2.55 us  [the longest x1 1.58 us: pack_projected(): projected = projected.reshape(videos, per_video, 3, HEADS, HEAD_DIM)]
  transfers between devices with their start and end apart: 3 -> 3, of which waited for: 3 -> 3; matrix products, arithmetic and copies ran while one was open for 4% -> 3% of each run, Pallas kernels for 0% -> 0%
where the time goes in v1:
time: 194 us; the launch traced here: 192 us
  blocking collectives  48.2 us (25%)
  waiting for transfers between devices  46.8 us (24%)
  local copies, waits for them, and re-layouts  32 us (16%)
  other arithmetic  17 us (9%)
  between operations  15.1 us (8%)
  starting transfers between devices  13.7 us (7%)
  matrix products  10.8 us (6%)
  Pallas kernels  8.63 us (4%)
    all_to_all x1, blocking collectives, local(): lax.all_to_all(packed.reshape(head_count * videos, per_video, 3 * group_w...  31.9 us
    reduce_scatter x1, waiting for transfers between devices, local(): lax.psum_scatter(jnp.dot(cross_mixture, cross_wo, preferred_element_type=...  18.7 us
    all_to_all x1, waiting for transfers between devices, local(): lax.all_to_all(copies, ('head', 'tile'), split_axis=0, concat_axis=0, til...  17.9 us
    all_to_all x1, blocking collectives, local(): lax.all_to_all(own_mixture.reshape(head_count * tile_count, per_video, gr...  16.4 us
    all_to_all x1, waiting for transfers between devices, local(): lax.all_to_all(cross_out, 'tile', split_axis=0, concat_axis=0, tiled=True)  10.3 us
    all_to_all x1, starting transfers between devices, local(): lax.all_to_all(cross_out, 'tile', split_axis=0, concat_axis=0, tiled=True)  9.03 us
    pallas_call x1, Pallas kernels, stream_matmul(): pl.pallas_call(_matmul_kernel, grid=(columns // column_block,), in_specs=...  8.63 us
    unnamed x32, local copies, waits for them, and re-layouts  6.75 us
  transfers between devices with their start and end apart: 3, of which 3 were waited for; matrix products, arithmetic and copies ran while one was open for 3% of the time, Pallas kernels for 0%

profile of v1, /device:TPU:1, one launch (start us, length us, event | category | flops | bytes accessed | tf_op | source)
XLA Modules:
  0.0 192.3 jit_solution(2683670359694854020)
XLA Ops:
  7.2 1.9 %slice_bitcast_fusion.3 = (f32[32,1536]{1,0:T(8,128)}, f32[32,1536]{1,0:T(8,128)S(1)}, f32[32,1536]{1,0:T(8,128)S(1)}) fusion(f32[32,3,1536]{2,0,1:T(8,128)} %param.22), kind=kLoop, calls=%fused_computation.73 | loop fusion | flops 49152 | bytes 1179648 | tf_op jit(solution)/shard_map/mul | solution.py:204
  9.1 1.1 convert_reduce_fusion
  10.2 1.2 fusion.24
  12.9 8.6 %shard_map.185 = f32[96,4608]{1,0:T(8,128)} custom-call(bf16[96,1536]{1,0:T(8,128)(2,1)} %reshape.194.x_ref, bf16[1536,4608]{1,0:T(8,128)(2,1)} %w_ref.1), custom_call_target="tpu_custom_call" | custom-call | flops 1358954496 | bytes 16220160 | tf_op jit(solution)/shard_map/pallas_call | solution.py:111
  21.5 1.6 reshape.195
  23.9 1.2 multiply_reduce_fusion.1
  26.3 1.9 stack.8
  28.2 1.5 copy.104
  29.7 1.4 add_rsqrt_fusion.1
  31.1 1.4 copy.105
  32.5 1.5 copy.109
  34.1 1.4 add_rsqrt_fusion
  35.4 1.4 copy.110
  38.2 1.3 copy.108
  39.6 1.3 copy.106
  43.2 1.4 multiply_multiply_fusion.1
  48.5 31.9 %all_to_all.20 = bf16[128,3,1152]{2,1,0:T(4,128)(2,1)S(1)} all-to-all(bf16[128,3,1152]{2,1,0:T(4,128)(2,1)S(1)} %reshape.205), channel_id=1, replica_groups=mesh['head'=4,'tile'=32] {'head','tile'}, dimensions={0} | all-to-all | bytes 1769472 | tf_op jit(solution)/shard_map/all_to_all | solution.py:177
  83.4 16.4 %all_to_all.21 = bf16[128,3,384]{2,1,0:T(4,128)(2,1)S(1)} all-to-all(bf16[128,3,384]{2,1,0:T(4,128)(2,1)S(1)} %reshape_reshape.7), channel_id=1, replica_groups=mesh['head'=4,'tile'=32] {'head','tile'}, dimensions={0} | all-to-all | bytes 589824 | tf_op jit(solution)/shard_map/all_to_all | solution.py:189
  100.2 3.3 %fusion.57 = (f32[32,3]{0,1:T(4,128)S(1)}, f32[32,3,1536]{2,0,1:T(8,128)S(1)}) fusion(bf16[32,3,1536]{2,0,1:T(8,128)(2,1)S(1)} %dot_general.34, bf16[1536,1536]{1,0:T(8,128)(2,1)} %param.28, f32[32,1536]{1,0:T(8,128)S(1)} %copy-done.5, bf16[32,3,1536]{2,0,1:T(8,128)(2,1)S(1)} %copy-done.2), kind=kOutput, calls=%fused_computation.114 | convolution fusion | flops 453574560 | bytes 6095232 | tf_op jit(solution)/shard_map/dot_general | solution.py:201
  104.1 1.6 broadcast_in_dim.5
  105.7 4.6 %all-to-all-start.2 = ((bf16[128,3,1536]{2,1,0:T(4,128)(2,1)}), bf16[128,3,1536]{2,1,0:T(4,128)(2,1)S(1)}, u32[]{:S(2)}, u32[]{:S(2)}) async-start(bf16[128,3,1536]{2,1,0:T(4,128)(2,1)} %bitcast.102), calls=%async_computation.2 | async-start | bytes 3145728 | tf_op jit(solution)/shard_map/all_to_all | solution.py:209
  110.4 1.9 %copy.124 = bf16[1,512,384]{1,2,0:T(8,128)(2,1)} copy(bf16[1,512,384]{2,1,0:T(8,128)(2,1)} %param.33) | data formatting | bytes 786432 | tf_op args[15]
  113.0 1.9 copy.121
  114.9 2.4 %copy.120 = bf16[1536,384]{0,1:T(8,128)(2,1)} copy(bf16[1536,384]{1,0:T(8,128)(2,1)} %param.30) | data formatting | bytes 2359296 | tf_op args[12]
  117.3 17.9 %all-to-all-done.2 = bf16[128,3,1536]{2,1,0:T(4,128)(2,1)S(1)} async-done(((bf16[128,3,1536]{2,1,0:T(4,128)(2,1)}), bf16[128,3,1536]{2,1,0:T(4,128)(2,1)S(1)}, u32[]{:S(2)}, u32[]{:S(2)}) %all-to-all-start.2) | async-done | bytes 1179680 | tf_op jit(solution)/shard_map/all_to_all | solution.py:209
  135.2 2.2 %reshape.203 = bf16[384,1536,1]{1,0,2:T(8,128)(2,1)} reshape(bf16[128,3,1536]{2,1,0:T(4,128)(2,1)S(1)} %all-to-all-done.2) | data formatting | bytes 2359296 | tf_op jit(solution)/shard_map/reshape | solution.py:210
  137.3 2.5 %multiply_reduce_fusion.3 = (f32[384,3]{0,1:T(4,128)S(1)}, f32[384,3,128]{0,2,1:T(8,128)S(1)}) fusion(bf16[384,1536,1]{1,0,2:T(8,128)(2,1)} %reshape.203, bf16[3,128,1536]{2,1,0:T(8,128)(2,1)} %bitcast.105), kind=kOutput, calls=%fused_computation.46 | convolution fusion | flops 453278592 | bytes 2953728 | tf_op jit(solution)/shard_map/dot_general | solution.py:211
  141.4 1.8 convolution_convert_fusion
  143.6 18.7 %reduce-scatter.2.cloned.1.call-done = bf16[96,1536]{1,0:T(8,128)(2,1)} async-done(((bf16[384,1536]{1,0:T(8,128)(2,1)}), bf16[96,1536]{1,0:T(8,128)(2,1)}) %reduce-scatter.2.cloned.1.call-update) | async-done | bytes 294928 | tf_op jit(solution)/shard_map/reduce_scatter | solution.py:222
  162.3 1.9 reshape.201
  164.1 9.0 %all-to-all-start.3 = ((bf16[32,3,1536]{2,1,0:T(4,128)(2,1)}), bf16[32,3,1536]{2,1,0:T(4,128)(2,1)S(1)}, u32[]{:S(2)}, u32[]{:S(2)}) async-start(bf16[32,3,1536]{2,1,0:T(4,128)(2,1)} %reshape.201), calls=%async_computation.4 | async-start | bytes 786432 | tf_op jit(solution)/shard_map/all_to_all | solution.py:229
  173.2 10.3 %all-to-all-done.3 = bf16[32,3,1536]{2,1,0:T(4,128)(2,1)S(1)} async-done(((bf16[32,3,1536]{2,1,0:T(4,128)(2,1)}), bf16[32,3,1536]{2,1,0:T(4,128)(2,1)S(1)}, u32[]{:S(2)}, u32[]{:S(2)}) %all-to-all-start.3) | async-done | bytes 294944 | tf_op jit(solution)/shard_map/all_to_all | solution.py:229
  (75 shorter events, 18.8 us)
Async XLA Ops:
  7.2 134.2 %copy-start = (bf16[384,1536]{1,0:T(8,128)(2,1)S(1)}, bf16[384,1536]{1,0:T(8,128)(2,1)}, u32[]{:S(2)}) copy-start(bf16[384,1536]{1,0:T(8,128)(2,1)} %param.34) | copy-start | bytes 3538948
  7.2 4.2 %copy-start.1 = (bf16[32,3,1536]{2,0,1:T(8,128)(2,1)S(1)}, bf16[32,3,1536]{2,0,1:T(8,128)(2,1)}, u32[]{:S(2)}) copy-start(bf16[32,3,1536]{2,0,1:T(8,128)(2,1)} %param.18) | copy-start | bytes 884740
  23.1 13.8 %copy-start.12 = (s32[32,3]{0,1:T(4,128)S(1)}, s32[32,3]{0,1:T(4,128)}, u32[]{:S(2)}) copy-start(s32[32,3]{0,1:T(4,128)} %param.20) | copy-start | bytes 1156
  45.2 1.0 copy-start.4
  82.8 17.3 %copy-start.2 = (bf16[32,3,1536]{2,0,1:T(8,128)(2,1)S(1)}, bf16[32,3,1536]{2,0,1:T(8,128)(2,1)}, u32[]{:S(2)}) copy-start(bf16[32,3,1536]{2,0,1:T(8,128)(2,1)} %param.18) | copy-start | bytes 884740
  82.8 17.3 %copy-start.5 = (f32[32,1536]{1,0:T(8,128)S(1)}, f32[32,1536]{1,0:T(8,128)}, u32[]{:S(2)}) copy-start(f32[32,1536]{1,0:T(8,128)} %get-tuple-element.30) | copy-start | bytes 589828
  100.2 3.6 %copy-start.10 = (f32[1536]{0:T(1024)S(1)}, f32[1536]{0:T(1024)}, u32[]{:S(2)}) copy-start(f32[1536]{0:T(1024)} %param.29) | copy-start | bytes 18436
  105.7 29.5 %all-to-all-start.2 = ((bf16[128,3,1536]{2,1,0:T(4,128)(2,1)}), bf16[128,3,1536]{2,1,0:T(4,128)(2,1)S(1)}, u32[]{:S(2)}, u32[]{:S(2)}) async-start(bf16[128,3,1536]{2,1,0:T(4,128)(2,1)} %bitcast.102), calls=%async_computation.2 | async-start | bytes 3145728 | tf_op jit(solution)/shard_map/all_to_all | solution.py:209
  110.3 51.9 %reduce-scatter.2.cloned.1.call-start = ((), (), s32[]{:S(2)}) async-start(), calls=%async_computation.5 | async-start | bytes 1474560 | tf_op jit(solution)/shard_map/reduce_scatter | solution.py:222
  137.3 2.5 %copy-start.3 = (bf16[1,512,384]{1,2,0:T(8,128)(2,1)S(1)}, bf16[1,512,384]{1,2,0:T(8,128)(2,1)}, u32[]{:S(2)}) copy-start(bf16[1,512,384]{1,2,0:T(8,128)(2,1)} %copy.121) | copy-start | bytes 1179652
  137.3 2.5 %copy-start.11 = (f32[384]{0:T(512)S(1)}, f32[384]{0:T(512)}, u32[]{:S(2)}) copy-start(f32[384]{0:T(512)} %param.31) | copy-start | bytes 4612
  139.8 1.0 copy-start.7
  141.4 1.9 copy-start.6
  164.1 20.4 %copy-start.8 = (bf16[1536,64]{0,1:T(8,128)(2,1)S(1)}, bf16[1536,64]{0,1:T(8,128)(2,1)}, u32[]{:S(2)}) copy-start(bf16[1536,64]{0,1:T(8,128)(2,1)} %param.35) | copy-start | bytes 589828
  164.1 20.4 %copy-start.9 = (f32[32,3,64]{2,0,1:T(8,128)S(1)}, f32[32,3,64]{2,0,1:T(8,128)}, u32[]{:S(2)}) copy-start(f32[32,3,64]{2,0,1:T(8,128)} %param.19) | copy-start | bytes 73732
  164.1 20.4 %copy-start.13 = (f32[32]{0:T(128)S(1)}, f32[32]{0:T(128)}, u32[]{:S(2)}) copy-start(f32[32]{0:T(128)} %param.24) | copy-start | bytes 388
  164.1 19.3 %all-to-all-start.3 = ((bf16[32,3,1536]{2,1,0:T(4,128)(2,1)}), bf16[32,3,1536]{2,1,0:T(4,128)(2,1)S(1)}, u32[]{:S(2)}, u32[]{:S(2)}) async-start(bf16[32,3,1536]{2,1,0:T(4,128)(2,1)} %reshape.201), calls=%async_computation.4 | async-start | bytes 786432 | tf_op jit(solution)/shard_map/all_to_all | solution.py:229
Sparse Core Ops, SparseCore 0:
  143.4 18.8 reduce-scatter.1

commit v2 on v0

--- a/solution.py
+++ b/solution.py
@@ -3,6 +3,8 @@
 import jax
 import jax.numpy as jnp
 from jax import lax
+from jax.experimental import pallas as pl
+from jax.experimental.pallas import tpu as pltpu
 from jax.sharding import PartitionSpec as P
 
 HEADS = 12
@@ -99,23 +101,59 @@
     return (mixture / jnp.transpose(totals)[:, :, None]).astype(jnp.bfloat16)
 
 
+def _qkv_kernel(x_ref, w_ref, cos_ref, sin_ref, gain_ref, o_ref):
+    section = pl.program_id(1)
+    projected = jnp.dot(x_ref[...], w_ref[...], preferred_element_type=jnp.float32)
+
+    @pl.when(section == 2)
+    def _():
+        o_ref[0] = projected.astype(o_ref.dtype)
+
+    @pl.when(section < 2)
+    def _():
+        gains = gain_ref[pl.ds(jnp.minimum(section, 1), 1), :]
+        cosine = cos_ref[...]
+        sine_signed = sin_ref[...]
+        parts = []
+        for head in range(projected.shape[1] // HEAD_DIM):
+            lanes = slice(head * HEAD_DIM, (head + 1) * HEAD_DIM)
+            piece = projected[:, lanes]
+            mean_square = jnp.mean(piece * piece, axis=-1, keepdims=True)
+            normed = piece * lax.rsqrt(mean_square + EPSILON) * gains[:, lanes]
+            swapped = pltpu.roll(normed, HEAD_DIM // 2, 1)
+            parts.append(normed * cosine + swapped * sine_signed)
+        o_ref[0] = jnp.concatenate(parts, axis=-1).astype(o_ref.dtype)
+
+
 def pack_projected(block_in, cell_map, w_qkv, self_q_gain, self_k_gain, head_count):
     videos, per_video, model_width = block_in.shape
-    projected = jnp.dot(
-        block_in.reshape(-1, model_width), w_qkv, preferred_element_type=jnp.float32
-    )
-    projected = projected.reshape(videos, per_video, 3, HEADS, HEAD_DIM)
-    angles = rope_angles(cell_map)
-    queries = rotate(
-        head_norm(projected[:, :, 0], self_q_gain.reshape(HEADS, HEAD_DIM)), angles
-    ).astype(jnp.bfloat16)
-    keys_all = rotate(
-        head_norm(projected[:, :, 1], self_k_gain.reshape(HEADS, HEAD_DIM)), angles
-    ).astype(jnp.bfloat16)
-    values_all = projected[:, :, 2].astype(jnp.bfloat16)
-    packed = jnp.stack([queries, keys_all, values_all], axis=2)
+    rows = block_in.reshape(-1, model_width)
+    token_total = rows.shape[0]
     group_width = model_width // head_count
-    packed = packed.reshape(videos, per_video, 3, head_count, group_width).transpose(3, 0, 1, 2, 4)
+    angles = rope_angles(cell_map).reshape(token_total, HEAD_DIM // 2)
+    cosine = jnp.cos(angles)
+    sine = jnp.sin(angles)
+    cos_full = jnp.concatenate([cosine, cosine], axis=-1)
+    sin_signed = jnp.concatenate([-sine, sine], axis=-1)
+    gains = jnp.stack([self_q_gain, self_k_gain])
+    packed = pl.pallas_call(
+        _qkv_kernel,
+        grid=(head_count, 3),
+        in_specs=[
+            pl.BlockSpec((token_total, model_width), lambda g, s: (0, 0)),
+            pl.BlockSpec((model_width, group_width), lambda g, s: (0, s * head_count + g)),
+            pl.BlockSpec((token_total, HEAD_DIM), lambda g, s: (0, 0)),
+            pl.BlockSpec((token_total, HEAD_DIM), lambda g, s: (0, 0)),
+            pl.BlockSpec((2, group_width), lambda g, s: (0, g)),
+        ],
+        out_specs=pl.BlockSpec((1, token_total, group_width), lambda g, s: (g, 0, s)),
+        out_shape=jax.ShapeDtypeStruct((head_count, token_total, 3 * group_width), jnp.bfloat16),
+        cost_estimate=pl.CostEstimate(
+            flops=2 * token_total * model_width * 3 * model_width,
+            bytes_accessed=2 * model_width * 3 * model_width + 4 * token_total * 3 * model_width,
+            transcendentals=0,
+        ),
+    )(rows, w_qkv, cos_full, sin_signed, gains)
     return packed.reshape(head_count, videos, per_video, 3 * group_width)
 
 

time: 189 us -> 179 us (0.947)
  local copies, waits for them, and re-layouts: 36.6 us -> 22.9 us
  Pallas kernels: 0 us -> 12.6 us
  matrix products: 18.5 us -> 11.9 us
    unnamed x35 -> x28, local copies, waits for them, and re-layouts: 25.6 us -> 6.71 us
    pallas_call x0 -> x1, Pallas kernels: none -> 12.6 us  [pack_projected(): pl.pallas_call(_qkv_kernel, grid=(head_count, 3), in_specs=[pl.BlockSpec(...]
    dot_general x1 -> x0, matrix products: 7.61 us -> none  [pack_projected(): jnp.dot(block_in.reshape(-1, model_width), w_qkv, preferred_element_type=...]
    reshape x1, local copies, waits for them, and re-layouts: 0.83 us -> 3.48 us  [local(): arrived = arrived.reshape(-1, 3, group_heads, HEAD_DIM)]
where the time goes in v2:
time: 179 us; the launch traced here: 178 us
  blocking collectives  48.4 us (27%)
  waiting for transfers between devices  46.7 us (26%)
  local copies, waits for them, and re-layouts  22.9 us (13%)
  between operations  15 us (8%)
  starting transfers between devices  13.9 us (8%)
  Pallas kernels  12.6 us (7%)
  matrix products  11.9 us (7%)
  other arithmetic  6.83 us (4%)
    all_to_all x1, blocking collectives, local(): lax.all_to_all(packed.reshape(head_count * videos, per_video, 3 * group_w...  32 us
    reduce_scatter x1, waiting for transfers between devices, local(): lax.psum_scatter(jnp.dot(cross_mixture, cross_wo, preferred_element_type=...  18.7 us
    all_to_all x1, waiting for transfers between devices, local(): lax.all_to_all(copies, ('head', 'tile'), split_axis=0, concat_axis=0, til...  17.7 us
    all_to_all x1, blocking collectives, local(): lax.all_to_all(own_mixture.reshape(head_count * tile_count, per_video, gr...  16.4 us
    pallas_call x1, Pallas kernels, pack_projected(): pl.pallas_call(_qkv_kernel, grid=(head_count, 3), in_specs=[pl.BlockSpec(...  12.6 us
    all_to_all x1, waiting for transfers between devices, local(): lax.all_to_all(cross_out, 'tile', split_axis=0, concat_axis=0, tiled=True)  10.3 us
    all_to_all x1, starting transfers between devices, local(): lax.all_to_all(cross_out, 'tile', split_axis=0, concat_axis=0, tiled=True)  9.08 us
    unnamed x28, local copies, waits for them, and re-layouts  6.71 us
  transfers between devices with their start and end apart: 3, of which 3 were waited for; matrix products, arithmetic and copies ran while one was open for 4% of the time, Pallas kernels for 0%

profile of v2, /device:TPU:1, one launch (start us, length us, event | category | flops | bytes accessed | tf_op | source)
XLA Modules:
  0.0 178.3 jit_solution(6361300623112431739)
XLA Ops:
  7.2 0.8 fusion.42
  8.6 1.2 slice_bitcast_fusion.1
  9.8 1.1 convert_reduce_fusion
  11.7 1.0 reshape.117.x_ref
  12.8 0.6 pad_maximum_fusion.3.gain_ref
  13.7 0.7 pad_maximum_fusion.1
  14.5 12.6 %shard_map.185 = bf16[4,96,1152]{2,1,0:T(8,128)(2,1)} custom-call(bf16[96,1536]{1,0:T(8,128)(2,1)} %reshape.117.x_ref, bf16[1536,4608]{1,0:T(8,128)(2,1)} %w_ref.1, f32[96,128]{1,0:T(8,128)} %get-tuple-element.43.cos_ref, f32[96,128]{1,0:T(8,128)} %get-tuple-element.44.sin_ref, f32[2,1536]{1,0:T(2,128)} %pad_maximum_fusion.3.gain_ref), custom_call_target="tpu_custom_call" | custom-call | flops 1358954496 | bytes 15925248 | tf_op jit(solution)/shard_map/pallas_call | solution.py:139
  27.1 2.5 %reshape_reshape.6 = bf16[128,3,1152]{2,1,0:T(4,128)(2,1)S(1)} reshape(bf16[4,96,1152]{2,1,0:T(8,128)(2,1)} %shard_map.185) | data formatting | bytes 1769472 | tf_op jit(solution)/shard_map/reshape;reshape | solution.py:192
  29.6 32.0 %all_to_all.20 = bf16[128,3,1152]{2,1,0:T(4,128)(2,1)} all-to-all(bf16[128,3,1152]{2,1,0:T(4,128)(2,1)S(1)} %reshape_reshape.6), channel_id=1, replica_groups=mesh['head'=4,'tile'=32] {'head','tile'}, dimensions={0} | all-to-all | bytes 1769472 | tf_op jit(solution)/shard_map/all_to_all | solution.py:191
  61.6 3.5 %reshape.118 = bf16[384,3,3,128]{3,2,1,0:T(4,128)(2,1)S(1)} reshape(bf16[128,3,1152]{2,1,0:T(4,128)(2,1)} %all_to_all.20) | data formatting | bytes 1769472 | tf_op jit(solution)/shard_map/reshape | solution.py:198
  65.1 1.3 fusion.53
  66.7 1.6 fusion.10
  68.2 0.4 fusion.15
  69.2 16.4 %all_to_all.21 = bf16[128,3,384]{2,1,0:T(4,128)(2,1)S(1)} all-to-all(bf16[128,3,384]{2,1,0:T(4,128)(2,1)S(1)} %reshape_reshape.7), channel_id=1, replica_groups=mesh['head'=4,'tile'=32] {'head','tile'}, dimensions={0} | all-to-all | bytes 589824 | tf_op jit(solution)/shard_map/all_to_all | solution.py:203
  86.0 3.3 %fusion.55 = (f32[32,3]{0,1:T(4,128)S(1)}, f32[32,3,1536]{2,0,1:T(8,128)S(1)}) fusion(bf16[32,3,1536]{2,0,1:T(8,128)(2,1)S(1)} %dot_general.34, bf16[1536,1536]{1,0:T(8,128)(2,1)} %param.28, f32[32,1536]{1,0:T(8,128)S(1)} %get-tuple-element.24, bf16[32,3,1536]{2,0,1:T(8,128)(2,1)S(1)} %copy-done.1), kind=kOutput, calls=%fused_computation.98 | convolution fusion | flops 453574560 | bytes 6095232 | tf_op jit(solution)/shard_map/dot_general | solution.py:215
  90.0 1.6 broadcast_in_dim.5
  91.6 4.6 %all-to-all-start.2 = ((bf16[128,3,1536]{2,1,0:T(4,128)(2,1)}), bf16[128,3,1536]{2,1,0:T(4,128)(2,1)S(1)}, u32[]{:S(2)}, u32[]{:S(2)}) async-start(bf16[128,3,1536]{2,1,0:T(4,128)(2,1)} %bitcast.72), calls=%async_computation.2 | async-start | bytes 3145728 | tf_op jit(solution)/shard_map/all_to_all | solution.py:223
  96.4 2.4 %copy.63 = bf16[1536,384]{0,1:T(8,128)(2,1)} copy(bf16[1536,384]{1,0:T(8,128)(2,1)} %param.30) | data formatting | bytes 2359296 | tf_op args[12]
  99.5 1.9 %copy.64 = bf16[1,512,384]{1,2,0:T(8,128)(2,1)} copy(bf16[1,512,384]{2,1,0:T(8,128)(2,1)} %param.32) | data formatting | bytes 786432 | tf_op args[14]
  101.4 1.9 %copy.67 = bf16[1,512,384]{1,2,0:T(8,128)(2,1)} copy(bf16[1,512,384]{2,1,0:T(8,128)(2,1)} %param.33) | data formatting | bytes 786432 | tf_op args[15]
  103.3 17.7 %all-to-all-done.2 = bf16[128,3,1536]{2,1,0:T(4,128)(2,1)S(1)} async-done(((bf16[128,3,1536]{2,1,0:T(4,128)(2,1)}), bf16[128,3,1536]{2,1,0:T(4,128)(2,1)S(1)}, u32[]{:S(2)}, u32[]{:S(2)}) %all-to-all-start.2) | async-done | bytes 1179680 | tf_op jit(solution)/shard_map/all_to_all | solution.py:223
  121.0 2.2 %reshape.125 = bf16[384,1536,1]{1,0,2:T(8,128)(2,1)} reshape(bf16[128,3,1536]{2,1,0:T(4,128)(2,1)S(1)} %all-to-all-done.2) | data formatting | bytes 2359296 | tf_op jit(solution)/shard_map/reshape | solution.py:224
  123.2 2.5 %multiply_reduce_fusion.1 = (f32[384,3]{0,1:T(4,128)S(1)}, f32[384,3,128]{0,2,1:T(8,128)S(1)}) fusion(bf16[384,1536,1]{1,0,2:T(8,128)(2,1)} %reshape.125, bf16[3,128,1536]{2,1,0:T(8,128)(2,1)} %bitcast.75), kind=kOutput, calls=%fused_computation.34 | convolution fusion | flops 453278592 | bytes 2953728 | tf_op jit(solution)/shard_map/dot_general | solution.py:225
  125.7 0.8 fusion.8
  126.7 0.6 fusion.14
  127.3 1.8 %convolution_convert_fusion = bf16[384,1536]{1,0:T(8,128)(2,1)} fusion(bf16[384,384]{0,1:T(8,128)(2,1)S(1)} %bitcast.78, bf16[384,1536]{1,0:T(8,128)(2,1)S(1)} %copy-done), kind=kOutput, calls=%fused_computation.2 | convolution fusion | flops 453574656 | bytes 2654208 | tf_op jit(solution)/shard_map/dot_general | solution.py:237
  129.4 18.7 %reduce-scatter.2.cloned.1.call-done = bf16[96,1536]{1,0:T(8,128)(2,1)} async-done(((bf16[384,1536]{1,0:T(8,128)(2,1)}), bf16[96,1536]{1,0:T(8,128)(2,1)}) %reduce-scatter.2.cloned.1.call-update) | async-done | bytes 294928 | tf_op jit(solution)/shard_map/reduce_scatter | solution.py:236
  148.1 1.9 %reshape.123 = bf16[32,3,1536]{2,1,0:T(4,128)(2,1)} reshape(bf16[96,1536]{1,0:T(8,128)(2,1)} %reduce-scatter.2.cloned.1.call-done) | data formatting | bytes 589824 | tf_op jit(solution)/shard_map/reshape | solution.py:242
  150.0 9.1 %all-to-all-start.3 = ((bf16[32,3,1536]{2,1,0:T(4,128)(2,1)}), bf16[32,3,1536]{2,1,0:T(4,128)(2,1)S(1)}, u32[]{:S(2)}, u32[]{:S(2)}) async-start(bf16[32,3,1536]{2,1,0:T(4,128)(2,1)} %reshape.123), calls=%async_computation.4 | async-start | bytes 786432 | tf_op jit(solution)/shard_map/all_to_all | solution.py:243
  159.2 10.3 %all-to-all-done.3 = bf16[32,3,1536]{2,1,0:T(4,128)(2,1)S(1)} async-done(((bf16[32,3,1536]{2,1,0:T(4,128)(2,1)}), bf16[32,3,1536]{2,1,0:T(4,128)(2,1)S(1)}, u32[]{:S(2)}, u32[]{:S(2)}) %all-to-all-start.3) | async-done | bytes 294944 | tf_op jit(solution)/shard_map/all_to_all | solution.py:243
  169.6 0.9 multiply_reduce_fusion
  170.5 0.9 fusion.19
  (61 shorter events, 4.6 us)
Async XLA Ops:
  7.2 120.1 %copy-start = (bf16[384,1536]{1,0:T(8,128)(2,1)S(1)}, bf16[384,1536]{1,0:T(8,128)(2,1)}, u32[]{:S(2)}) copy-start(bf16[384,1536]{1,0:T(8,128)(2,1)} %param.34) | copy-start | bytes 3538948
  7.2 3.7 %copy-start.1 = (bf16[32,3,1536]{2,0,1:T(8,128)(2,1)S(1)}, bf16[32,3,1536]{2,0,1:T(8,128)(2,1)}, u32[]{:S(2)}) copy-start(bf16[32,3,1536]{2,0,1:T(8,128)(2,1)} %param.18) | copy-start | bytes 884740
  9.8 2.8 %copy-start.8 = (f32[1536]{0:T(1024)S(1)}, f32[1536]{0:T(1024)}, u32[]{:S(2)}) copy-start(f32[1536]{0:T(1024)} %param.27) | copy-start | bytes 18436
  9.8 2.8 %copy-start.9 = (f32[1536]{0:T(1024)S(1)}, f32[1536]{0:T(1024)}, u32[]{:S(2)}) copy-start(f32[1536]{0:T(1024)} %param.26) | copy-start | bytes 18436
  86.0 3.6 %copy-start.7 = (f32[1536]{0:T(1024)S(1)}, f32[1536]{0:T(1024)}, u32[]{:S(2)}) copy-start(f32[1536]{0:T(1024)} %param.29) | copy-start | bytes 18436
  91.6 29.5 %all-to-all-start.2 = ((bf16[128,3,1536]{2,1,0:T(4,128)(2,1)}), bf16[128,3,1536]{2,1,0:T(4,128)(2,1)S(1)}, u32[]{:S(2)}, u32[]{:S(2)}) async-start(bf16[128,3,1536]{2,1,0:T(4,128)(2,1)} %bitcast.72), calls=%async_computation.2 | async-start | bytes 3145728 | tf_op jit(solution)/shard_map/all_to_all | solution.py:223
  96.2 52.0 %reduce-scatter.2.cloned.1.call-start = ((), (), s32[]{:S(2)}) async-start(), calls=%async_computation.5 | async-start | bytes 1474560 | tf_op jit(solution)/shard_map/reduce_scatter | solution.py:236
  123.2 2.5 %copy-start.2 = (bf16[1,512,384]{1,2,0:T(8,128)(2,1)S(1)}, bf16[1,512,384]{1,2,0:T(8,128)(2,1)}, u32[]{:S(2)}) copy-start(bf16[1,512,384]{1,2,0:T(8,128)(2,1)} %copy.64) | copy-start | bytes 1179652
  123.2 2.5 %copy-start.10 = (f32[384]{0:T(512)S(1)}, f32[384]{0:T(512)}, u32[]{:S(2)}) copy-start(f32[384]{0:T(512)} %param.31) | copy-start | bytes 4612
  125.7 1.0 copy-start.4
  127.3 1.9 %copy-start.3 = (f32[32,2,1536]{2,1,0:T(2,128)S(1)}, f32[32,2,1536]{2,1,0:T(2,128)}, u32[]{:S(2)}) copy-start(f32[32,2,1536]{2,1,0:T(2,128)} %param.23) | copy-start | bytes 1179652
  150.0 20.5 %copy-start.5 = (bf16[1536,64]{0,1:T(8,128)(2,1)S(1)}, bf16[1536,64]{0,1:T(8,128)(2,1)}, u32[]{:S(2)}) copy-start(bf16[1536,64]{0,1:T(8,128)(2,1)} %param.35) | copy-start | bytes 589828
  150.0 20.5 %copy-start.6 = (f32[32,3,64]{2,0,1:T(8,128)S(1)}, f32[32,3,64]{2,0,1:T(8,128)}, u32[]{:S(2)}) copy-start(f32[32,3,64]{2,0,1:T(8,128)} %param.19) | copy-start | bytes 73732
  150.0 20.5 %copy-start.11 = (f32[32]{0:T(128)S(1)}, f32[32]{0:T(128)}, u32[]{:S(2)}) copy-start(f32[32]{0:T(128)} %param.24) | copy-start | bytes 388
  150.0 19.4 %all-to-all-start.3 = ((bf16[32,3,1536]{2,1,0:T(4,128)(2,1)}), bf16[32,3,1536]{2,1,0:T(4,128)(2,1)S(1)}, u32[]{:S(2)}, u32[]{:S(2)}) async-start(bf16[32,3,1536]{2,1,0:T(4,128)(2,1)} %reshape.123), calls=%async_computation.4 | async-start | bytes 786432 | tf_op jit(solution)/shard_map/all_to_all | solution.py:243
Sparse Core Ops, SparseCore 0:
  129.2 18.8 reduce-scatter.1

commit v3 on v2

--- a/solution.py
+++ b/solution.py
@@ -233,14 +233,17 @@
     cross_mixture = attend_text(
         cross_queries, own_text_keys, own_text_values, text_lengths[0]
     ).reshape(-1, group_width)
-    summed = lax.psum_scatter(
-        jnp.dot(cross_mixture, cross_wo, preferred_element_type=jnp.float32).astype(jnp.bfloat16),
-        "head",
-        scatter_dimension=0,
+    partial = jnp.dot(cross_mixture, cross_wo, preferred_element_type=jnp.float32).astype(
+        jnp.bfloat16
+    )
+    returned_partials = lax.all_to_all(
+        partial.reshape(head_count * tile_count, per_video, model_width),
+        ("head", "tile"),
+        split_axis=0,
+        concat_axis=0,
         tiled=True,
-    )
-    cross_out = summed.reshape(tile_count, per_video, model_width)
-    returned_cross = lax.all_to_all(cross_out, "tile", split_axis=0, concat_axis=0, tiled=True)
+    ).reshape(head_count, videos, per_video, model_width)
+    returned_cross = jnp.sum(returned_partials.astype(jnp.float32), axis=0).astype(jnp.bfloat16)
     after_cross = after_self + returned_cross.astype(jnp.float32)
     hidden_next = after_cross.astype(jnp.bfloat16)
     head_shift = head_modulation[:, 0][:, None, :]

time: 179 us -> 160 us (0.89)
  between operations: 15 us -> 1.62 us
  waiting for transfers between devices: 46.7 us -> 40.5 us
  starting transfers between devices: 13.9 us -> 9.32 us
  other arithmetic: 6.83 us -> 11.4 us
    reduce_scatter x1 -> x0, waiting for transfers between devices: 18.7 us -> none  [local(): lax.psum_scatter(jnp.dot(cross_mixture, cross_wo, preferred_element_type=...]
    all_to_all x1, waiting for transfers between devices: 10.3 us -> 22.6 us  [local(): lax.all_to_all(partial.reshape(head_count * tile_count, per_video, model_...]
    all_to_all x1, starting transfers between devices: 9.08 us -> 4.68 us  [local(): lax.all_to_all(partial.reshape(head_count * tile_count, per_video, model_...]
    reduce_sum x0 -> x1, other arithmetic: none -> 1.81 us  [local(): jnp.sum(returned_partials.astype(jnp.float32), axis=0).astype(jnp.bfloat16)]
    unnamed x28 -> x30, local copies, waits for them, and re-layouts: 6.71 us -> 6.78 us
  transfers between devices with their start and end apart: 3 -> 2, of which waited for: 3 -> 2; matrix products, arithmetic and copies ran while one was open for 4% -> 5% of each run, Pallas kernels for 0% -> 0%
where the time goes in v3:
time: 160 us; the launch traced here: 159 us
  blocking collectives  48.3 us (30%)
  waiting for transfers between devices  40.5 us (25%)
  local copies, waits for them, and re-layouts  24.3 us (15%)
  Pallas kernels  12.6 us (8%)
  other arithmetic  11.4 us (7%)
  matrix products  10.9 us (7%)
  starting transfers between devices  9.32 us (6%)
  between operations  1.62 us (1%)
    all_to_all x1, blocking collectives, local(): lax.all_to_all(packed.reshape(head_count * videos, per_video, 3 * group_w...  31.9 us
    all_to_all x1, waiting for transfers between devices, local(): lax.all_to_all(partial.reshape(head_count * tile_count, per_video, model_...  22.6 us
    all_to_all x1, waiting for transfers between devices, local(): lax.all_to_all(copies, ('head', 'tile'), split_axis=0, concat_axis=0, til...  17.9 us
    all_to_all x1, blocking collectives, local(): lax.all_to_all(own_mixture.reshape(head_count * tile_count, per_video, gr...  16.4 us
    pallas_call x1, Pallas kernels, pack_projected(): pl.pallas_call(_qkv_kernel, grid=(head_count, 3), in_specs=[pl.BlockSpec(...  12.6 us
    unnamed x30, local copies, waits for them, and re-layouts  6.78 us
    all_to_all x1, starting transfers between devices, local(): lax.all_to_all(partial.reshape(head_count * tile_count, per_video, model_...  4.68 us
    all_to_all x1, starting transfers between devices, local(): lax.all_to_all(copies, ('head', 'tile'), split_axis=0, concat_axis=0, til...  4.64 us
  transfers between devices with their start and end apart: 2, of which 2 were waited for; matrix products, arithmetic and copies ran while one was open for 5% of the time, Pallas kernels for 0%

profile of v3, /device:TPU:1, one launch (start us, length us, event | category | flops | bytes accessed | tf_op | source)
XLA Modules:
  0.0 159.0 jit_solution(11860816163695433812)
XLA Ops:
  0.7 0.8 fusion.42
  2.1 1.2 slice_bitcast_fusion.1
  3.3 1.1 convert_reduce_fusion
  5.1 1.0 reshape.120.x_ref
  7.2 0.7 pad_maximum_fusion.1
  7.9 12.6 %shard_map.185 = bf16[4,96,1152]{2,1,0:T(8,128)(2,1)} custom-call(bf16[96,1536]{1,0:T(8,128)(2,1)} %reshape.120.x_ref, bf16[1536,4608]{1,0:T(8,128)(2,1)} %w_ref.1, f32[96,128]{1,0:T(8,128)} %get-tuple-element.43.cos_ref, f32[96,128]{1,0:T(8,128)} %get-tuple-element.44.sin_ref, f32[2,1536]{1,0:T(2,128)} %pad_maximum_fusion.3.gain_ref), custom_call_target="tpu_custom_call" | custom-call | flops 1358954496 | bytes 15925248 | tf_op jit(solution)/shard_map/pallas_call | solution.py:139
  20.5 2.5 %reshape_reshape.6 = bf16[128,3,1152]{2,1,0:T(4,128)(2,1)S(1)} reshape(bf16[4,96,1152]{2,1,0:T(8,128)(2,1)} %shard_map.185) | data formatting | bytes 1769472 | tf_op jit(solution)/shard_map/reshape;reshape | solution.py:192
  23.1 31.9 %all_to_all.20 = bf16[128,3,1152]{2,1,0:T(4,128)(2,1)} all-to-all(bf16[128,3,1152]{2,1,0:T(4,128)(2,1)S(1)} %reshape_reshape.6), channel_id=1, replica_groups=mesh['head'=4,'tile'=32] {'head','tile'}, dimensions={0} | all-to-all | bytes 1769472 | tf_op jit(solution)/shard_map/all_to_all | solution.py:191
  55.0 3.5 %reshape.121 = bf16[384,3,3,128]{3,2,1,0:T(4,128)(2,1)S(1)} reshape(bf16[128,3,1152]{2,1,0:T(4,128)(2,1)} %all_to_all.20) | data formatting | bytes 1769472 | tf_op jit(solution)/shard_map/reshape | solution.py:198
  58.5 1.3 fusion.53
  60.1 1.6 fusion.10
  62.6 16.4 %all_to_all.21 = bf16[128,3,384]{2,1,0:T(4,128)(2,1)S(1)} all-to-all(bf16[128,3,384]{2,1,0:T(4,128)(2,1)S(1)} %reshape_reshape.7), channel_id=1, replica_groups=mesh['head'=4,'tile'=32] {'head','tile'}, dimensions={0} | all-to-all | bytes 589824 | tf_op jit(solution)/shard_map/all_to_all | solution.py:203
  79.4 3.3 %fusion.55 = (f32[32,3]{0,1:T(4,128)S(1)}, f32[32,3,1536]{2,0,1:T(8,128)S(1)}) fusion(bf16[32,3,1536]{2,0,1:T(8,128)(2,1)S(1)} %dot_general.34, bf16[1536,1536]{1,0:T(8,128)(2,1)} %param.28, f32[32,1536]{1,0:T(8,128)S(1)} %get-tuple-element.24, bf16[32,3,1536]{2,0,1:T(8,128)(2,1)S(1)} %copy-done.2), kind=kOutput, calls=%fused_computation.98 | convolution fusion | flops 453574560 | bytes 6095232 | tf_op jit(solution)/shard_map/dot_general | solution.py:215
  83.4 1.6 broadcast_in_dim.5
  85.0 4.6 %all-to-all-start.2 = ((bf16[128,3,1536]{2,1,0:T(4,128)(2,1)}), bf16[128,3,1536]{2,1,0:T(4,128)(2,1)S(1)}, u32[]{:S(2)}, u32[]{:S(2)}) async-start(bf16[128,3,1536]{2,1,0:T(4,128)(2,1)} %bitcast.74), calls=%async_computation.2 | async-start | bytes 3145728 | tf_op jit(solution)/shard_map/all_to_all | solution.py:223
  89.6 2.4 %copy.62 = bf16[1536,384]{0,1:T(8,128)(2,1)} copy(bf16[1536,384]{1,0:T(8,128)(2,1)} %param.30) | data formatting | bytes 2359296 | tf_op args[12]
  92.7 1.9 %copy.63 = bf16[1,512,384]{1,2,0:T(8,128)(2,1)} copy(bf16[1,512,384]{2,1,0:T(8,128)(2,1)} %param.32) | data formatting | bytes 786432 | tf_op args[14]
  94.6 1.9 %copy.66 = bf16[1,512,384]{1,2,0:T(8,128)(2,1)} copy(bf16[1,512,384]{2,1,0:T(8,128)(2,1)} %param.33) | data formatting | bytes 786432 | tf_op args[15]
  96.6 17.9 %all-to-all-done.2 = bf16[128,3,1536]{2,1,0:T(4,128)(2,1)S(1)} async-done(((bf16[128,3,1536]{2,1,0:T(4,128)(2,1)}), bf16[128,3,1536]{2,1,0:T(4,128)(2,1)S(1)}, u32[]{:S(2)}, u32[]{:S(2)}) %all-to-all-start.2) | async-done | bytes 1179680 | tf_op jit(solution)/shard_map/all_to_all | solution.py:223
  114.4 2.2 %reshape.129 = bf16[384,1536,1]{1,0,2:T(8,128)(2,1)} reshape(bf16[128,3,1536]{2,1,0:T(4,128)(2,1)S(1)} %all-to-all-done.2) | data formatting | bytes 2359296 | tf_op jit(solution)/shard_map/reshape | solution.py:224
  116.6 2.5 %multiply_reduce_fusion.1 = (f32[384,3]{0,1:T(4,128)S(1)}, f32[384,3,128]{0,2,1:T(8,128)S(1)}) fusion(bf16[384,1536,1]{1,0,2:T(8,128)(2,1)} %reshape.129, bf16[3,128,1536]{2,1,0:T(8,128)(2,1)} %bitcast.77), kind=kOutput, calls=%fused_computation.34 | convolution fusion | flops 453278592 | bytes 2953728 | tf_op jit(solution)/shard_map/dot_general | solution.py:225
  119.1 0.8 fusion.8
  120.7 0.8 convolution_convert_fusion
  121.5 2.0 %reshape.126 = bf16[128,3,1536]{2,1,0:T(4,128)(2,1)} reshape(bf16[384,1536]{1,0:T(8,128)(2,1)S(1)} %convolution_convert_fusion) | data formatting | bytes 2359296 | tf_op jit(solution)/shard_map/reshape | solution.py:240
  123.5 4.7 %all-to-all-start.3 = ((bf16[128,3,1536]{2,1,0:T(4,128)(2,1)}), bf16[128,3,1536]{2,1,0:T(4,128)(2,1)S(1)}, u32[]{:S(2)}, u32[]{:S(2)}) async-start(bf16[128,3,1536]{2,1,0:T(4,128)(2,1)} %reshape.126), calls=%async_computation.3 | async-start | bytes 3145728 | tf_op jit(solution)/shard_map/all_to_all | solution.py:239
  128.2 1.5 fusion.54
  129.7 0.7 copy_bitcast_fusion.5
  130.4 22.6 %all-to-all-done.3 = bf16[128,3,1536]{2,1,0:T(4,128)(2,1)S(1)} async-done(((bf16[128,3,1536]{2,1,0:T(4,128)(2,1)}), bf16[128,3,1536]{2,1,0:T(4,128)(2,1)S(1)}, u32[]{:S(2)}, u32[]{:S(2)}) %all-to-all-start.3) | async-done | bytes 1179680 | tf_op jit(solution)/shard_map/all_to_all | solution.py:239
  153.0 1.8 %reduce_sum.101 = bf16[32,3,1536]{2,1,0:T(4,128)(2,1)} reduce(bf16[4,32,3,1536]{3,2,1,0:T(4,128)(2,1)S(1)} %bitcast.73, bf16[]{:T(256)} %constant.86.clone.1), dimensions={0}, to_apply=%region_7.8 | reduce | flops 442368 | bytes 1474562 | tf_op jit(solution)/shard_map/reduce_sum | solution.py:246
  154.9 1.2 fusion.49
  156.1 1.9 %multiply_reduce_fusion = (f32[32,3]{0,1:T(4,128)S(1)}, bf16[32,3,1536]{2,0,1:T(8,128)(2,1)}) fusion(f32[32,3]{0,1:T(4,128)S(1)} %broadcast_multiply_fusion.3, f32[32,3,1536]{2,0,1:T(8,128)S(1)} %get-tuple-element.38, bf16[32,3,1536]{2,1,0:T(4,128)(2,1)} %reduce_sum.101), kind=kLoop, calls=%fused_computation.31 | loop fusion | flops 884640 | bytes 1180416 | tf_op jit(solution)/shard_map/reduce_sum | solution.py:22
  158.0 0.9 fusion.19
  (61 shorter events, 5.4 us)
Async XLA Ops:
  0.6 120.0 %copy-start = (bf16[384,1536]{1,0:T(8,128)(2,1)S(1)}, bf16[384,1536]{1,0:T(8,128)(2,1)}, u32[]{:S(2)}) copy-start(bf16[384,1536]{1,0:T(8,128)(2,1)} %param.34) | copy-start | bytes 3538948
  0.6 3.7 %copy-start.2 = (bf16[32,3,1536]{2,0,1:T(8,128)(2,1)S(1)}, bf16[32,3,1536]{2,0,1:T(8,128)(2,1)}, u32[]{:S(2)}) copy-start(bf16[32,3,1536]{2,0,1:T(8,128)(2,1)} %param.18) | copy-start | bytes 884740
  3.3 2.8 %copy-start.9 = (f32[1536]{0:T(1024)S(1)}, f32[1536]{0:T(1024)}, u32[]{:S(2)}) copy-start(f32[1536]{0:T(1024)} %param.27) | copy-start | bytes 18436
  3.3 2.8 %copy-start.10 = (f32[1536]{0:T(1024)S(1)}, f32[1536]{0:T(1024)}, u32[]{:S(2)}) copy-start(f32[1536]{0:T(1024)} %param.26) | copy-start | bytes 18436
  79.4 3.6 %copy-start.8 = (f32[1536]{0:T(1024)S(1)}, f32[1536]{0:T(1024)}, u32[]{:S(2)}) copy-start(f32[1536]{0:T(1024)} %param.29) | copy-start | bytes 18436
  85.0 29.5 %all-to-all-start.2 = ((bf16[128,3,1536]{2,1,0:T(4,128)(2,1)}), bf16[128,3,1536]{2,1,0:T(4,128)(2,1)S(1)}, u32[]{:S(2)}, u32[]{:S(2)}) async-start(bf16[128,3,1536]{2,1,0:T(4,128)(2,1)} %bitcast.74), calls=%async_computation.2 | async-start | bytes 3145728 | tf_op jit(solution)/shard_map/all_to_all | solution.py:223
  116.6 2.5 %copy-start.3 = (bf16[1,512,384]{1,2,0:T(8,128)(2,1)S(1)}, bf16[1,512,384]{1,2,0:T(8,128)(2,1)}, u32[]{:S(2)}) copy-start(bf16[1,512,384]{1,2,0:T(8,128)(2,1)} %copy.63) | copy-start | bytes 1179652
  116.6 2.5 %copy-start.11 = (f32[384]{0:T(512)S(1)}, f32[384]{0:T(512)}, u32[]{:S(2)}) copy-start(f32[384]{0:T(512)} %param.31) | copy-start | bytes 4612
  119.1 1.0 copy-start.5
  123.5 29.5 %all-to-all-start.3 = ((bf16[128,3,1536]{2,1,0:T(4,128)(2,1)}), bf16[128,3,1536]{2,1,0:T(4,128)(2,1)S(1)}, u32[]{:S(2)}, u32[]{:S(2)}) async-start(bf16[128,3,1536]{2,1,0:T(4,128)(2,1)} %reshape.126), calls=%async_computation.3 | async-start | bytes 3145728 | tf_op jit(solution)/shard_map/all_to_all | solution.py:239
  153.0 4.9 %copy-start.12 = (f32[32]{0:T(128)S(1)}, f32[32]{0:T(128)}, u32[]{:S(2)}) copy-start(f32[32]{0:T(128)} %param.24) | copy-start | bytes 388
  154.8 3.1 %copy-start.1 = (bf16[32,3,1536]{2,1,0:T(4,128)(2,1)S(1)}, bf16[32,3,1536]{2,1,0:T(4,128)(2,1)}, u32[]{:S(2)}) copy-start(bf16[32,3,1536]{2,1,0:T(4,128)(2,1)} %reduce_sum.101) | copy-start | bytes 884740
  154.8 3.1 %copy-start.4 = (f32[32,1536]{1,0:T(8,128)S(1)}, f32[32,1536]{1,0:T(8,128)}, u32[]{:S(2)}) copy-start(f32[32,1536]{1,0:T(8,128)} %get-tuple-element.46) | copy-start | bytes 589828
  154.8 3.1 %copy-start.6 = (bf16[1536,64]{0,1:T(8,128)(2,1)S(1)}, bf16[1536,64]{0,1:T(8,128)(2,1)}, u32[]{:S(2)}) copy-start(bf16[1536,64]{0,1:T(8,128)(2,1)} %param.35) | copy-start | bytes 589828
  154.9 3.1 %copy-start.7 = (f32[32,3,64]{2,0,1:T(8,128)S(1)}, f32[32,3,64]{2,0,1:T(8,128)}, u32[]{:S(2)}) copy-start(f32[32,3,64]{2,0,1:T(8,128)} %param.19) | copy-start | bytes 73732

commit v4 on v3

--- a/solution.py
+++ b/solution.py
@@ -101,60 +101,88 @@
     return (mixture / jnp.transpose(totals)[:, :, None]).astype(jnp.bfloat16)
 
 
-def _qkv_kernel(x_ref, w_ref, cos_ref, sin_ref, gain_ref, o_ref):
-    section = pl.program_id(1)
-    projected = jnp.dot(x_ref[...], w_ref[...], preferred_element_type=jnp.float32)
-
-    @pl.when(section == 2)
+def _qkv_kernel(
+    tokens_ref, shift_ref, scale_ref, wq_ref, wk_ref, wv_ref, cos_ref, sin_ref, gain_ref,
+    o_ref, normed_ref,
+):
+    group = pl.program_id(0)
+    videos = shift_ref.shape[0]
+    per_video = tokens_ref.shape[0] // videos
+    group_width = wq_ref.shape[1]
+
+    @pl.when(group == 0)
     def _():
-        o_ref[0] = projected.astype(o_ref.dtype)
-
-    @pl.when(section < 2)
-    def _():
-        gains = gain_ref[pl.ds(jnp.minimum(section, 1), 1), :]
-        cosine = cos_ref[...]
-        sine_signed = sin_ref[...]
-        parts = []
-        for head in range(projected.shape[1] // HEAD_DIM):
-            lanes = slice(head * HEAD_DIM, (head + 1) * HEAD_DIM)
-            piece = projected[:, lanes]
-            mean_square = jnp.mean(piece * piece, axis=-1, keepdims=True)
-            normed = piece * lax.rsqrt(mean_square + EPSILON) * gains[:, lanes]
-            swapped = pltpu.roll(normed, HEAD_DIM // 2, 1)
-            parts.append(normed * cosine + swapped * sine_signed)
-        o_ref[0] = jnp.concatenate(parts, axis=-1).astype(o_ref.dtype)
-
-
-def pack_projected(block_in, cell_map, w_qkv, self_q_gain, self_k_gain, head_count):
-    videos, per_video, model_width = block_in.shape
-    rows = block_in.reshape(-1, model_width)
-    token_total = rows.shape[0]
+        shift = shift_ref[...]
+        scale = 1.0 + scale_ref[...]
+        for slot in range(per_video):
+            rows = slice(slot * videos, (slot + 1) * videos)
+            normed_ref[rows, :] = (layer_norm(tokens_ref[rows, :].astype(jnp.float32)) * scale + shift).astype(
+                normed_ref.dtype
+            )
+
+    block_in = normed_ref[...]
+    cosine = cos_ref[...]
+    sine_signed = sin_ref[...]
+    for section, w_ref in enumerate((wq_ref, wk_ref, wv_ref)):
+        projected = jnp.dot(block_in, w_ref[...], preferred_element_type=jnp.float32)
+        if section < 2:
+            gains = gain_ref[section : section + 1, :]
+            parts = []
+            for head in range(group_width // HEAD_DIM):
+                lanes = slice(head * HEAD_DIM, (head + 1) * HEAD_DIM)
+                piece = projected[:, lanes]
+                mean_square = jnp.mean(piece * piece, axis=-1, keepdims=True)
+                normed = piece * lax.rsqrt(mean_square + EPSILON) * gains[:, lanes]
+                swapped = pltpu.roll(normed, HEAD_DIM // 2, 1)
+                parts.append(normed * cosine + swapped * sine_signed)
+            projected = jnp.concatenate(parts, axis=-1)
+        result = projected.astype(o_ref.dtype)
+        for slot in range(per_video):
+            column = (slot * 3 + section) * group_width
+            o_ref[0, :, column : column + group_width] = result[slot * videos : (slot + 1) * videos, :]
+
+
+def pack_projected(hidden, block_modulation, cell_map, w_qkv, self_q_gain, self_k_gain, head_count):
+    videos, per_video, model_width = hidden.shape
+    tokens = jnp.transpose(hidden, (1, 0, 2)).reshape(-1, model_width)
+    token_total = tokens.shape[0]
     group_width = model_width // head_count
-    angles = rope_angles(cell_map).reshape(token_total, HEAD_DIM // 2)
+    angles = rope_angles(jnp.transpose(cell_map, (1, 0))).reshape(token_total, HEAD_DIM // 2)
     cosine = jnp.cos(angles)
     sine = jnp.sin(angles)
     cos_full = jnp.concatenate([cosine, cosine], axis=-1)
     sin_signed = jnp.concatenate([-sine, sine], axis=-1)
     gains = jnp.stack([self_q_gain, self_k_gain])
+    whole = lambda g: (0, 0)
     packed = pl.pallas_call(
         _qkv_kernel,
-        grid=(head_count, 3),
+        grid=(head_count,),
         in_specs=[
-            pl.BlockSpec((token_total, model_width), lambda g, s: (0, 0)),
-            pl.BlockSpec((model_width, group_width), lambda g, s: (0, s * head_count + g)),
-            pl.BlockSpec((token_total, HEAD_DIM), lambda g, s: (0, 0)),
-            pl.BlockSpec((token_total, HEAD_DIM), lambda g, s: (0, 0)),
-            pl.BlockSpec((2, group_width), lambda g, s: (0, g)),
+            pl.BlockSpec((token_total, model_width), whole),
+            pl.BlockSpec((videos, model_width), whole),
+            pl.BlockSpec((videos, model_width), whole),
+            pl.BlockSpec((model_width, group_width), lambda g: (0, g)),
+            pl.BlockSpec((model_width, group_width), lambda g: (0, head_count + g)),
+            pl.BlockSpec((model_width, group_width), lambda g: (0, 2 * head_count + g)),
+            pl.BlockSpec((token_total, HEAD_DIM), whole),
+            pl.BlockSpec((token_total, HEAD_DIM), whole),
+            pl.BlockSpec((2, group_width), lambda g: (0, g)),
         ],
-        out_specs=pl.BlockSpec((1, token_total, group_width), lambda g, s: (g, 0, s)),
-        out_shape=jax.ShapeDtypeStruct((head_count, token_total, 3 * group_width), jnp.bfloat16),
+        out_specs=pl.BlockSpec((1, videos, per_video * 3 * group_width), lambda g: (g, 0, 0)),
+        out_shape=jax.ShapeDtypeStruct(
+            (head_count, videos, per_video * 3 * group_width), jnp.bfloat16
+        ),
+        scratch_shapes=[pltpu.VMEM((token_total, model_width), jnp.bfloat16)],
         cost_estimate=pl.CostEstimate(
             flops=2 * token_total * model_width * 3 * model_width,
-            bytes_accessed=2 * model_width * 3 * model_width + 4 * token_total * 3 * model_width,
+            bytes_accessed=2 * model_width * 3 * model_width + 8 * token_total * 3 * model_width,
             transcendentals=0,
         ),
-    )(rows, w_qkv, cos_full, sin_signed, gains)
-    return packed.reshape(head_count, videos, per_video, 3 * group_width)
+    )(
+        tokens, block_modulation[:, 0], block_modulation[:, 1], w_qkv, w_qkv, w_qkv,
+        cos_full, sin_signed, gains,
+    )
+    return packed.reshape(head_count * videos, per_video * 3 * group_width)
 
 
 def local(
@@ -183,18 +211,11 @@
     group_heads = HEADS // head_count
     group_width = group_heads * HEAD_DIM
     stream = hidden.astype(jnp.float32)
-    block_shift = block_modulation[:, 0][:, None, :]
-    block_scale = block_modulation[:, 1][:, None, :]
     block_gate = block_modulation[:, 2][:, None, :]
-    block_in = (layer_norm(stream) * (1.0 + block_scale) + block_shift).astype(jnp.bfloat16)
-    packed = pack_projected(block_in, cell_map, w_qkv, self_q_gain, self_k_gain, head_count)
-    arrived = lax.all_to_all(
-        packed.reshape(head_count * videos, per_video, 3 * group_width),
-        ("head", "tile"),
-        split_axis=0,
-        concat_axis=0,
-        tiled=True,
-    )
+    packed = pack_projected(
+        hidden, block_modulation, cell_map, w_qkv, self_q_gain, self_k_gain, head_count
+    )
+    arrived = lax.all_to_all(packed, ("head", "tile"), split_axis=0, concat_axis=0, tiled=True)
     arrived = arrived.reshape(-1, 3, group_heads, HEAD_DIM)
     own_queries = arrived[:, 0]
     own_keys = arrived[:, 1]

time: 160 us -> 163 us (1.019)
  other arithmetic: 11.4 us -> 17.3 us
  local copies, waits for them, and re-layouts: 24.3 us -> 28.8 us
  Pallas kernels: 12.6 us -> 8.63 us
  blocking collectives: 48.3 us -> 45.6 us
    all_to_all x0 -> x2, other arithmetic: none -> 8.7 us  [local(): lax.all_to_all(packed, ('head', 'tile'), split_axis=0, concat_axis=0, til...]
    unnamed x30, local copies, waits for them, and re-layouts: 6.78 us -> 13.4 us
    pallas_call x1, Pallas kernels: 12.6 us -> 8.63 us  [pack_projected(): pl.pallas_call(_qkv_kernel, grid=(head_count,), in_specs=[pl.BlockSpec((t...]
    all_to_all x1, blocking collectives: 31.9 us -> 29.2 us  [local(): lax.all_to_all(packed, ('head', 'tile'), split_axis=0, concat_axis=0, til...]
    another operation x1 -> x0, local copies, waits for them, and re-layouts: 2.52 us -> none  [local(): packed.reshape(head_count * videos, per_video, 3 * group_width)]
    mul x0 -> x1, local copies, waits for them, and re-layouts: none -> 1.94 us  [local(): after_self = stream + block_gate * self_update]
where the time goes in v4:
time: 163 us; the launch traced here: 162 us
  blocking collectives  45.6 us (28%)
  waiting for transfers between devices  40.6 us (25%)
  local copies, waits for them, and re-layouts  28.8 us (18%)
  other arithmetic  17.3 us (11%)
  matrix products  9.81 us (6%)
  starting transfers between devices  9.53 us (6%)
  Pallas kernels  8.63 us (5%)
    all_to_all x1, blocking collectives, local(): lax.all_to_all(packed, ('head', 'tile'), split_axis=0, concat_axis=0, til...  29.2 us
    all_to_all x1, waiting for transfers between devices, local(): lax.all_to_all(partial.reshape(head_count * tile_count, per_video, model_...  22.7 us
    all_to_all x1, waiting for transfers between devices, local(): lax.all_to_all(copies, ('head', 'tile'), split_axis=0, concat_axis=0, til...  17.9 us
    all_to_all x1, blocking collectives, local(): lax.all_to_all(own_mixture.reshape(head_count * tile_count, per_video, gr...  16.5 us
    unnamed x30, local copies, waits for them, and re-layouts  13.4 us
    all_to_all x2, other arithmetic, local(): lax.all_to_all(packed, ('head', 'tile'), split_axis=0, concat_axis=0, til...  8.7 us
    pallas_call x1, Pallas kernels, pack_projected(): pl.pallas_call(_qkv_kernel, grid=(head_count,), in_specs=[pl.BlockSpec((t...  8.63 us
    all_to_all x1, starting transfers between devices, local(): lax.all_to_all(copies, ('head', 'tile'), split_axis=0, concat_axis=0, til...  4.85 us
  transfers between devices with their start and end apart: 2, of which 2 were waited for; matrix products, arithmetic and copies ran while one was open for 5% of the time, Pallas kernels for 0%

profile of v4, /device:TPU:1, one launch (start us, length us, event | category | flops | bytes accessed | tf_op | source)
XLA Modules:
  0.0 161.9 jit_solution(10752830859918025592)
XLA Ops:
  0.7 0.8 fusion.38
  1.7 1.9 %slice_bitcast_fusion.2 = (f32[32,1536]{1,0:T(8,128)}, f32[32,1536]{1,0:T(8,128)}, f32[32,1536]{1,0:T(8,128)}) fusion(f32[32,3,1536]{2,0,1:T(8,128)} %param.22), kind=kLoop, calls=%fused_computation.47 | loop fusion | bytes 1179648 | tf_op jit(solution)/shard_map/mul | solution.py:239
  3.7 0.7 stack.10
  6.1 0.7 pad_maximum_fusion.1
  6.9 8.6 %shard_map.185 = bf16[4,32,3456]{2,1,0:T(8,128)(2,1)} custom-call(bf16[96,1536]{1,0:T(8,128)(2,1)} %bitcast.116, f32[32,1536]{1,0:T(8,128)} %get-tuple-element.26.shift_ref, f32[32,1536]{1,0:T(8,128)} %get-tuple-element.25.scale_ref, bf16[1536,4608]{1,0:T(8,128)(2,1)} %wv_ref.1, bf16[1536,4608]{1,0:T(8,128)(2,1)} %wv_ref.1, bf16[1536,4608]{1,0:T(8,128)(2,1)} %wv_ref.1, ...), custom_call_target="tpu_custom_call" | custom-call | flops 1358954496 | bytes 17694720 | tf_op jit(solution)/shard_map/pallas_call | solution.py:157
  16.0 2.4 %reduce.2 = bf16[128,3456]{1,0:T(8,128)(2,1)S(1)} reduce(bf16[128,1,3456]{2,0,1:T(8,128)(2,1)} %bitcast.111, bf16[]{:T(256)} %broadcast.134), dimensions={1}, to_apply=%copy.42.reduce_sub_computation | reduce | bytes 1769474 | tf_op jit(solution)/shard_map/all_to_all | solution.py:218
  18.4 0.9 reshape.126
  19.3 29.2 %all_to_all.24 = bf16[128,2,1728]{2,1,0:T(2,128)(2,1)} all-to-all(bf16[128,2,1728]{2,1,0:T(2,128)(2,1)S(1)} %reshape.126), channel_id=1, replica_groups=mesh['head'=4,'tile'=32] {'head','tile'}, dimensions={0} | all-to-all | bytes 1769472 | tf_op jit(solution)/shard_map/all_to_all | solution.py:218
  48.5 5.8 %reshape.127 = bf16[128,1,3456]{2,1,0:T(2,128)(2,1)S(1)} reshape(bf16[128,2,1728]{2,1,0:T(2,128)(2,1)} %all_to_all.24) | data formatting | bytes 1769472
  54.3 6.3 %reduce.1 = bf16[128,3456]{1,0:T(8,128)(2,1)} reduce(bf16[128,1,3456]{2,1,0:T(2,128)(2,1)S(1)} %reshape.127, bf16[]{:T(256)} %constant.91), dimensions={1}, to_apply=%all_to_all.16.reduce_sub_computation | reduce | bytes 1769474 | tf_op jit(solution)/shard_map/all_to_all | solution.py:218
  60.6 2.5 %reshape.114 = bf16[384,3,3,128]{3,2,1,0:T(4,128)(2,1)S(1)} reshape(bf16[128,3456]{1,0:T(8,128)(2,1)} %reduce.1) | data formatting | bytes 1769472 | tf_op jit(solution)/shard_map/reshape | solution.py:219
  65.2 16.5 %all_to_all.25 = bf16[128,3,384]{2,1,0:T(4,128)(2,1)S(1)} all-to-all(bf16[128,3,384]{2,1,0:T(4,128)(2,1)S(1)} %reshape_reshape.3), channel_id=1, replica_groups=mesh['head'=4,'tile'=32] {'head','tile'}, dimensions={0} | all-to-all | bytes 589824 | tf_op jit(solution)/shard_map/all_to_all | solution.py:224
  82.1 3.3 %fusion.51 = (f32[32,3]{0,1:T(4,128)S(1)}, f32[32,3,1536]{2,0,1:T(8,128)S(1)}) fusion(bf16[32,3,1536]{2,0,1:T(8,128)(2,1)S(1)} %dot_general.34, bf16[1536,1536]{1,0:T(8,128)(2,1)} %param.28, f32[32,1536]{1,0:T(8,128)S(1)} %copy-done.4, bf16[32,3,1536]{2,0,1:T(8,128)(2,1)S(1)} %copy-done.3), kind=kOutput, calls=%fused_computation.91 | convolution fusion | flops 453574560 | bytes 6095232 | tf_op jit(solution)/shard_map/dot_general | solution.py:236
  86.1 1.6 broadcast_in_dim.5
  87.7 4.9 %all-to-all-start.2 = ((bf16[128,3,1536]{2,1,0:T(4,128)(2,1)}), bf16[128,3,1536]{2,1,0:T(4,128)(2,1)S(1)}, u32[]{:S(2)}, u32[]{:S(2)}) async-start(bf16[128,3,1536]{2,1,0:T(4,128)(2,1)} %bitcast.110), calls=%async_computation.2 | async-start | bytes 3145728 | tf_op jit(solution)/shard_map/all_to_all | solution.py:244
  92.5 2.4 %copy.50 = bf16[1536,384]{0,1:T(8,128)(2,1)} copy(bf16[1536,384]{1,0:T(8,128)(2,1)} %param.30) | data formatting | bytes 2359296 | tf_op args[12]
  95.6 1.9 %copy.51 = bf16[1,512,384]{1,2,0:T(8,128)(2,1)} copy(bf16[1,512,384]{2,1,0:T(8,128)(2,1)} %param.32) | data formatting | bytes 786432 | tf_op args[14]
  97.5 1.9 %copy.54 = bf16[1,512,384]{1,2,0:T(8,128)(2,1)} copy(bf16[1,512,384]{2,1,0:T(8,128)(2,1)} %param.33) | data formatting | bytes 786432 | tf_op args[15]
  99.4 17.9 %all-to-all-done.2 = bf16[128,3,1536]{2,1,0:T(4,128)(2,1)S(1)} async-done(((bf16[128,3,1536]{2,1,0:T(4,128)(2,1)}), bf16[128,3,1536]{2,1,0:T(4,128)(2,1)S(1)}, u32[]{:S(2)}, u32[]{:S(2)}) %all-to-all-start.2) | async-done | bytes 1179680 | tf_op jit(solution)/shard_map/all_to_all | solution.py:244
  117.4 2.2 %reshape.122 = bf16[384,1536,1]{1,0,2:T(8,128)(2,1)} reshape(bf16[128,3,1536]{2,1,0:T(4,128)(2,1)S(1)} %all-to-all-done.2) | data formatting | bytes 2359296 | tf_op jit(solution)/shard_map/reshape | solution.py:245
  119.5 2.5 %multiply_reduce_fusion.1 = (f32[384,3]{0,1:T(4,128)S(1)}, f32[384,3,128]{0,2,1:T(8,128)S(1)}) fusion(bf16[384,1536,1]{1,0,2:T(8,128)(2,1)} %reshape.122, bf16[3,128,1536]{2,1,0:T(8,128)(2,1)} %bitcast.114), kind=kOutput, calls=%fused_computation.26 | convolution fusion | flops 453278592 | bytes 2953728 | tf_op jit(solution)/shard_map/dot_general | solution.py:246
  122.0 0.8 fusion.8
  123.6 0.8 convolution_convert_fusion
  124.4 2.0 %reshape.119 = bf16[128,3,1536]{2,1,0:T(4,128)(2,1)} reshape(bf16[384,1536]{1,0:T(8,128)(2,1)S(1)} %convolution_convert_fusion) | data formatting | bytes 2359296 | tf_op jit(solution)/shard_map/reshape | solution.py:261
  126.4 4.7 %all-to-all-start.3 = ((bf16[128,3,1536]{2,1,0:T(4,128)(2,1)}), bf16[128,3,1536]{2,1,0:T(4,128)(2,1)S(1)}, u32[]{:S(2)}, u32[]{:S(2)}) async-start(bf16[128,3,1536]{2,1,0:T(4,128)(2,1)} %reshape.119), calls=%async_computation.3 | async-start | bytes 3145728 | tf_op jit(solution)/shard_map/all_to_all | solution.py:260
  131.1 1.5 fusion.50
  132.6 0.7 copy_bitcast_fusion.5
  133.3 22.7 %all-to-all-done.3 = bf16[128,3,1536]{2,1,0:T(4,128)(2,1)S(1)} async-done(((bf16[128,3,1536]{2,1,0:T(4,128)(2,1)}), bf16[128,3,1536]{2,1,0:T(4,128)(2,1)S(1)}, u32[]{:S(2)}, u32[]{:S(2)}) %all-to-all-start.3) | async-done | bytes 1179680 | tf_op jit(solution)/shard_map/all_to_all | solution.py:260
  156.0 1.8 %reduce_sum.81 = bf16[32,3,1536]{2,1,0:T(4,128)(2,1)} reduce(bf16[4,32,3,1536]{3,2,1,0:T(4,128)(2,1)S(1)} %bitcast.109, bf16[]{:T(256)} %constant.83.clone.1), dimensions={0}, to_apply=%region_5.6 | reduce | flops 442368 | bytes 1474562 | tf_op jit(solution)/shard_map/reduce_sum | solution.py:267
  157.8 1.2 fusion.45
  159.0 1.9 %multiply_reduce_fusion = (f32[32,3]{0,1:T(4,128)S(1)}, bf16[32,3,1536]{2,0,1:T(8,128)(2,1)}) fusion(f32[32,3]{0,1:T(4,128)S(1)} %broadcast_multiply_fusion.3, f32[32,3,1536]{2,0,1:T(8,128)S(1)} %get-tuple-element.38, bf16[32,3,1536]{2,1,0:T(4,128)(2,1)} %reduce_sum.81), kind=kLoop, calls=%fused_computation.23 | loop fusion | flops 884640 | bytes 1180416 | tf_op jit(solution)/shard_map/reduce_sum | solution.py:22
  160.9 0.9 fusion.19
  (53 shorter events, 6.4 us)
Async XLA Ops:
  0.6 122.9 %copy-start = (bf16[384,1536]{1,0:T(8,128)(2,1)S(1)}, bf16[384,1536]{1,0:T(8,128)(2,1)}, u32[]{:S(2)}) copy-start(bf16[384,1536]{1,0:T(8,128)(2,1)} %param.34) | copy-start | bytes 3538948
  64.7 17.4 %copy-start.3 = (bf16[32,3,1536]{2,0,1:T(8,128)(2,1)S(1)}, bf16[32,3,1536]{2,0,1:T(8,128)(2,1)}, u32[]{:S(2)}) copy-start(bf16[32,3,1536]{2,0,1:T(8,128)(2,1)} %param.18) | copy-start | bytes 884740
  64.7 17.4 %copy-start.4 = (f32[32,1536]{1,0:T(8,128)S(1)}, f32[32,1536]{1,0:T(8,128)}, u32[]{:S(2)}) copy-start(f32[32,1536]{1,0:T(8,128)} %get-tuple-element.24) | copy-start | bytes 589828
  82.1 3.6 %copy-start.9 = (f32[1536]{0:T(1024)S(1)}, f32[1536]{0:T(1024)}, u32[]{:S(2)}) copy-start(f32[1536]{0:T(1024)} %param.29) | copy-start | bytes 18436
  87.7 29.7 %all-to-all-start.2 = ((bf16[128,3,1536]{2,1,0:T(4,128)(2,1)}), bf16[128,3,1536]{2,1,0:T(4,128)(2,1)S(1)}, u32[]{:S(2)}, u32[]{:S(2)}) async-start(bf16[128,3,1536]{2,1,0:T(4,128)(2,1)} %bitcast.110), calls=%async_computation.2 | async-start | bytes 3145728 | tf_op jit(solution)/shard_map/all_to_all | solution.py:244
  119.5 2.5 %copy-start.2 = (bf16[1,512,384]{1,2,0:T(8,128)(2,1)S(1)}, bf16[1,512,384]{1,2,0:T(8,128)(2,1)}, u32[]{:S(2)}) copy-start(bf16[1,512,384]{1,2,0:T(8,128)(2,1)} %copy.51) | copy-start | bytes 1179652
  119.5 2.5 %copy-start.10 = (f32[384]{0:T(512)S(1)}, f32[384]{0:T(512)}, u32[]{:S(2)}) copy-start(f32[384]{0:T(512)} %param.31) | copy-start | bytes 4612
  122.0 1.0 copy-start.6
  126.4 29.5 %all-to-all-start.3 = ((bf16[128,3,1536]{2,1,0:T(4,128)(2,1)}), bf16[128,3,1536]{2,1,0:T(4,128)(2,1)S(1)}, u32[]{:S(2)}, u32[]{:S(2)}) async-start(bf16[128,3,1536]{2,1,0:T(4,128)(2,1)} %reshape.119), calls=%async_computation.3 | async-start | bytes 3145728 | tf_op jit(solution)/shard_map/all_to_all | solution.py:260
  155.9 4.9 %copy-start.11 = (f32[32]{0:T(128)S(1)}, f32[32]{0:T(128)}, u32[]{:S(2)}) copy-start(f32[32]{0:T(128)} %param.24) | copy-start | bytes 388
  157.8 3.1 %copy-start.1 = (bf16[32,3,1536]{2,1,0:T(4,128)(2,1)S(1)}, bf16[32,3,1536]{2,1,0:T(4,128)(2,1)}, u32[]{:S(2)}) copy-start(bf16[32,3,1536]{2,1,0:T(4,128)(2,1)} %reduce_sum.81) | copy-start | bytes 884740
  157.8 3.1 %copy-start.5 = (f32[32,1536]{1,0:T(8,128)S(1)}, f32[32,1536]{1,0:T(8,128)}, u32[]{:S(2)}) copy-start(f32[32,1536]{1,0:T(8,128)} %get-tuple-element.46) | copy-start | bytes 589828
  157.8 3.1 %copy-start.7 = (bf16[1536,64]{0,1:T(8,128)(2,1)S(1)}, bf16[1536,64]{0,1:T(8,128)(2,1)}, u32[]{:S(2)}) copy-start(bf16[1536,64]{0,1:T(8,128)(2,1)} %param.35) | copy-start | bytes 589828
  157.8 3.1 %copy-start.8 = (f32[32,3,64]{2,0,1:T(8,128)S(1)}, f32[32,3,64]{2,0,1:T(8,128)}, u32[]{:S(2)}) copy-start(f32[32,3,64]{2,0,1:T(8,128)} %param.19) | copy-start | bytes 73732

commit v5 on v3

--- a/solution.py
+++ b/solution.py
@@ -101,28 +101,27 @@
     return (mixture / jnp.transpose(totals)[:, :, None]).astype(jnp.bfloat16)
 
 
-def _qkv_kernel(x_ref, w_ref, cos_ref, sin_ref, gain_ref, o_ref):
-    section = pl.program_id(1)
-    projected = jnp.dot(x_ref[...], w_ref[...], preferred_element_type=jnp.float32)
-
-    @pl.when(section == 2)
-    def _():
-        o_ref[0] = projected.astype(o_ref.dtype)
-
-    @pl.when(section < 2)
-    def _():
-        gains = gain_ref[pl.ds(jnp.minimum(section, 1), 1), :]
-        cosine = cos_ref[...]
-        sine_signed = sin_ref[...]
-        parts = []
-        for head in range(projected.shape[1] // HEAD_DIM):
-            lanes = slice(head * HEAD_DIM, (head + 1) * HEAD_DIM)
-            piece = projected[:, lanes]
-            mean_square = jnp.mean(piece * piece, axis=-1, keepdims=True)
-            normed = piece * lax.rsqrt(mean_square + EPSILON) * gains[:, lanes]
-            swapped = pltpu.roll(normed, HEAD_DIM // 2, 1)
-            parts.append(normed * cosine + swapped * sine_signed)
-        o_ref[0] = jnp.concatenate(parts, axis=-1).astype(o_ref.dtype)
+def _qkv_kernel(x_ref, wq_ref, wk_ref, wv_ref, cos_ref, sin_ref, gain_ref, o_ref):
+    block_in = x_ref[...]
+    cosine = cos_ref[...]
+    sine_signed = sin_ref[...]
+    group_width = wq_ref.shape[1]
+    for section, w_ref in enumerate((wq_ref, wk_ref, wv_ref)):
+        projected = jnp.dot(block_in, w_ref[...], preferred_element_type=jnp.float32)
+        if section < 2:
+            gains = gain_ref[section : section + 1, :]
+            parts = []
+            for head in range(group_width // HEAD_DIM):
+                lanes = slice(head * HEAD_DIM, (head + 1) * HEAD_DIM)
+                piece = projected[:, lanes]
+                mean_square = jnp.mean(piece * piece, axis=-1, keepdims=True)
+                normed = piece * lax.rsqrt(mean_square + EPSILON) * gains[:, lanes]
+                swapped = pltpu.roll(normed, HEAD_DIM // 2, 1)
+                parts.append(normed * cosine + swapped * sine_signed)
+            projected = jnp.concatenate(parts, axis=-1)
+        o_ref[0, :, section * group_width : (section + 1) * group_width] = projected.astype(
+            o_ref.dtype
+        )
 
 
 def pack_projected(block_in, cell_map, w_qkv, self_q_gain, self_k_gain, head_count):
@@ -136,24 +135,27 @@
     cos_full = jnp.concatenate([cosine, cosine], axis=-1)
     sin_signed = jnp.concatenate([-sine, sine], axis=-1)
     gains = jnp.stack([self_q_gain, self_k_gain])
+    whole = lambda g: (0, 0)
     packed = pl.pallas_call(
         _qkv_kernel,
-        grid=(head_count, 3),
+        grid=(head_count,),
         in_specs=[
-            pl.BlockSpec((token_total, model_width), lambda g, s: (0, 0)),
-            pl.BlockSpec((model_width, group_width), lambda g, s: (0, s * head_count + g)),
-            pl.BlockSpec((token_total, HEAD_DIM), lambda g, s: (0, 0)),
-            pl.BlockSpec((token_total, HEAD_DIM), lambda g, s: (0, 0)),
-            pl.BlockSpec((2, group_width), lambda g, s: (0, g)),
+            pl.BlockSpec((token_total, model_width), whole),
+            pl.BlockSpec((model_width, group_width), lambda g: (0, g)),
+            pl.BlockSpec((model_width, group_width), lambda g: (0, head_count + g)),
+            pl.BlockSpec((model_width, group_width), lambda g: (0, 2 * head_count + g)),
+            pl.BlockSpec((token_total, HEAD_DIM), whole),
+            pl.BlockSpec((token_total, HEAD_DIM), whole),
+            pl.BlockSpec((2, group_width), lambda g: (0, g)),
         ],
-        out_specs=pl.BlockSpec((1, token_total, group_width), lambda g, s: (g, 0, s)),
+        out_specs=pl.BlockSpec((1, token_total, 3 * group_width), lambda g: (g, 0, 0)),
         out_shape=jax.ShapeDtypeStruct((head_count, token_total, 3 * group_width), jnp.bfloat16),
         cost_estimate=pl.CostEstimate(
             flops=2 * token_total * model_width * 3 * model_width,
             bytes_accessed=2 * model_width * 3 * model_width + 4 * token_total * 3 * model_width,
             transcendentals=0,
         ),
-    )(rows, w_qkv, cos_full, sin_signed, gains)
+    )(rows, w_qkv, w_qkv, w_qkv, cos_full, sin_signed, gains)
     return packed.reshape(head_count, videos, per_video, 3 * group_width)
 
 

time: 160 us -> 155 us (0.969)
  Pallas kernels: 12.6 us -> 8.22 us
    pallas_call x1, Pallas kernels: 12.6 us -> 8.22 us  [pack_projected(): pl.pallas_call(_qkv_kernel, grid=(head_count,), in_specs=[pl.BlockSpec((t...]
where the time goes in v5:
time: 155 us
  blocking collectives  48.3 us (31%)
  waiting for transfers between devices  40.5 us (26%)
  local copies, waits for them, and re-layouts  24.3 us (16%)
  other arithmetic  11.4 us (7%)
  matrix products  10.9 us (7%)
  starting transfers between devices  9.31 us (6%)
  Pallas kernels  8.22 us (5%)
  between operations  1.62 us (1%)
    all_to_all x1, blocking collectives, local(): lax.all_to_all(packed.reshape(head_count * videos, per_video, 3 * group_w...  32 us
    all_to_all x1, waiting for transfers between devices, local(): lax.all_to_all(partial.reshape(head_count * tile_count, per_video, model_...  22.6 us
    all_to_all x1, waiting for transfers between devices, local(): lax.all_to_all(copies, ('head', 'tile'), split_axis=0, concat_axis=0, til...  17.9 us
    all_to_all x1, blocking collectives, local(): lax.all_to_all(own_mixture.reshape(head_count * tile_count, per_video, gr...  16.4 us
    pallas_call x1, Pallas kernels, pack_projected(): pl.pallas_call(_qkv_kernel, grid=(head_count,), in_specs=[pl.BlockSpec((t...  8.22 us
    unnamed x30, local copies, waits for them, and re-layouts  6.78 us
    all_to_all x1, starting transfers between devices, local(): lax.all_to_all(partial.reshape(head_count * tile_count, per_video, model_...  4.68 us
    all_to_all x1, starting transfers between devices, local(): lax.all_to_all(copies, ('head', 'tile'), split_axis=0, concat_axis=0, til...  4.64 us
  transfers between devices with their start and end apart: 2, of which 2 were waited for; matrix products, arithmetic and copies ran while one was open for 5% of the time, Pallas kernels for 0%

profile of v5, /device:TPU:1, one launch (start us, length us, event | category | flops | bytes accessed | tf_op | source)
XLA Modules:
  0.0 154.6 jit_solution(2445306440850361775)
XLA Ops:
  0.7 0.8 fusion.42
  2.1 1.2 slice_bitcast_fusion.1
  3.3 1.1 convert_reduce_fusion
  5.1 1.0 reshape.120.x_ref
  7.2 0.7 pad_maximum_fusion.1
  7.9 8.2 %shard_map.185 = bf16[4,96,1152]{2,1,0:T(8,128)(2,1)} custom-call(bf16[96,1536]{1,0:T(8,128)(2,1)} %reshape.120.x_ref, bf16[1536,4608]{1,0:T(8,128)(2,1)} %wv_ref.1, bf16[1536,4608]{1,0:T(8,128)(2,1)} %wv_ref.1, bf16[1536,4608]{1,0:T(8,128)(2,1)} %wv_ref.1, f32[96,128]{1,0:T(8,128)} %get-tuple-element.43.cos_ref, f32[96,128]{1,0:T(8,128)} %get-tuple-element.44.sin_ref, ...), custom_call_target="tpu_custom_call" | custom-call | flops 1358954496 | bytes 15925248 | tf_op jit(solution)/shard_map/pallas_call | solution.py:139
  16.2 2.5 %reshape_reshape.6 = bf16[128,3,1152]{2,1,0:T(4,128)(2,1)S(1)} reshape(bf16[4,96,1152]{2,1,0:T(8,128)(2,1)} %shard_map.185) | data formatting | bytes 1769472 | tf_op jit(solution)/shard_map/reshape;reshape | solution.py:194
  18.7 32.0 %all_to_all.20 = bf16[128,3,1152]{2,1,0:T(4,128)(2,1)} all-to-all(bf16[128,3,1152]{2,1,0:T(4,128)(2,1)S(1)} %reshape_reshape.6), channel_id=1, replica_groups=mesh['head'=4,'tile'=32] {'head','tile'}, dimensions={0} | all-to-all | bytes 1769472 | tf_op jit(solution)/shard_map/all_to_all | solution.py:193
  50.6 3.5 %reshape.121 = bf16[384,3,3,128]{3,2,1,0:T(4,128)(2,1)S(1)} reshape(bf16[128,3,1152]{2,1,0:T(4,128)(2,1)} %all_to_all.20) | data formatting | bytes 1769472 | tf_op jit(solution)/shard_map/reshape | solution.py:200
  54.1 1.3 fusion.53
  55.7 1.6 %fusion.10 = (f32[3,384]{1,0:T(4,128)S(1)}, f32[3,384,384]{1,2,0:T(8,128)S(1)}) fusion(bf16[384,1,3,128]{3,2,1,0:T(4,128)(2,1)} %get-tuple-element.20, bf16[384,1,3,128]{3,2,1,0:T(4,128)(2,1)} %get-tuple-element.21), kind=kOutput, calls=%fused_computation.9 | convolution fusion | flops 114129792 | bytes 2363904 | tf_op jit(solution)/shard_map/while/body/eval_jaxpr/qhd,khd->hqk/dot_general | solution.py:73
  58.3 16.4 %all_to_all.21 = bf16[128,3,384]{2,1,0:T(4,128)(2,1)S(1)} all-to-all(bf16[128,3,384]{2,1,0:T(4,128)(2,1)S(1)} %reshape_reshape.7), channel_id=1, replica_groups=mesh['head'=4,'tile'=32] {'head','tile'}, dimensions={0} | all-to-all | bytes 589824 | tf_op jit(solution)/shard_map/all_to_all | solution.py:205
  75.1 3.3 %fusion.55 = (f32[32,3]{0,1:T(4,128)S(1)}, f32[32,3,1536]{2,0,1:T(8,128)S(1)}) fusion(bf16[32,3,1536]{2,0,1:T(8,128)(2,1)S(1)} %dot_general.34, bf16[1536,1536]{1,0:T(8,128)(2,1)} %param.28, f32[32,1536]{1,0:T(8,128)S(1)} %get-tuple-element.24, bf16[32,3,1536]{2,0,1:T(8,128)(2,1)S(1)} %copy-done.2), kind=kOutput, calls=%fused_computation.98 | convolution fusion | flops 453574560 | bytes 6095232 | tf_op jit(solution)/shard_map/dot_general | solution.py:217
  79.0 1.6 %broadcast_in_dim.5 = bf16[4,32,3,1536]{3,2,1,0:T(4,128)(2,1)} broadcast(bf16[32,3,1536]{2,1,0:T(4,128)(2,1)S(1)} %copy.61), dimensions={1,2,3} | broadcast | bytes 1474560 | tf_op jit(solution)/shard_map/broadcast_in_dim | solution.py:222
  80.6 4.6 %all-to-all-start.2 = ((bf16[128,3,1536]{2,1,0:T(4,128)(2,1)}), bf16[128,3,1536]{2,1,0:T(4,128)(2,1)S(1)}, u32[]{:S(2)}, u32[]{:S(2)}) async-start(bf16[128,3,1536]{2,1,0:T(4,128)(2,1)} %bitcast.74), calls=%async_computation.2 | async-start | bytes 3145728 | tf_op jit(solution)/shard_map/all_to_all | solution.py:225
  85.2 2.4 %copy.62 = bf16[1536,384]{0,1:T(8,128)(2,1)} copy(bf16[1536,384]{1,0:T(8,128)(2,1)} %param.30) | data formatting | bytes 2359296 | tf_op args[12]
  88.3 1.9 %copy.63 = bf16[1,512,384]{1,2,0:T(8,128)(2,1)} copy(bf16[1,512,384]{2,1,0:T(8,128)(2,1)} %param.32) | data formatting | bytes 786432 | tf_op args[14]
  90.3 1.9 %copy.66 = bf16[1,512,384]{1,2,0:T(8,128)(2,1)} copy(bf16[1,512,384]{2,1,0:T(8,128)(2,1)} %param.33) | data formatting | bytes 786432 | tf_op args[15]
  92.2 17.9 %all-to-all-done.2 = bf16[128,3,1536]{2,1,0:T(4,128)(2,1)S(1)} async-done(((bf16[128,3,1536]{2,1,0:T(4,128)(2,1)}), bf16[128,3,1536]{2,1,0:T(4,128)(2,1)S(1)}, u32[]{:S(2)}, u32[]{:S(2)}) %all-to-all-start.2) | async-done | bytes 1179680 | tf_op jit(solution)/shard_map/all_to_all | solution.py:225
  110.1 2.2 %reshape.129 = bf16[384,1536,1]{1,0,2:T(8,128)(2,1)} reshape(bf16[128,3,1536]{2,1,0:T(4,128)(2,1)S(1)} %all-to-all-done.2) | data formatting | bytes 2359296 | tf_op jit(solution)/shard_map/reshape | solution.py:226
  112.2 2.5 %multiply_reduce_fusion.1 = (f32[384,3]{0,1:T(4,128)S(1)}, f32[384,3,128]{0,2,1:T(8,128)S(1)}) fusion(bf16[384,1536,1]{1,0,2:T(8,128)(2,1)} %reshape.129, bf16[3,128,1536]{2,1,0:T(8,128)(2,1)} %bitcast.77), kind=kOutput, calls=%fused_computation.34 | convolution fusion | flops 453278592 | bytes 2953728 | tf_op jit(solution)/shard_map/dot_general | solution.py:227
  114.8 0.8 fusion.8
  116.3 0.8 convolution_convert_fusion
  117.1 2.0 %reshape.126 = bf16[128,3,1536]{2,1,0:T(4,128)(2,1)} reshape(bf16[384,1536]{1,0:T(8,128)(2,1)S(1)} %convolution_convert_fusion) | data formatting | bytes 2359296 | tf_op jit(solution)/shard_map/reshape | solution.py:242
  119.1 4.7 %all-to-all-start.3 = ((bf16[128,3,1536]{2,1,0:T(4,128)(2,1)}), bf16[128,3,1536]{2,1,0:T(4,128)(2,1)S(1)}, u32[]{:S(2)}, u32[]{:S(2)}) async-start(bf16[128,3,1536]{2,1,0:T(4,128)(2,1)} %reshape.126), calls=%async_computation.3 | async-start | bytes 3145728 | tf_op jit(solution)/shard_map/all_to_all | solution.py:241
  123.8 1.5 fusion.54
  125.3 0.7 copy_bitcast_fusion.5
  126.0 22.6 %all-to-all-done.3 = bf16[128,3,1536]{2,1,0:T(4,128)(2,1)S(1)} async-done(((bf16[128,3,1536]{2,1,0:T(4,128)(2,1)}), bf16[128,3,1536]{2,1,0:T(4,128)(2,1)S(1)}, u32[]{:S(2)}, u32[]{:S(2)}) %all-to-all-start.3) | async-done | bytes 1179680 | tf_op jit(solution)/shard_map/all_to_all | solution.py:241
  148.7 1.8 %reduce_sum.101 = bf16[32,3,1536]{2,1,0:T(4,128)(2,1)} reduce(bf16[4,32,3,1536]{3,2,1,0:T(4,128)(2,1)S(1)} %bitcast.73, bf16[]{:T(256)} %constant.86.clone.1), dimensions={0}, to_apply=%region_7.8 | reduce | flops 442368 | bytes 1474562 | tf_op jit(solution)/shard_map/reduce_sum | solution.py:248
  150.5 1.2 fusion.49
  151.7 1.9 %multiply_reduce_fusion = (f32[32,3]{0,1:T(4,128)S(1)}, bf16[32,3,1536]{2,0,1:T(8,128)(2,1)}) fusion(f32[32,3]{0,1:T(4,128)S(1)} %broadcast_multiply_fusion.3, f32[32,3,1536]{2,0,1:T(8,128)S(1)} %get-tuple-element.38, bf16[32,3,1536]{2,1,0:T(4,128)(2,1)} %reduce_sum.101), kind=kLoop, calls=%fused_computation.31 | loop fusion | flops 884640 | bytes 1180416 | tf_op jit(solution)/shard_map/reduce_sum | solution.py:22
  153.6 0.9 fusion.19
  (61 shorter events, 5.4 us)
Async XLA Ops:
  0.6 115.6 %copy-start = (bf16[384,1536]{1,0:T(8,128)(2,1)S(1)}, bf16[384,1536]{1,0:T(8,128)(2,1)}, u32[]{:S(2)}) copy-start(bf16[384,1536]{1,0:T(8,128)(2,1)} %param.34) | copy-start | bytes 3538948
  0.6 3.7 %copy-start.2 = (bf16[32,3,1536]{2,0,1:T(8,128)(2,1)S(1)}, bf16[32,3,1536]{2,0,1:T(8,128)(2,1)}, u32[]{:S(2)}) copy-start(bf16[32,3,1536]{2,0,1:T(8,128)(2,1)} %param.18) | copy-start | bytes 884740
  3.3 2.8 %copy-start.9 = (f32[1536]{0:T(1024)S(1)}, f32[1536]{0:T(1024)}, u32[]{:S(2)}) copy-start(f32[1536]{0:T(1024)} %param.27) | copy-start | bytes 18436
  3.3 2.8 %copy-start.10 = (f32[1536]{0:T(1024)S(1)}, f32[1536]{0:T(1024)}, u32[]{:S(2)}) copy-start(f32[1536]{0:T(1024)} %param.26) | copy-start | bytes 18436
  75.0 3.6 %copy-start.8 = (f32[1536]{0:T(1024)S(1)}, f32[1536]{0:T(1024)}, u32[]{:S(2)}) copy-start(f32[1536]{0:T(1024)} %param.29) | copy-start | bytes 18436
  80.6 29.5 %all-to-all-start.2 = ((bf16[128,3,1536]{2,1,0:T(4,128)(2,1)}), bf16[128,3,1536]{2,1,0:T(4,128)(2,1)S(1)}, u32[]{:S(2)}, u32[]{:S(2)}) async-start(bf16[128,3,1536]{2,1,0:T(4,128)(2,1)} %bitcast.74), calls=%async_computation.2 | async-start | bytes 3145728 | tf_op jit(solution)/shard_map/all_to_all | solution.py:225
  112.2 2.5 %copy-start.3 = (bf16[1,512,384]{1,2,0:T(8,128)(2,1)S(1)}, bf16[1,512,384]{1,2,0:T(8,128)(2,1)}, u32[]{:S(2)}) copy-start(bf16[1,512,384]{1,2,0:T(8,128)(2,1)} %copy.63) | copy-start | bytes 1179652
  112.2 2.5 %copy-start.11 = (f32[384]{0:T(512)S(1)}, f32[384]{0:T(512)}, u32[]{:S(2)}) copy-start(f32[384]{0:T(512)} %param.31) | copy-start | bytes 4612
  114.7 1.0 copy-start.5
  119.1 29.5 %all-to-all-start.3 = ((bf16[128,3,1536]{2,1,0:T(4,128)(2,1)}), bf16[128,3,1536]{2,1,0:T(4,128)(2,1)S(1)}, u32[]{:S(2)}, u32[]{:S(2)}) async-start(bf16[128,3,1536]{2,1,0:T(4,128)(2,1)} %reshape.126), calls=%async_computation.3 | async-start | bytes 3145728 | tf_op jit(solution)/shard_map/all_to_all | solution.py:241
  148.7 4.9 %copy-start.12 = (f32[32]{0:T(128)S(1)}, f32[32]{0:T(128)}, u32[]{:S(2)}) copy-start(f32[32]{0:T(128)} %param.24) | copy-start | bytes 388
  150.5 3.1 %copy-start.1 = (bf16[32,3,1536]{2,1,0:T(4,128)(2,1)S(1)}, bf16[32,3,1536]{2,1,0:T(4,128)(2,1)}, u32[]{:S(2)}) copy-start(bf16[32,3,1536]{2,1,0:T(4,128)(2,1)} %reduce_sum.101) | copy-start | bytes 884740
  150.5 3.1 %copy-start.4 = (f32[32,1536]{1,0:T(8,128)S(1)}, f32[32,1536]{1,0:T(8,128)}, u32[]{:S(2)}) copy-start(f32[32,1536]{1,0:T(8,128)} %get-tuple-element.46) | copy-start | bytes 589828
  150.5 3.1 %copy-start.6 = (bf16[1536,64]{0,1:T(8,128)(2,1)S(1)}, bf16[1536,64]{0,1:T(8,128)(2,1)}, u32[]{:S(2)}) copy-start(bf16[1536,64]{0,1:T(8,128)(2,1)} %param.35) | copy-start | bytes 589828
  150.5 3.1 %copy-start.7 = (f32[32,3,64]{2,0,1:T(8,128)S(1)}, f32[32,3,64]{2,0,1:T(8,128)}, u32[]{:S(2)}) copy-start(f32[32,3,64]{2,0,1:T(8,128)} %param.19) | copy-start | bytes 73732

commit v6 on v5

--- a/solution.py
+++ b/solution.py
@@ -64,27 +64,39 @@
     )
 
 
-def attend_self(queries, keys_own, values_own):
-    factor = 1.0 / math.sqrt(queries.shape[-1])
-    token_total = queries.shape[0]
-
-    def one_block(block_queries):
+def _self_attention_kernel(x_ref, o_ref):
+    group_width = o_ref.shape[1]
+    factor = 1.0 / math.sqrt(HEAD_DIM)
+    for head in range(group_width // HEAD_DIM):
+        lanes = slice(head * HEAD_DIM, (head + 1) * HEAD_DIM)
+        queries = x_ref[:, head * HEAD_DIM : (head + 1) * HEAD_DIM]
+        keys = x_ref[:, group_width + head * HEAD_DIM : group_width + (head + 1) * HEAD_DIM]
+        values = x_ref[:, 2 * group_width + head * HEAD_DIM : 2 * group_width + (head + 1) * HEAD_DIM]
         scores = (
-            jnp.einsum("qhd,khd->hqk", block_queries, keys_own, preferred_element_type=jnp.float32)
+            lax.dot_general(
+                queries, keys, (((1,), (1,)), ((), ())), preferred_element_type=jnp.float32
+            )
             * factor
         )
         weights = jnp.exp(scores)
-        totals = jnp.sum(weights, axis=-1)
-        mixture = jnp.einsum(
-            "hqk,khd->qhd",
-            weights.astype(jnp.bfloat16),
-            values_own,
-            preferred_element_type=jnp.float32,
+        totals = jnp.sum(weights, axis=-1, keepdims=True)
+        mixture = jnp.dot(
+            weights.astype(jnp.bfloat16), values, preferred_element_type=jnp.float32
         )
-        return (mixture / jnp.transpose(totals)[:, :, None]).astype(jnp.bfloat16)
-
-    blocked = queries.reshape((token_total // token_total, token_total) + queries.shape[1:])
-    return lax.map(one_block, blocked).reshape(queries.shape)
+        o_ref[:, lanes] = (mixture / totals).astype(o_ref.dtype)
+
+
+def attend_self(arrived, group_width):
+    token_total = arrived.shape[0]
+    return pl.pallas_call(
+        _self_attention_kernel,
+        out_shape=jax.ShapeDtypeStruct((token_total, group_width), jnp.bfloat16),
+        cost_estimate=pl.CostEstimate(
+            flops=4 * token_total * token_total * group_width,
+            bytes_accessed=2 * token_total * 4 * group_width,
+            transcendentals=token_total * token_total * (group_width // HEAD_DIM),
+        ),
+    )(arrived)
 
 
 def attend_text(queries, keys_own, values_own, length):
@@ -197,11 +209,7 @@
         concat_axis=0,
         tiled=True,
     )
-    arrived = arrived.reshape(-1, 3, group_heads, HEAD_DIM)
-    own_queries = arrived[:, 0]
-    own_keys = arrived[:, 1]
-    own_values = arrived[:, 2]
-    own_mixture = attend_self(own_queries, own_keys, own_values)
+    own_mixture = attend_self(arrived.reshape(-1, 3 * group_width), group_width)
     returned = lax.all_to_all(
         own_mixture.reshape(head_count * tile_count, per_video, group_width),
         ("head", "tile"),

time: 155 us -> 155 us (level)
  Pallas kernels: 8.22 us -> 10.9 us
  matrix products: 10.9 us -> 8.92 us
    pallas_call x0 -> x1, Pallas kernels: none -> 2.73 us  [attend_self(): pl.pallas_call(_self_attention_kernel, out_shape=jax.ShapeDtypeStruct((to...]
    dot_general x2 -> x0, matrix products: 2 us -> none  [the longest x1 1.56 us: one_block(): jnp.einsum('qhd,khd->hqk', block_queries, keys_own, preferred_element_typ...]
    reshape x1 -> x2, local copies, waits for them, and re-layouts: 3.48 us -> 4.4 us  [the longest x1 3.3 us: local(): own_mixture = attend_self(arrived.reshape(-1, 3 * group_width), group_width)]
    unnamed x30 -> x29, local copies, waits for them, and re-layouts: 6.78 us -> 6.47 us
where the time goes in v6:
time: 155 us; the launch traced here: 154 us
  blocking collectives  48.3 us (31%)
  waiting for transfers between devices  40.6 us (26%)
  local copies, waits for them, and re-layouts  23.1 us (15%)
  other arithmetic  11.4 us (7%)
  Pallas kernels  10.9 us (7%)
  starting transfers between devices  9.49 us (6%)
  matrix products  8.92 us (6%)
  between operations  1.59 us (1%)
    all_to_all x1, blocking collectives, local(): lax.all_to_all(packed.reshape(head_count * videos, per_video, 3 * group_w...  32 us
    all_to_all x1, waiting for transfers between devices, local(): lax.all_to_all(partial.reshape(head_count * tile_count, per_video, model_...  22.7 us
    all_to_all x1, waiting for transfers between devices, local(): lax.all_to_all(copies, ('head', 'tile'), split_axis=0, concat_axis=0, til...  17.9 us
    all_to_all x1, blocking collectives, local(): lax.all_to_all(own_mixture.reshape(head_count * tile_count, per_video, gr...  16.4 us
    pallas_call x1, Pallas kernels, pack_projected(): pl.pallas_call(_qkv_kernel, grid=(head_count,), in_specs=[pl.BlockSpec((t...  8.22 us
    unnamed x29, local copies, waits for them, and re-layouts  6.47 us
    all_to_all x1, starting transfers between devices, local(): lax.all_to_all(partial.reshape(head_count * tile_count, per_video, model_...  4.86 us
    all_to_all x1, starting transfers between devices, local(): lax.all_to_all(copies, ('head', 'tile'), split_axis=0, concat_axis=0, til...  4.63 us
  transfers between devices with their start and end apart: 2, of which 2 were waited for; matrix products, arithmetic and copies ran while one was open for 5% of the time, Pallas kernels for 0%

profile of v6, /device:TPU:1, one launch (start us, length us, event | category | flops | bytes accessed | tf_op | source)
XLA Modules:
  0.0 154.3 jit_solution(6548793800062468835)
XLA Ops:
  0.7 0.8 fusion.34
  2.1 1.2 slice_bitcast_fusion.1
  3.3 1.1 convert_reduce_fusion
  5.1 1.0 reshape.120.x_ref
  7.2 0.7 pad_maximum_fusion.1
  7.9 8.2 %shard_map.185 = bf16[4,96,1152]{2,1,0:T(8,128)(2,1)} custom-call(bf16[96,1536]{1,0:T(8,128)(2,1)} %reshape.120.x_ref, bf16[1536,4608]{1,0:T(8,128)(2,1)} %wv_ref.1, bf16[1536,4608]{1,0:T(8,128)(2,1)} %wv_ref.1, bf16[1536,4608]{1,0:T(8,128)(2,1)} %wv_ref.1, f32[96,128]{1,0:T(8,128)} %get-tuple-element.23.cos_ref, f32[96,128]{1,0:T(8,128)} %get-tuple-element.24.sin_ref, ...), custom_call_target="tpu_custom_call" | custom-call | flops 1358954496 | bytes 15925248 | tf_op jit(solution)/shard_map/pallas_call | solution.py:151
  16.2 2.5 %reshape_reshape.3 = bf16[128,3,1152]{2,1,0:T(4,128)(2,1)S(1)} reshape(bf16[4,96,1152]{2,1,0:T(8,128)(2,1)} %shard_map.185) | data formatting | bytes 1769472 | tf_op jit(solution)/shard_map/reshape;reshape | solution.py:206
  18.7 32.0 %all_to_all.20 = bf16[128,3,1152]{2,1,0:T(4,128)(2,1)} all-to-all(bf16[128,3,1152]{2,1,0:T(4,128)(2,1)S(1)} %reshape_reshape.3), channel_id=1, replica_groups=mesh['head'=4,'tile'=32] {'head','tile'}, dimensions={0} | all-to-all | bytes 1769472 | tf_op jit(solution)/shard_map/all_to_all | solution.py:205
  50.7 3.3 %reshape.121.x_ref = bf16[384,1152]{1,0:T(8,128)(2,1)} reshape(bf16[128,3,1152]{2,1,0:T(4,128)(2,1)} %all_to_all.20) | data formatting | bytes 1769472 | tf_op jit(solution)/shard_map/reshape | solution.py:212
  54.0 2.7 %shard_map.186 = bf16[384,384]{1,0:T(8,128)(2,1)} custom-call(bf16[384,1152]{1,0:T(8,128)(2,1)} %reshape.121.x_ref), custom_call_target="tpu_custom_call" | custom-call | flops 226492416 | bytes 1179648 | tf_op jit(solution)/shard_map/pallas_call | solution.py:91
  56.7 1.1 reshape.122
  57.8 16.4 %all_to_all.21 = bf16[128,3,384]{2,1,0:T(4,128)(2,1)S(1)} all-to-all(bf16[128,3,384]{2,1,0:T(4,128)(2,1)S(1)} %reshape.122), channel_id=1, replica_groups=mesh['head'=4,'tile'=32] {'head','tile'}, dimensions={0} | all-to-all | bytes 589824 | tf_op jit(solution)/shard_map/all_to_all | solution.py:213
  74.6 3.3 %fusion.45 = (f32[32,3]{0,1:T(4,128)S(1)}, f32[32,3,1536]{2,0,1:T(8,128)S(1)}) fusion(bf16[32,3,1536]{2,0,1:T(8,128)(2,1)S(1)} %dot_general.24, bf16[1536,1536]{1,0:T(8,128)(2,1)} %param.28, f32[32,1536]{1,0:T(8,128)S(1)} %get-tuple-element.6, bf16[32,3,1536]{2,0,1:T(8,128)(2,1)S(1)} %copy-done.2), kind=kOutput, calls=%fused_computation.85 | convolution fusion | flops 453574560 | bytes 6095232 | tf_op jit(solution)/shard_map/dot_general | solution.py:225
  78.5 1.6 %broadcast_in_dim.2 = bf16[4,32,3,1536]{3,2,1,0:T(4,128)(2,1)} broadcast(bf16[32,3,1536]{2,1,0:T(4,128)(2,1)S(1)} %copy.49), dimensions={1,2,3} | broadcast | bytes 1474560 | tf_op jit(solution)/shard_map/broadcast_in_dim | solution.py:230
  80.1 4.6 %all-to-all-start.2 = ((bf16[128,3,1536]{2,1,0:T(4,128)(2,1)}), bf16[128,3,1536]{2,1,0:T(4,128)(2,1)S(1)}, u32[]{:S(2)}, u32[]{:S(2)}) async-start(bf16[128,3,1536]{2,1,0:T(4,128)(2,1)} %bitcast.54), calls=%async_computation.2 | async-start | bytes 3145728 | tf_op jit(solution)/shard_map/all_to_all | solution.py:233
  84.7 2.4 %copy.50 = bf16[1536,384]{0,1:T(8,128)(2,1)} copy(bf16[1536,384]{1,0:T(8,128)(2,1)} %param.30) | data formatting | bytes 2359296 | tf_op args[12]
  87.8 1.9 %copy.51 = bf16[1,512,384]{1,2,0:T(8,128)(2,1)} copy(bf16[1,512,384]{2,1,0:T(8,128)(2,1)} %param.32) | data formatting | bytes 786432 | tf_op args[14]
  89.7 1.9 %copy.54 = bf16[1,512,384]{1,2,0:T(8,128)(2,1)} copy(bf16[1,512,384]{2,1,0:T(8,128)(2,1)} %param.33) | data formatting | bytes 786432 | tf_op args[15]
  91.6 17.9 %all-to-all-done.2 = bf16[128,3,1536]{2,1,0:T(4,128)(2,1)S(1)} async-done(((bf16[128,3,1536]{2,1,0:T(4,128)(2,1)}), bf16[128,3,1536]{2,1,0:T(4,128)(2,1)S(1)}, u32[]{:S(2)}, u32[]{:S(2)}) %all-to-all-start.2) | async-done | bytes 1179680 | tf_op jit(solution)/shard_map/all_to_all | solution.py:233
  109.6 2.2 %reshape.130 = bf16[384,1536,1]{1,0,2:T(8,128)(2,1)} reshape(bf16[128,3,1536]{2,1,0:T(4,128)(2,1)S(1)} %all-to-all-done.2) | data formatting | bytes 2359296 | tf_op jit(solution)/shard_map/reshape | solution.py:234
  111.7 2.5 %multiply_reduce_fusion.1 = (f32[384,3]{0,1:T(4,128)S(1)}, f32[384,3,128]{0,2,1:T(8,128)S(1)}) fusion(bf16[384,1536,1]{1,0,2:T(8,128)(2,1)} %reshape.130, bf16[3,128,1536]{2,1,0:T(8,128)(2,1)} %bitcast.57), kind=kOutput, calls=%fused_computation.27 | convolution fusion | flops 453278592 | bytes 2953728 | tf_op jit(solution)/shard_map/dot_general | solution.py:235
  114.3 0.8 fusion.8
  115.8 0.8 convolution_convert_fusion
  116.6 2.0 %reshape.127 = bf16[128,3,1536]{2,1,0:T(4,128)(2,1)} reshape(bf16[384,1536]{1,0:T(8,128)(2,1)S(1)} %convolution_convert_fusion) | data formatting | bytes 2359296 | tf_op jit(solution)/shard_map/reshape | solution.py:250
  118.7 4.9 %all-to-all-start.3 = ((bf16[128,3,1536]{2,1,0:T(4,128)(2,1)}), bf16[128,3,1536]{2,1,0:T(4,128)(2,1)S(1)}, u32[]{:S(2)}, u32[]{:S(2)}) async-start(bf16[128,3,1536]{2,1,0:T(4,128)(2,1)} %reshape.127), calls=%async_computation.3 | async-start | bytes 3145728 | tf_op jit(solution)/shard_map/all_to_all | solution.py:249
  123.5 1.5 fusion.44
  125.0 0.7 copy_bitcast_fusion.1
  125.7 22.7 %all-to-all-done.3 = bf16[128,3,1536]{2,1,0:T(4,128)(2,1)S(1)} async-done(((bf16[128,3,1536]{2,1,0:T(4,128)(2,1)}), bf16[128,3,1536]{2,1,0:T(4,128)(2,1)S(1)}, u32[]{:S(2)}, u32[]{:S(2)}) %all-to-all-start.3) | async-done | bytes 1179680 | tf_op jit(solution)/shard_map/all_to_all | solution.py:249
  148.4 1.8 %reduce_sum.90 = bf16[32,3,1536]{2,1,0:T(4,128)(2,1)} reduce(bf16[4,32,3,1536]{3,2,1,0:T(4,128)(2,1)S(1)} %bitcast.53, bf16[]{:T(256)} %constant.72.clone.1), dimensions={0}, to_apply=%region_6.7 | reduce | flops 442368 | bytes 1474562 | tf_op jit(solution)/shard_map/reduce_sum | solution.py:256
  150.2 1.2 fusion.40
  151.4 1.9 %multiply_reduce_fusion = (f32[32,3]{0,1:T(4,128)S(1)}, bf16[32,3,1536]{2,0,1:T(8,128)(2,1)}) fusion(f32[32,3]{0,1:T(4,128)S(1)} %broadcast_multiply_fusion.3, f32[32,3,1536]{2,0,1:T(8,128)S(1)} %get-tuple-element.18, bf16[32,3,1536]{2,1,0:T(4,128)(2,1)} %reduce_sum.90), kind=kLoop, calls=%fused_computation.24 | loop fusion | flops 884640 | bytes 1180416 | tf_op jit(solution)/shard_map/reduce_sum | solution.py:22
  153.4 0.9 fusion.15
  (57 shorter events, 4.2 us)
Async XLA Ops:
  0.6 115.2 %copy-start = (bf16[384,1536]{1,0:T(8,128)(2,1)S(1)}, bf16[384,1536]{1,0:T(8,128)(2,1)}, u32[]{:S(2)}) copy-start(bf16[384,1536]{1,0:T(8,128)(2,1)} %param.34) | copy-start | bytes 3538948
  0.6 3.7 %copy-start.2 = (bf16[32,3,1536]{2,0,1:T(8,128)(2,1)S(1)}, bf16[32,3,1536]{2,0,1:T(8,128)(2,1)}, u32[]{:S(2)}) copy-start(bf16[32,3,1536]{2,0,1:T(8,128)(2,1)} %param.18) | copy-start | bytes 884740
  3.3 2.8 %copy-start.9 = (f32[1536]{0:T(1024)S(1)}, f32[1536]{0:T(1024)}, u32[]{:S(2)}) copy-start(f32[1536]{0:T(1024)} %param.27) | copy-start | bytes 18436
  3.3 2.8 %copy-start.10 = (f32[1536]{0:T(1024)S(1)}, f32[1536]{0:T(1024)}, u32[]{:S(2)}) copy-start(f32[1536]{0:T(1024)} %param.26) | copy-start | bytes 18436
  74.6 3.6 %copy-start.8 = (f32[1536]{0:T(1024)S(1)}, f32[1536]{0:T(1024)}, u32[]{:S(2)}) copy-start(f32[1536]{0:T(1024)} %param.29) | copy-start | bytes 18436
  80.1 29.5 %all-to-all-start.2 = ((bf16[128,3,1536]{2,1,0:T(4,128)(2,1)}), bf16[128,3,1536]{2,1,0:T(4,128)(2,1)S(1)}, u32[]{:S(2)}, u32[]{:S(2)}) async-start(bf16[128,3,1536]{2,1,0:T(4,128)(2,1)} %bitcast.54), calls=%async_computation.2 | async-start | bytes 3145728 | tf_op jit(solution)/shard_map/all_to_all | solution.py:233
  111.7 2.5 %copy-start.3 = (bf16[1,512,384]{1,2,0:T(8,128)(2,1)S(1)}, bf16[1,512,384]{1,2,0:T(8,128)(2,1)}, u32[]{:S(2)}) copy-start(bf16[1,512,384]{1,2,0:T(8,128)(2,1)} %copy.51) | copy-start | bytes 1179652
  111.7 2.5 %copy-start.11 = (f32[384]{0:T(512)S(1)}, f32[384]{0:T(512)}, u32[]{:S(2)}) copy-start(f32[384]{0:T(512)} %param.31) | copy-start | bytes 4612
  114.3 1.0 copy-start.5
  118.7 29.7 %all-to-all-start.3 = ((bf16[128,3,1536]{2,1,0:T(4,128)(2,1)}), bf16[128,3,1536]{2,1,0:T(4,128)(2,1)S(1)}, u32[]{:S(2)}, u32[]{:S(2)}) async-start(bf16[128,3,1536]{2,1,0:T(4,128)(2,1)} %reshape.127), calls=%async_computation.3 | async-start | bytes 3145728 | tf_op jit(solution)/shard_map/all_to_all | solution.py:249
  150.2 3.1 %copy-start.1 = (bf16[32,3,1536]{2,1,0:T(4,128)(2,1)S(1)}, bf16[32,3,1536]{2,1,0:T(4,128)(2,1)}, u32[]{:S(2)}) copy-start(bf16[32,3,1536]{2,1,0:T(4,128)(2,1)} %reduce_sum.90) | copy-start | bytes 884740
  150.2 3.1 %copy-start.4 = (f32[32,1536]{1,0:T(8,128)S(1)}, f32[32,1536]{1,0:T(8,128)}, u32[]{:S(2)}) copy-start(f32[32,1536]{1,0:T(8,128)} %get-tuple-element.26) | copy-start | bytes 589828
  150.2 3.1 %copy-start.6 = (bf16[1536,64]{0,1:T(8,128)(2,1)S(1)}, bf16[1536,64]{0,1:T(8,128)(2,1)}, u32[]{:S(2)}) copy-start(bf16[1536,64]{0,1:T(8,128)(2,1)} %param.35) | copy-start | bytes 589828
  150.2 3.1 %copy-start.7 = (f32[32,3,64]{2,0,1:T(8,128)S(1)}, f32[32,3,64]{2,0,1:T(8,128)}, u32[]{:S(2)}) copy-start(f32[32,3,64]{2,0,1:T(8,128)} %param.19) | copy-start | bytes 73732
  150.2 3.2 %copy-start.12 = (f32[32]{0:T(128)S(1)}, f32[32]{0:T(128)}, u32[]{:S(2)}) copy-start(f32[32]{0:T(128)} %param.24) | copy-start | bytes 388

commit v7 on v6

--- a/solution.py
+++ b/solution.py
@@ -99,18 +99,54 @@
     )(arrived)
 
 
-def attend_text(queries, keys_own, values_own, length):
-    factor = 1.0 / math.sqrt(queries.shape[-1])
-    live_mask = (jnp.arange(keys_own.shape[0]) < length).astype(jnp.float32)
-    scores = (
-        jnp.einsum("qhd,khd->hqk", queries, keys_own, preferred_element_type=jnp.float32) * factor
-    )
-    weights = jnp.exp(scores) * live_mask
-    totals = jnp.sum(weights, axis=-1)
-    mixture = jnp.einsum(
-        "hqk,khd->qhd", weights.astype(jnp.bfloat16), values_own, preferred_element_type=jnp.float32
-    )
-    return (mixture / jnp.transpose(totals)[:, :, None]).astype(jnp.bfloat16)
+def _cross_kernel(length_ref, x_ref, wq_ref, gain_ref, keys_ref, values_ref, wo_ref, o_ref, mixed_ref):
+    factor = 1.0 / math.sqrt(HEAD_DIM)
+    group_width = wq_ref.shape[1]
+    text = keys_ref.shape[0]
+    projected = jnp.dot(x_ref[...], wq_ref[...], preferred_element_type=jnp.float32)
+    gains = gain_ref[...]
+    live = (lax.broadcasted_iota(jnp.int32, (1, text), 1) < length_ref[0]).astype(jnp.float32)
+    for head in range(group_width // HEAD_DIM):
+        lanes = slice(head * HEAD_DIM, (head + 1) * HEAD_DIM)
+        piece = projected[:, lanes]
+        mean_square = jnp.mean(piece * piece, axis=-1, keepdims=True)
+        queries = (piece * lax.rsqrt(mean_square + EPSILON) * gains[:, lanes]).astype(jnp.bfloat16)
+        scores = (
+            lax.dot_general(
+                queries, keys_ref[:, lanes], (((1,), (1,)), ((), ())),
+                preferred_element_type=jnp.float32,
+            )
+            * factor
+        )
+        weights = jnp.exp(scores) * live
+        totals = jnp.sum(weights, axis=-1, keepdims=True)
+        mixture = jnp.dot(
+            weights.astype(jnp.bfloat16), values_ref[:, lanes], preferred_element_type=jnp.float32
+        )
+        mixed_ref[:, lanes] = (mixture / totals).astype(mixed_ref.dtype)
+    o_ref[...] = jnp.dot(mixed_ref[...], wo_ref[...], preferred_element_type=jnp.float32).astype(
+        o_ref.dtype
+    )
+
+
+def cross_partial(owner_cross, cross_wq, cross_q_gain, keys_own, values_own, length, cross_wo):
+    token_total, model_width = owner_cross.shape
+    group_width = cross_wq.shape[1]
+    text = keys_own.shape[0]
+    vmem = pl.BlockSpec(memory_space=pltpu.VMEM)
+    return pl.pallas_call(
+        _cross_kernel,
+        in_specs=[pl.BlockSpec(memory_space=pltpu.SMEM)] + [vmem] * 6,
+        out_specs=vmem,
+        out_shape=jax.ShapeDtypeStruct((token_total, model_width), jnp.bfloat16),
+        scratch_shapes=[pltpu.VMEM((token_total, group_width), jnp.bfloat16)],
+        cost_estimate=pl.CostEstimate(
+            flops=4 * token_total * model_width * group_width + 4 * token_total * text * group_width,
+            bytes_accessed=4 * model_width * group_width + 4 * text * group_width
+            + 4 * token_total * model_width,
+            transcendentals=token_total * text * (group_width // HEAD_DIM),
+        ),
+    )(length, owner_cross, cross_wq, cross_q_gain.reshape(1, group_width), keys_own, values_own, cross_wo)
 
 
 def _qkv_kernel(x_ref, wq_ref, wk_ref, wv_ref, cos_ref, sin_ref, gain_ref, o_ref):
@@ -232,19 +268,8 @@
     )
     owner_cross = lax.all_to_all(copies, ("head", "tile"), split_axis=0, concat_axis=0, tiled=True)
     owner_cross = owner_cross.reshape(-1, model_width)
-    cross_queries = jnp.dot(owner_cross, cross_wq, preferred_element_type=jnp.float32).reshape(
-        -1, group_heads, HEAD_DIM
-    )
-    cross_queries = head_norm(cross_queries, cross_q_gain.reshape(group_heads, HEAD_DIM)).astype(
-        jnp.bfloat16
-    )
-    own_text_keys = text_keys[0].reshape(-1, group_heads, HEAD_DIM)
-    own_text_values = text_values[0].reshape(-1, group_heads, HEAD_DIM)
-    cross_mixture = attend_text(
-        cross_queries, own_text_keys, own_text_values, text_lengths[0]
-    ).reshape(-1, group_width)
-    partial = jnp.dot(cross_mixture, cross_wo, preferred_element_type=jnp.float32).astype(
-        jnp.bfloat16
+    partial = cross_partial(
+        owner_cross, cross_wq, cross_q_gain, text_keys[0], text_values[0], text_lengths, cross_wo
     )
     returned_partials = lax.all_to_all(
         partial.reshape(head_count * tile_count, per_video, model_width),

time: 155 us -> 153 us (0.987)
  waiting for transfers between devices: 40.6 us -> 48.1 us
  local copies, waits for them, and re-layouts: 23.1 us -> 16 us
  Pallas kernels: 10.9 us -> 16.4 us
  matrix products: 8.92 us -> 4.26 us
  other arithmetic: 11.4 us -> 7.84 us
    unnamed x29 -> x18, local copies, waits for them, and re-layouts: 6.47 us -> 0.05 us
    all_to_all x1, waiting for transfers between devices: 17.9 us -> 23.6 us  [local(): lax.all_to_all(copies, ('head', 'tile'), split_axis=0, concat_axis=0, til...]
    pallas_call x0 -> x1, Pallas kernels: none -> 5.43 us  [cross_partial(): pl.pallas_call(_cross_kernel, in_specs=[pl.BlockSpec(memory_space=pltpu.S...]
    dot_general x4 -> x0, matrix products: 4.67 us -> none  [the longest x1 2.48 us: local(): jnp.dot(owner_cross, cross_wq, preferred_element_type=jnp.float32)]
    all_to_all x1, waiting for transfers between devices: 22.7 us -> 24.5 us  [local(): lax.all_to_all(partial.reshape(head_count * tile_count, per_video, model_...]
    reshape x1, local copies, waits for them, and re-layouts: 3.3 us -> 1.53 us  [local(): own_mixture = attend_self(arrived.reshape(-1, 3 * group_width), group_width)]
    reshape x1, local copies, waits for them, and re-layouts: 2.03 us -> 3.78 us  [local(): partial.reshape(head_count * tile_count, per_video, model_width)]
  transfers between devices with their start and end apart: 2 -> 2, of which waited for: 2 -> 2; matrix products, arithmetic and copies ran while one was open for 5% -> 1% of each run, Pallas kernels for 0% -> 0%
where the time goes in v7:
time: 153 us; the launch traced here: 152 us
  blocking collectives  48.3 us (32%)
  waiting for transfers between devices  48.1 us (31%)
  Pallas kernels  16.4 us (11%)
  local copies, waits for them, and re-layouts  16 us (10%)
  starting transfers between devices  9.56 us (6%)
  other arithmetic  7.84 us (5%)
  matrix products  4.26 us (3%)
  between operations  1.54 us (1%)
    all_to_all x1, blocking collectives, local(): lax.all_to_all(packed.reshape(head_count * videos, per_video, 3 * group_w...  31.9 us
    all_to_all x1, waiting for transfers between devices, local(): lax.all_to_all(partial.reshape(head_count * tile_count, per_video, model_...  24.5 us
    all_to_all x1, waiting for transfers between devices, local(): lax.all_to_all(copies, ('head', 'tile'), split_axis=0, concat_axis=0, til...  23.6 us
    all_to_all x1, blocking collectives, local(): lax.all_to_all(own_mixture.reshape(head_count * tile_count, per_video, gr...  16.4 us
    pallas_call x1, Pallas kernels, pack_projected(): pl.pallas_call(_qkv_kernel, grid=(head_count,), in_specs=[pl.BlockSpec((t...  8.22 us
    pallas_call x1, Pallas kernels, cross_partial(): pl.pallas_call(_cross_kernel, in_specs=[pl.BlockSpec(memory_space=pltpu.S...  5.43 us
    all_to_all x1, starting transfers between devices, local(): lax.all_to_all(partial.reshape(head_count * tile_count, per_video, model_...  4.8 us
    all_to_all x1, starting transfers between devices, local(): lax.all_to_all(copies, ('head', 'tile'), split_axis=0, concat_axis=0, til...  4.76 us
  transfers between devices with their start and end apart: 2, of which 2 were waited for; matrix products, arithmetic and copies ran while one was open for 1% of the time, Pallas kernels for 0%

profile of v7, /device:TPU:1, one launch (start us, length us, event | category | flops | bytes accessed | tf_op | source)
XLA Modules:
  0.0 151.9 jit_solution(6325136214755852864)
XLA Ops:
  0.7 0.8 fusion.24
  2.0 1.2 slice_bitcast_fusion.1
  3.2 1.1 convert_reduce_fusion
  4.6 0.2 fusion.14
  4.8 0.3 copy.35
  5.1 1.0 reshape.103.x_ref
  6.2 0.6 pad_maximum_fusion.3.gain_ref
  6.9 0.3 fusion.30
  7.2 0.7 pad_maximum_fusion.1
  7.9 8.2 %shard_map.185 = bf16[4,96,1152]{2,1,0:T(8,128)(2,1)} custom-call(bf16[96,1536]{1,0:T(8,128)(2,1)} %reshape.103.x_ref, bf16[1536,4608]{1,0:T(8,128)(2,1)} %wv_ref.1, bf16[1536,4608]{1,0:T(8,128)(2,1)} %wv_ref.1, bf16[1536,4608]{1,0:T(8,128)(2,1)} %wv_ref.1, f32[96,128]{1,0:T(8,128)} %get-tuple-element.19.cos_ref, f32[96,128]{1,0:T(8,128)} %get-tuple-element.20.sin_ref, ...), custom_call_target="tpu_custom_call" | custom-call | flops 1358954496 | bytes 15925248 | tf_op jit(solution)/shard_map/pallas_call | solution.py:187
  16.1 2.5 %reshape_reshape.3 = bf16[128,3,1152]{2,1,0:T(4,128)(2,1)S(1)} reshape(bf16[4,96,1152]{2,1,0:T(8,128)(2,1)} %shard_map.185) | data formatting | bytes 1769472 | tf_op jit(solution)/shard_map/reshape;reshape | solution.py:242
  18.6 31.9 %all_to_all.20 = bf16[128,3,1152]{2,1,0:T(4,128)(2,1)S(1)} all-to-all(bf16[128,3,1152]{2,1,0:T(4,128)(2,1)S(1)} %reshape_reshape.3), channel_id=1, replica_groups=mesh['head'=4,'tile'=32] {'head','tile'}, dimensions={0} | all-to-all | bytes 1769472 | tf_op jit(solution)/shard_map/all_to_all | solution.py:241
  50.5 1.5 %reshape.104.x_ref = bf16[384,1152]{1,0:T(8,128)(2,1)} reshape(bf16[128,3,1152]{2,1,0:T(4,128)(2,1)S(1)} %all_to_all.20) | data formatting | bytes 1769472 | tf_op jit(solution)/shard_map/reshape | solution.py:248
  52.0 2.7 %shard_map.186 = bf16[384,384]{1,0:T(8,128)(2,1)} custom-call(bf16[384,1152]{1,0:T(8,128)(2,1)} %reshape.104.x_ref), custom_call_target="tpu_custom_call" | custom-call | flops 226492416 | bytes 1179648 | tf_op jit(solution)/shard_map/pallas_call | solution.py:91
  54.7 1.1 reshape.105
  55.8 16.4 %all_to_all.21 = bf16[128,3,384]{2,1,0:T(4,128)(2,1)S(1)} all-to-all(bf16[128,3,384]{2,1,0:T(4,128)(2,1)S(1)} %reshape.105), channel_id=1, replica_groups=mesh['head'=4,'tile'=32] {'head','tile'}, dimensions={0} | all-to-all | bytes 589824 | tf_op jit(solution)/shard_map/all_to_all | solution.py:249
  72.2 0.3 copy.61
  72.7 3.3 %fusion.33 = (f32[32,3]{0,1:T(4,128)S(1)}, f32[32,3,1536]{2,0,1:T(8,128)S(1)}) fusion(bf16[32,3,1536]{2,0,1:T(8,128)(2,1)S(1)} %dot_general.8, bf16[1536,1536]{1,0:T(8,128)(2,1)} %param.28, f32[32,1536]{1,0:T(8,128)S(1)} %get-tuple-element.6, bf16[32,3,1536]{2,0,1:T(8,128)(2,1)S(1)} %copy-done.1), kind=kOutput, calls=%fused_computation.67 | convolution fusion | flops 453574560 | bytes 6095232 | tf_op jit(solution)/shard_map/dot_general | solution.py:261
  76.4 0.3 copy.40
  76.6 1.6 %broadcast_in_dim.2 = bf16[4,32,3,1536]{3,2,1,0:T(4,128)(2,1)} broadcast(bf16[32,3,1536]{2,1,0:T(4,128)(2,1)S(1)} %copy.40), dimensions={1,2,3} | broadcast | bytes 1474560 | tf_op jit(solution)/shard_map/broadcast_in_dim | solution.py:266
  78.2 4.8 %all-to-all-start.2 = ((bf16[128,3,1536]{2,1,0:T(4,128)(2,1)}), bf16[128,3,1536]{2,1,0:T(4,128)(2,1)S(1)}, u32[]{:S(2)}, u32[]{:S(2)}) async-start(bf16[128,3,1536]{2,1,0:T(4,128)(2,1)} %bitcast.34), calls=%async_computation.2 | async-start | bytes 3145728 | tf_op jit(solution)/shard_map/all_to_all | solution.py:269
  83.0 0.6 reshape.109.gain_ref
  84.2 23.6 %all-to-all-done.2 = bf16[128,3,1536]{2,1,0:T(4,128)(2,1)S(1)} async-done(((bf16[128,3,1536]{2,1,0:T(4,128)(2,1)}), bf16[128,3,1536]{2,1,0:T(4,128)(2,1)S(1)}, u32[]{:S(2)}, u32[]{:S(2)}) %all-to-all-start.2) | async-done | bytes 1179680 | tf_op jit(solution)/shard_map/all_to_all | solution.py:269
  107.8 2.2 %reshape.108.x_ref = bf16[384,1536]{1,0:T(8,128)(2,1)} reshape(bf16[128,3,1536]{2,1,0:T(4,128)(2,1)S(1)} %all-to-all-done.2) | data formatting | bytes 2359296 | tf_op jit(solution)/shard_map/reshape | solution.py:270
  110.0 5.4 %shard_map.187 = bf16[384,1536]{1,0:T(8,128)(2,1)} custom-call(s32[1]{0:T(128)S(6)} %copy.62.length_ref, bf16[384,1536]{1,0:T(8,128)(2,1)} %reshape.108.x_ref, bf16[1536,384]{1,0:T(8,128)(2,1)} %wq_ref.3, f32[1,384]{1,0:T(1,128)} %reshape.109.gain_ref, bf16[512,384]{1,0:T(8,128)(2,1)} %bitcast.37, bf16[512,384]{1,0:T(8,128)(2,1)} %bitcast.38, ...), custom_call_target="tpu_custom_call" | custom-call | flops 1207959552 | bytes 5505024 | tf_op jit(solution)/shard_map/pallas_call | solution.py:137
  115.4 3.8 %reshape.110 = bf16[128,3,1536]{2,1,0:T(4,128)(2,1)} reshape(bf16[384,1536]{1,0:T(8,128)(2,1)} %shard_map.187) | data formatting | bytes 2359296 | tf_op jit(solution)/shard_map/reshape | solution.py:275
  119.2 4.8 %all-to-all-start.3 = ((bf16[128,3,1536]{2,1,0:T(4,128)(2,1)}), bf16[128,3,1536]{2,1,0:T(4,128)(2,1)S(1)}, u32[]{:S(2)}, u32[]{:S(2)}) async-start(bf16[128,3,1536]{2,1,0:T(4,128)(2,1)} %reshape.110), calls=%async_computation.3 | async-start | bytes 3145728 | tf_op jit(solution)/shard_map/all_to_all | solution.py:274
  124.0 0.3 fusion.32
  124.3 24.5 %all-to-all-done.3 = bf16[128,3,1536]{2,1,0:T(4,128)(2,1)S(1)} async-done(((bf16[128,3,1536]{2,1,0:T(4,128)(2,1)}), bf16[128,3,1536]{2,1,0:T(4,128)(2,1)S(1)}, u32[]{:S(2)}, u32[]{:S(2)}) %all-to-all-start.3) | async-done | bytes 1179680 | tf_op jit(solution)/shard_map/all_to_all | solution.py:274
  148.8 1.1 reduce_sum.70
  150.1 0.9 multiply_reduce_fusion
  151.0 0.9 fusion.8
  (42 shorter events, 1.8 us)
Async XLA Ops:
  0.6 150.3 %copy-start = (bf16[1536,64]{0,1:T(8,128)(2,1)S(1)}, bf16[1536,64]{0,1:T(8,128)(2,1)}, u32[]{:S(2)}) copy-start(bf16[1536,64]{0,1:T(8,128)(2,1)} %param.35) | copy-start | bytes 589828
  0.6 3.7 %copy-start.1 = (bf16[32,3,1536]{2,0,1:T(8,128)(2,1)S(1)}, bf16[32,3,1536]{2,0,1:T(8,128)(2,1)}, u32[]{:S(2)}) copy-start(bf16[32,3,1536]{2,0,1:T(8,128)(2,1)} %param.18) | copy-start | bytes 884740
  3.2 2.8 %copy-start.5 = (f32[1536]{0:T(1024)S(1)}, f32[1536]{0:T(1024)}, u32[]{:S(2)}) copy-start(f32[1536]{0:T(1024)} %param.27) | copy-start | bytes 18436
  3.2 2.8 %copy-start.6 = (f32[1536]{0:T(1024)S(1)}, f32[1536]{0:T(1024)}, u32[]{:S(2)}) copy-start(f32[1536]{0:T(1024)} %param.26) | copy-start | bytes 18436
  72.6 3.6 %copy-start.4 = (f32[1536]{0:T(1024)S(1)}, f32[1536]{0:T(1024)}, u32[]{:S(2)}) copy-start(f32[1536]{0:T(1024)} %param.29) | copy-start | bytes 18436
  78.2 4.8 %copy-start.7 = (f32[384]{0:T(512)S(1)}, f32[384]{0:T(512)}, u32[]{:S(2)}) copy-start(f32[384]{0:T(512)} %param.31) | copy-start | bytes 4612
  78.2 29.6 %all-to-all-start.2 = ((bf16[128,3,1536]{2,1,0:T(4,128)(2,1)}), bf16[128,3,1536]{2,1,0:T(4,128)(2,1)S(1)}, u32[]{:S(2)}, u32[]{:S(2)}) async-start(bf16[128,3,1536]{2,1,0:T(4,128)(2,1)} %bitcast.34), calls=%async_computation.2 | async-start | bytes 3145728 | tf_op jit(solution)/shard_map/all_to_all | solution.py:269
  119.2 4.8 %copy-start.2 = (f32[32,2,1536]{2,1,0:T(2,128)S(1)}, f32[32,2,1536]{2,1,0:T(2,128)}, u32[]{:S(2)}) copy-start(f32[32,2,1536]{2,1,0:T(2,128)} %param.23) | copy-start | bytes 1179652
  119.2 29.6 %all-to-all-start.3 = ((bf16[128,3,1536]{2,1,0:T(4,128)(2,1)}), bf16[128,3,1536]{2,1,0:T(4,128)(2,1)S(1)}, u32[]{:S(2)}, u32[]{:S(2)}) async-start(bf16[128,3,1536]{2,1,0:T(4,128)(2,1)} %reshape.110), calls=%async_computation.3 | async-start | bytes 3145728 | tf_op jit(solution)/shard_map/all_to_all | solution.py:274
  149.9 1.1 copy-start.3
  149.9 1.1 copy-start.8

commit v8 on v7

--- a/solution.py
+++ b/solution.py
@@ -99,21 +99,16 @@
     )(arrived)
 
 
-def _cross_kernel(length_ref, x_ref, wq_ref, gain_ref, keys_ref, values_ref, wo_ref, o_ref, mixed_ref):
+def _cross_kernel(length_ref, q_ref, keys_ref, values_ref, wo_ref, o_ref, mixed_ref):
     factor = 1.0 / math.sqrt(HEAD_DIM)
-    group_width = wq_ref.shape[1]
+    group_width = q_ref.shape[1]
     text = keys_ref.shape[0]
-    projected = jnp.dot(x_ref[...], wq_ref[...], preferred_element_type=jnp.float32)
-    gains = gain_ref[...]
     live = (lax.broadcasted_iota(jnp.int32, (1, text), 1) < length_ref[0]).astype(jnp.float32)
     for head in range(group_width // HEAD_DIM):
         lanes = slice(head * HEAD_DIM, (head + 1) * HEAD_DIM)
-        piece = projected[:, lanes]
-        mean_square = jnp.mean(piece * piece, axis=-1, keepdims=True)
-        queries = (piece * lax.rsqrt(mean_square + EPSILON) * gains[:, lanes]).astype(jnp.bfloat16)
         scores = (
             lax.dot_general(
-                queries, keys_ref[:, lanes], (((1,), (1,)), ((), ())),
+                q_ref[:, lanes], keys_ref[:, lanes], (((1,), (1,)), ((), ())),
                 preferred_element_type=jnp.float32,
             )
             * factor
@@ -129,24 +124,33 @@
     )
 
 
-def cross_partial(owner_cross, cross_wq, cross_q_gain, keys_own, values_own, length, cross_wo):
-    token_total, model_width = owner_cross.shape
-    group_width = cross_wq.shape[1]
+def cross_partial(queries, keys_own, values_own, length, cross_wo):
+    token_total, group_width = queries.shape
+    model_width = cross_wo.shape[1]
     text = keys_own.shape[0]
     vmem = pl.BlockSpec(memory_space=pltpu.VMEM)
     return pl.pallas_call(
         _cross_kernel,
-        in_specs=[pl.BlockSpec(memory_space=pltpu.SMEM)] + [vmem] * 6,
+        in_specs=[pl.BlockSpec(memory_space=pltpu.SMEM)] + [vmem] * 4,
         out_specs=vmem,
         out_shape=jax.ShapeDtypeStruct((token_total, model_width), jnp.bfloat16),
         scratch_shapes=[pltpu.VMEM((token_total, group_width), jnp.bfloat16)],
         cost_estimate=pl.CostEstimate(
-            flops=4 * token_total * model_width * group_width + 4 * token_total * text * group_width,
-            bytes_accessed=4 * model_width * group_width + 4 * text * group_width
-            + 4 * token_total * model_width,
+            flops=2 * token_total * model_width * group_width + 4 * token_total * text * group_width,
+            bytes_accessed=2 * model_width * group_width + 4 * text * group_width
+            + 2 * token_total * (model_width + group_width),
             transcendentals=token_total * text * (group_width // HEAD_DIM),
         ),
-    )(length, owner_cross, cross_wq, cross_q_gain.reshape(1, group_width), keys_own, values_own, cross_wo)
+    )(length, queries, keys_own, values_own, cross_wo)
+
+
+def gather_over_head(shard, head_count):
+    pieces = [shard]
+    for shift in range(1, head_count):
+        pieces.append(
+            lax.ppermute(shard, "head", [(i, (i + shift) % head_count) for i in range(head_count)])
+        )
+    return pieces
 
 
 def _qkv_kernel(x_ref, wq_ref, wk_ref, wv_ref, cos_ref, sin_ref, gain_ref, o_ref):
@@ -232,6 +236,8 @@
     videos, per_video, model_width = hidden.shape
     group_heads = HEADS // head_count
     group_width = group_heads * HEAD_DIM
+    weight_pieces = gather_over_head(cross_wq, head_count)
+    gain_pieces = gather_over_head(cross_q_gain, head_count)
     stream = hidden.astype(jnp.float32)
     block_shift = block_modulation[:, 0][:, None, :]
     block_scale = block_modulation[:, 1][:, None, :]
@@ -263,14 +269,23 @@
     )
     after_self = stream + block_gate * self_update
     cross_in = (layer_norm(after_self) * cross_gain).astype(jnp.bfloat16)
-    copies = jnp.broadcast_to(cross_in[None], (head_count,) + cross_in.shape).reshape(
-        head_count * videos, per_video, model_width
-    )
-    owner_cross = lax.all_to_all(copies, ("head", "tile"), split_axis=0, concat_axis=0, tiled=True)
-    owner_cross = owner_cross.reshape(-1, model_width)
-    partial = cross_partial(
-        owner_cross, cross_wq, cross_q_gain, text_keys[0], text_values[0], text_lengths, cross_wo
-    )
+    token_rows = cross_in.reshape(-1, model_width)
+    query_blocks = []
+    for weight_piece, gain_piece in zip(weight_pieces, gain_pieces):
+        block = jnp.dot(token_rows, weight_piece, preferred_element_type=jnp.float32)
+        block = head_norm(block.reshape(-1, group_heads, HEAD_DIM), gain_piece.reshape(group_heads, HEAD_DIM))
+        query_blocks.append(block.astype(jnp.bfloat16).reshape(videos, per_video, group_width))
+    by_shift = jnp.stack([query_blocks[(-g) % head_count] for g in range(head_count)])
+    head_index = lax.axis_index("head")
+    by_group = jnp.roll(by_shift, head_index, axis=0)
+    owner_queries = lax.all_to_all(
+        by_group.reshape(head_count * videos, per_video, group_width),
+        ("head", "tile"),
+        split_axis=0,
+        concat_axis=0,
+        tiled=True,
+    ).reshape(-1, group_width)
+    partial = cross_partial(owner_queries, text_keys[0], text_values[0], text_lengths, cross_wo)
     returned_partials = lax.all_to_all(
         partial.reshape(head_count * tile_count, per_video, model_width),
         ("head", "tile"),

time: 153 us -> 191 us (1.25)
  waiting for transfers between devices: 48.1 us -> 77.4 us
  blocking collectives: 48.3 us -> 31.9 us
  starting transfers between devices: 9.56 us -> 24.3 us
  local copies, waits for them, and re-layouts: 16 us -> 22.6 us
  matrix products: 4.26 us -> 7.89 us
    ppermute x0 -> x6, waiting for transfers between devices: none -> 37.4 us  [gather_over_head(): lax.ppermute(shard, 'head', [(i, (i + shift) % head_count) for i in range...]
    all_to_all x1 -> x0, blocking collectives: 16.4 us -> none  [local(): lax.all_to_all(own_mixture.reshape(head_count * tile_count, per_video, gr...]
    all_to_all x1 -> x2, waiting for transfers between devices: 23.6 us -> 15.5 us  [the longest x1 11.5 us: local(): lax.all_to_all(by_group.reshape(head_count * videos, per_video, group_wid...]
    ppermute x0 -> x6, starting transfers between devices: none -> 7.95 us  [gather_over_head(): lax.ppermute(shard, 'head', [(i, (i + shift) % head_count) for i in range...]
    all_to_all x1 -> x2, starting transfers between devices: 4.76 us -> 11.6 us  [the longest x1 7 us: local(): lax.all_to_all(by_group.reshape(head_count * videos, per_video, group_wid...]
    dot_general x0 -> x3, local copies, waits for them, and re-layouts: none -> 4.69 us  [local(): jnp.dot(token_rows, weight_piece, preferred_element_type=jnp.float32)]
    dot_general x0 -> x4, matrix products: none -> 3.63 us  [local(): jnp.dot(token_rows, weight_piece, preferred_element_type=jnp.float32)]
    unnamed x18 -> x34, local copies, waits for them, and re-layouts: 0.05 us -> 2.84 us
  transfers between devices with their start and end apart: 2 -> 9, of which waited for: 2 -> 5; matrix products, arithmetic and copies ran while one was open for 1% -> 9% of each run, Pallas kernels for 0% -> 0%
where the time goes in v8:
time: 191 us; the launch traced here: 190 us
  waiting for transfers between devices  77.4 us (41%)
  blocking collectives  31.9 us (17%)
  starting transfers between devices  24.3 us (13%)
  local copies, waits for them, and re-layouts  22.6 us (12%)
  Pallas kernels  15.1 us (8%)
  other arithmetic  9.34 us (5%)
  matrix products  7.89 us (4%)
    ppermute x6, waiting for transfers between devices, gather_over_head(): lax.ppermute(shard, 'head', [(i, (i + shift) % head_count) for i in range...  37.4 us
    all_to_all x1, blocking collectives, local(): lax.all_to_all(packed.reshape(head_count * videos, per_video, 3 * group_w...  31.9 us
    all_to_all x1, waiting for transfers between devices, local(): lax.all_to_all(partial.reshape(head_count * tile_count, per_video, model_...  24.5 us
    all_to_all x1, waiting for transfers between devices, local(): lax.all_to_all(by_group.reshape(head_count * videos, per_video, group_wid...  11.5 us
    pallas_call x1, Pallas kernels, pack_projected(): pl.pallas_call(_qkv_kernel, grid=(head_count,), in_specs=[pl.BlockSpec((t...  8.22 us
    ppermute x6, starting transfers between devices, gather_over_head(): lax.ppermute(shard, 'head', [(i, (i + shift) % head_count) for i in range...  7.95 us
    all_to_all x1, starting transfers between devices, local(): lax.all_to_all(by_group.reshape(head_count * videos, per_video, group_wid...  7 us
    all_to_all x1, starting transfers between devices, local(): lax.all_to_all(partial.reshape(head_count * tile_count, per_video, model_...  4.76 us
  transfers between devices with their start and end apart: 9, of which 5 were waited for; matrix products, arithmetic and copies ran while one was open for 9% of the time, Pallas kernels for 0%

profile of v8, /device:TPU:1, one launch (start us, length us, event | category | flops | bytes accessed | tf_op | source)
XLA Modules:
  0.0 190.3 jit_solution(14796292079426507581)
XLA Ops:
  2.0 1.8 slice_bitcast_fusion.1
  4.8 1.0 reshape.146.x_ref
  7.6 8.2 %shard_map.185 = bf16[4,96,1152]{2,1,0:T(8,128)(2,1)} custom-call(bf16[96,1536]{1,0:T(8,128)(2,1)} %reshape.146.x_ref, bf16[1536,4608]{1,0:T(8,128)(2,1)} %wv_ref.1, bf16[1536,4608]{1,0:T(8,128)(2,1)} %wv_ref.1, bf16[1536,4608]{1,0:T(8,128)(2,1)} %wv_ref.1, f32[96,128]{1,0:T(8,128)} %get-tuple-element.27.cos_ref, f32[96,128]{1,0:T(8,128)} %get-tuple-element.28.sin_ref, ...), custom_call_target="tpu_custom_call" | custom-call | flops 1358954496 | bytes 15925248 | tf_op jit(solution)/shard_map/pallas_call | solution.py:191
  15.8 2.5 %reshape_reshape.3 = bf16[128,3,1152]{2,1,0:T(4,128)(2,1)S(1)} reshape(bf16[4,96,1152]{2,1,0:T(8,128)(2,1)} %shard_map.185) | data formatting | bytes 1769472 | tf_op jit(solution)/shard_map/reshape;reshape | solution.py:248
  18.3 31.9 %all_to_all.20 = bf16[128,3,1152]{2,1,0:T(4,128)(2,1)S(1)} all-to-all(bf16[128,3,1152]{2,1,0:T(4,128)(2,1)S(1)} %reshape_reshape.3), channel_id=1, replica_groups=mesh['head'=4,'tile'=32] {'head','tile'}, dimensions={0} | all-to-all | bytes 1769472 | tf_op jit(solution)/shard_map/all_to_all | solution.py:247
  50.2 1.5 reshape.147.x_ref
  51.7 2.7 %shard_map.186 = bf16[384,384]{1,0:T(8,128)(2,1)} custom-call(bf16[384,1152]{1,0:T(8,128)(2,1)} %reshape.147.x_ref), custom_call_target="tpu_custom_call" | custom-call | flops 226492416 | bytes 1179648 | tf_op jit(solution)/shard_map/pallas_call | solution.py:91
  54.5 1.8 reshape.148
  56.3 4.6 %all-to-all-start.1 = ((bf16[128,3,384]{2,1,0:T(4,128)(2,1)}), bf16[128,3,384]{2,1,0:T(4,128)(2,1)S(1)}, u32[]{:S(2)}, u32[]{:S(2)}) async-start(bf16[128,3,384]{2,1,0:T(4,128)(2,1)} %reshape.148), calls=%async_computation.1 | async-start | bytes 786432 | tf_op jit(solution)/shard_map/all_to_all | solution.py:255
  60.9 1.5 collective-permute-start.4
  62.4 2.5 %collective-permute-start.2 = (bf16[1536,384]{1,0:T(8,128)(2,1)}, bf16[1536,384]{1,0:T(8,128)(2,1)}, u32[]{:S(2)}, u32[]{:S(2)}) collective-permute-start(bf16[1536,384]{1,0:T(8,128)(2,1)} %param.30), channel_id=1, source_target_pairs={{0,64},{32,96},{64,0},{96,32},{1,65},{33,97},{65,1},{97,33},{2,66}... | collective-permute-start | bytes 3538952 | tf_op jit(solution)/shard_map/ppermute | solution.py:151
  64.9 2.3 %collective-permute-start.3 = (f32[384]{0:T(512)S(1)}, f32[384]{0:T(512)S(1)}, u32[]{:S(2)}, u32[]{:S(2)}) collective-permute-start(f32[384]{0:T(512)S(1)} %copy-done.11), channel_id=1, source_target_pairs={{0,64},{32,96},{64,0},{96,32},{1,65},{33,97},{65,1},{97,33},{2,66}... | collective-permute-start | bytes 4616 | tf_op jit(solution)/shard_map/ppermute | solution.py:151
  67.6 1.6 copy.52
  69.2 4.0 %all-to-all-done.1 = bf16[128,3,384]{2,1,0:T(4,128)(2,1)S(1)} async-done(((bf16[128,3,384]{2,1,0:T(4,128)(2,1)}), bf16[128,3,384]{2,1,0:T(4,128)(2,1)S(1)}, u32[]{:S(2)}, u32[]{:S(2)}) %all-to-all-start.1) | async-done | bytes 294944 | tf_op jit(solution)/shard_map/all_to_all | solution.py:255
  73.6 3.3 %fusion.33 = (f32[32,3]{0,1:T(4,128)S(1)}, f32[32,3,1536]{2,0,1:T(8,128)S(1)}) fusion(bf16[32,3,1536]{2,0,1:T(8,128)(2,1)S(1)} %dot_general.36, bf16[1536,1536]{1,0:T(8,128)(2,1)} %param.28, f32[32,1536]{1,0:T(8,128)S(1)} %copy-done.2, bf16[32,3,1536]{2,0,1:T(8,128)(2,1)S(1)} %copy-done.1), kind=kOutput, calls=%fused_computation.88 | convolution fusion | flops 453574560 | bytes 6095232 | tf_op jit(solution)/shard_map/dot_general | solution.py:267
  79.4 13.9 %collective-permute-done.4 = bf16[1536,384]{1,0:T(8,128)(2,1)} collective-permute-done((bf16[1536,384]{1,0:T(8,128)(2,1)}, bf16[1536,384]{1,0:T(8,128)(2,1)}, u32[]{:S(2)}, u32[]{:S(2)}) %collective-permute-start.4) | collective-permute-done | bytes 1179680 | tf_op jit(solution)/shard_map/ppermute | solution.py:151
  93.4 1.2 collective-permute-start.1
  94.6 1.6 copy.58
  96.2 23.4 %collective-permute-done.2 = bf16[1536,384]{1,0:T(8,128)(2,1)} collective-permute-done((bf16[1536,384]{1,0:T(8,128)(2,1)}, bf16[1536,384]{1,0:T(8,128)(2,1)}, u32[]{:S(2)}, u32[]{:S(2)}) %collective-permute-start.2) | collective-permute-done | bytes 1179680 | tf_op jit(solution)/shard_map/ppermute | solution.py:151
  119.6 1.6 copy.56
  121.2 1.2 multiply_reduce_fusion.2
  122.4 1.2 multiply_reduce_fusion.3
  123.5 1.6 copy.54
  129.4 7.0 %all-to-all-start.2 = ((bf16[128,3,384]{2,1,0:T(4,128)(2,1)}), bf16[128,3,384]{2,1,0:T(4,128)(2,1)S(1)}, u32[]{:S(2)}, u32[]{:S(2)}) async-start(bf16[128,3,384]{2,1,0:T(4,128)(2,1)} %bitcast.18), calls=%async_computation.2 | async-start | bytes 786432 | tf_op jit(solution)/shard_map/all_to_all | solution.py:281
  137.1 11.5 %all-to-all-done.2 = bf16[128,3,384]{2,1,0:T(4,128)(2,1)S(1)} async-done(((bf16[128,3,384]{2,1,0:T(4,128)(2,1)}), bf16[128,3,384]{2,1,0:T(4,128)(2,1)S(1)}, u32[]{:S(2)}, u32[]{:S(2)}) %all-to-all-start.2) | async-done | bytes 294944 | tf_op jit(solution)/shard_map/all_to_all | solution.py:281
  148.6 1.0 reshape.152.q_ref
  149.6 4.2 %shard_map.187 = bf16[384,1536]{1,0:T(8,128)(2,1)} custom-call(s32[1]{0:T(128)S(6)} %copy.88.length_ref, bf16[384,384]{1,0:T(8,128)(2,1)} %reshape.152.q_ref, bf16[512,384]{1,0:T(8,128)(2,1)} %bitcast.61, bf16[512,384]{1,0:T(8,128)(2,1)} %bitcast.62, bf16[384,1536]{1,0:T(8,128)(2,1)} %wo_ref.1), custom_call_target="tpu_custom_call" | custom-call | flops 754974720 | bytes 3440640 | tf_op jit(solution)/shard_map/pallas_call | solution.py:132
  153.8 3.8 %reshape.153 = bf16[128,3,1536]{2,1,0:T(4,128)(2,1)} reshape(bf16[384,1536]{1,0:T(8,128)(2,1)} %shard_map.187) | data formatting | bytes 2359296 | tf_op jit(solution)/shard_map/reshape | solution.py:290
  157.5 4.8 %all-to-all-start.3 = ((bf16[128,3,1536]{2,1,0:T(4,128)(2,1)}), bf16[128,3,1536]{2,1,0:T(4,128)(2,1)S(1)}, u32[]{:S(2)}, u32[]{:S(2)}) async-start(bf16[128,3,1536]{2,1,0:T(4,128)(2,1)} %reshape.153), calls=%async_computation.3 | async-start | bytes 3145728 | tf_op jit(solution)/shard_map/all_to_all | solution.py:289
  162.7 24.5 %all-to-all-done.3 = bf16[128,3,1536]{2,1,0:T(4,128)(2,1)S(1)} async-done(((bf16[128,3,1536]{2,1,0:T(4,128)(2,1)}), bf16[128,3,1536]{2,1,0:T(4,128)(2,1)S(1)}, u32[]{:S(2)}, u32[]{:S(2)}) %all-to-all-start.3) | async-done | bytes 1179680 | tf_op jit(solution)/shard_map/all_to_all | solution.py:289
  187.1 1.1 reduce_sum.110
  189.3 0.9 fusion.8
  (95 shorter events, 12.8 us)
Async XLA Ops:
  0.6 188.7 %copy-start = (bf16[1536,64]{0,1:T(8,128)(2,1)S(1)}, bf16[1536,64]{0,1:T(8,128)(2,1)}, u32[]{:S(2)}) copy-start(bf16[1536,64]{0,1:T(8,128)(2,1)} %param.35) | copy-start | bytes 589828
  0.6 3.2 %copy-start.1 = (bf16[32,3,1536]{2,0,1:T(8,128)(2,1)S(1)}, bf16[32,3,1536]{2,0,1:T(8,128)(2,1)}, u32[]{:S(2)}) copy-start(bf16[32,3,1536]{2,0,1:T(8,128)(2,1)} %param.18) | copy-start | bytes 884740
  4.3 1.5 copy-start.9
  4.3 1.5 copy-start.10
  51.7 13.2 %copy-start.11 = (f32[384]{0:T(512)S(1)}, f32[384]{0:T(512)}, u32[]{:S(2)}) copy-start(f32[384]{0:T(512)} %param.31) | copy-start | bytes 4612
  56.3 16.9 %all-to-all-start.1 = ((bf16[128,3,384]{2,1,0:T(4,128)(2,1)}), bf16[128,3,384]{2,1,0:T(4,128)(2,1)S(1)}, u32[]{:S(2)}, u32[]{:S(2)}) async-start(bf16[128,3,384]{2,1,0:T(4,128)(2,1)} %reshape.148), calls=%async_computation.1 | async-start | bytes 786432 | tf_op jit(solution)/shard_map/all_to_all | solution.py:255
  60.9 32.5 %collective-permute-start.4 = (bf16[1536,384]{1,0:T(8,128)(2,1)}, bf16[1536,384]{1,0:T(8,128)(2,1)}, u32[]{:S(2)}, u32[]{:S(2)}) collective-permute-start(bf16[1536,384]{1,0:T(8,128)(2,1)} %param.30), channel_id=1, source_target_pairs={{0,32},{32,64},{64,96},{96,0},{1,33},{33,65},{65,97},{97,1},{2,34}... | collective-permute-start | bytes 3538952 | tf_op jit(solution)/shard_map/ppermute | solution.py:151
  62.4 57.2 %collective-permute-start.2 = (bf16[1536,384]{1,0:T(8,128)(2,1)}, bf16[1536,384]{1,0:T(8,128)(2,1)}, u32[]{:S(2)}, u32[]{:S(2)}) collective-permute-start(bf16[1536,384]{1,0:T(8,128)(2,1)} %param.30), channel_id=1, source_target_pairs={{0,64},{32,96},{64,0},{96,32},{1,65},{33,97},{65,1},{97,33},{2,66}... | collective-permute-start | bytes 3538952 | tf_op jit(solution)/shard_map/ppermute | solution.py:151
  64.9 60.9 %collective-permute-start.5 = (f32[384]{0:T(512)S(1)}, f32[384]{0:T(512)}, u32[]{:S(2)}, u32[]{:S(2)}) collective-permute-start(f32[384]{0:T(512)S(1)} %copy-done.11), channel_id=1, source_target_pairs={{0,32},{32,64},{64,96},{96,0},{1,33},{33,65},{65,97},{97,1},{2,34}... | collective-permute-start | bytes 4616 | tf_op jit(solution)/shard_map/ppermute | solution.py:151
  64.9 61.9 %collective-permute-start.3 = (f32[384]{0:T(512)S(1)}, f32[384]{0:T(512)S(1)}, u32[]{:S(2)}, u32[]{:S(2)}) collective-permute-start(f32[384]{0:T(512)S(1)} %copy-done.11), channel_id=1, source_target_pairs={{0,64},{32,96},{64,0},{96,32},{1,65},{33,97},{65,1},{97,33},{2,66}... | collective-permute-start | bytes 4616 | tf_op jit(solution)/shard_map/ppermute | solution.py:151
  67.2 56.3 %collective-permute-start = (bf16[1536,384]{1,0:T(8,128)(2,1)}, bf16[1536,384]{1,0:T(8,128)(2,1)}, u32[]{:S(2)}, u32[]{:S(2)}) collective-permute-start(bf16[1536,384]{1,0:T(8,128)(2,1)} %param.30), channel_id=1, source_target_pairs={{0,96},{32,0},{64,32},{96,64},{1,97},{33,1},{65,33},{97,65},{2,98}... | collective-permute-start | bytes 3538952 | tf_op jit(solution)/shard_map/ppermute | solution.py:151
  69.2 4.4 %copy-start.2 = (f32[32,1536]{1,0:T(8,128)S(1)}, f32[32,1536]{1,0:T(8,128)}, u32[]{:S(2)}) copy-start(f32[32,1536]{1,0:T(8,128)} %get-tuple-element.6) | copy-start | bytes 589828
  73.6 3.6 %copy-start.8 = (f32[1536]{0:T(1024)S(1)}, f32[1536]{0:T(1024)}, u32[]{:S(2)}) copy-start(f32[1536]{0:T(1024)} %param.29) | copy-start | bytes 18436
  93.4 33.9 %collective-permute-start.1 = (f32[384]{0:T(512)S(1)}, f32[384]{0:T(512)}, u32[]{:S(2)}, u32[]{:S(2)}) collective-permute-start(f32[384]{0:T(512)S(1)} %copy-done.11), channel_id=1, source_target_pairs={{0,96},{32,0},{64,32},{96,64},{1,97},{33,1},{65,33},{97,65},{2,98}... | collective-permute-start | bytes 4616 | tf_op jit(solution)/shard_map/ppermute | solution.py:151
  125.1 0.9 copy-start.4
  125.1 1.7 copy-start.3
  125.8 2.4 %copy-start.6 = (bf16[8,32,3,384]{3,2,1,0:T(4,128)(2,1)S(1)}, bf16[8,32,3,384]{3,2,1,0:T(4,128)(2,1)}, u32[]{:S(2)}) copy-start(bf16[8,32,3,384]{3,2,1,0:T(4,128)(2,1)} %constant_dynamic-update-slice_fusion.7) | copy-start | bytes 1769476
  129.4 19.2 %all-to-all-start.2 = ((bf16[128,3,384]{2,1,0:T(4,128)(2,1)}), bf16[128,3,384]{2,1,0:T(4,128)(2,1)S(1)}, u32[]{:S(2)}, u32[]{:S(2)}) async-start(bf16[128,3,384]{2,1,0:T(4,128)(2,1)} %bitcast.18), calls=%async_computation.2 | async-start | bytes 786432 | tf_op jit(solution)/shard_map/all_to_all | solution.py:281
  157.5 4.8 %copy-start.5 = (f32[32,2,1536]{2,1,0:T(2,128)S(1)}, f32[32,2,1536]{2,1,0:T(2,128)}, u32[]{:S(2)}) copy-start(f32[32,2,1536]{2,1,0:T(2,128)} %param.23) | copy-start | bytes 1179652
  157.5 29.6 %all-to-all-start.3 = ((bf16[128,3,1536]{2,1,0:T(4,128)(2,1)}), bf16[128,3,1536]{2,1,0:T(4,128)(2,1)S(1)}, u32[]{:S(2)}, u32[]{:S(2)}) async-start(bf16[128,3,1536]{2,1,0:T(4,128)(2,1)} %reshape.153), calls=%async_computation.3 | async-start | bytes 3145728 | tf_op jit(solution)/shard_map/all_to_all | solution.py:289
  188.2 1.1 copy-start.7
  188.2 1.1 copy-start.12

commit v9 on v7

--- a/solution.py
+++ b/solution.py
@@ -149,8 +149,23 @@
     )(length, owner_cross, cross_wq, cross_q_gain.reshape(1, group_width), keys_own, values_own, cross_wo)
 
 
-def _qkv_kernel(x_ref, wq_ref, wk_ref, wv_ref, cos_ref, sin_ref, gain_ref, o_ref):
-    block_in = x_ref[...]
+def _qkv_kernel(
+    hidden_ref, modulation_ref, wq_ref, wk_ref, wv_ref, cos_ref, sin_ref, gain_ref, o_ref, normed_ref
+):
+    group = pl.program_id(0)
+    videos, per_video, _ = hidden_ref.shape
+
+    @pl.when(group == 0)
+    def _():
+        shift = modulation_ref[:, 0, :]
+        scale = 1.0 + modulation_ref[:, 1, :]
+        for slot in range(per_video):
+            stream = hidden_ref[:, slot, :].astype(jnp.float32)
+            normed_ref[slot * videos : (slot + 1) * videos, :] = (
+                layer_norm(stream) * scale + shift
+            ).astype(normed_ref.dtype)
+
+    block_in = normed_ref[...]
     cosine = cos_ref[...]
     sine_signed = sin_ref[...]
     group_width = wq_ref.shape[1]
@@ -172,39 +187,42 @@
         )
 
 
-def pack_projected(block_in, cell_map, w_qkv, self_q_gain, self_k_gain, head_count):
-    videos, per_video, model_width = block_in.shape
-    rows = block_in.reshape(-1, model_width)
-    token_total = rows.shape[0]
+def pack_projected(hidden, block_modulation, cell_map, w_qkv, self_q_gain, self_k_gain, head_count):
+    videos, per_video, model_width = hidden.shape
+    token_total = videos * per_video
     group_width = model_width // head_count
-    angles = rope_angles(cell_map).reshape(token_total, HEAD_DIM // 2)
+    angles = rope_angles(jnp.transpose(cell_map, (1, 0))).reshape(token_total, HEAD_DIM // 2)
     cosine = jnp.cos(angles)
     sine = jnp.sin(angles)
     cos_full = jnp.concatenate([cosine, cosine], axis=-1)
     sin_signed = jnp.concatenate([-sine, sine], axis=-1)
     gains = jnp.stack([self_q_gain, self_k_gain])
-    whole = lambda g: (0, 0)
+    whole2 = lambda g: (0, 0)
+    whole3 = lambda g: (0, 0, 0)
     packed = pl.pallas_call(
         _qkv_kernel,
         grid=(head_count,),
         in_specs=[
-            pl.BlockSpec((token_total, model_width), whole),
+            pl.BlockSpec(hidden.shape, whole3),
+            pl.BlockSpec(block_modulation.shape, whole3),
             pl.BlockSpec((model_width, group_width), lambda g: (0, g)),
             pl.BlockSpec((model_width, group_width), lambda g: (0, head_count + g)),
             pl.BlockSpec((model_width, group_width), lambda g: (0, 2 * head_count + g)),
-            pl.BlockSpec((token_total, HEAD_DIM), whole),
-            pl.BlockSpec((token_total, HEAD_DIM), whole),
+            pl.BlockSpec((token_total, HEAD_DIM), whole2),
+            pl.BlockSpec((token_total, HEAD_DIM), whole2),
             pl.BlockSpec((2, group_width), lambda g: (0, g)),
         ],
         out_specs=pl.BlockSpec((1, token_total, 3 * group_width), lambda g: (g, 0, 0)),
         out_shape=jax.ShapeDtypeStruct((head_count, token_total, 3 * group_width), jnp.bfloat16),
+        scratch_shapes=[pltpu.VMEM((token_total, model_width), jnp.bfloat16)],
         cost_estimate=pl.CostEstimate(
             flops=2 * token_total * model_width * 3 * model_width,
             bytes_accessed=2 * model_width * 3 * model_width + 4 * token_total * 3 * model_width,
             transcendentals=0,
         ),
-    )(rows, w_qkv, w_qkv, w_qkv, cos_full, sin_signed, gains)
-    return packed.reshape(head_count, videos, per_video, 3 * group_width)
+    )(hidden, block_modulation, w_qkv, w_qkv, w_qkv, cos_full, sin_signed, gains)
+    packed = packed.reshape(head_count, per_video, videos, 3 * group_width)
+    return jnp.transpose(packed, (0, 2, 1, 3))
 
 
 def local(
@@ -233,11 +251,10 @@
     group_heads = HEADS // head_count
     group_width = group_heads * HEAD_DIM
     stream = hidden.astype(jnp.float32)
-    block_shift = block_modulation[:, 0][:, None, :]
-    block_scale = block_modulation[:, 1][:, None, :]
     block_gate = block_modulation[:, 2][:, None, :]
-    block_in = (layer_norm(stream) * (1.0 + block_scale) + block_shift).astype(jnp.bfloat16)
-    packed = pack_projected(block_in, cell_map, w_qkv, self_q_gain, self_k_gain, head_count)
+    packed = pack_projected(
+        hidden, block_modulation, cell_map, w_qkv, self_q_gain, self_k_gain, head_count
+    )
     arrived = lax.all_to_all(
         packed.reshape(head_count * videos, per_video, 3 * group_width),
         ("head", "tile"),

time: 153 us -> 153 us (level)
  blocking collectives: 48.3 us -> 31.9 us
  waiting for transfers between devices: 48.1 us -> 59.4 us
  starting transfers between devices: 9.56 us -> 14.1 us
  local copies, waits for them, and re-layouts: 16 us -> 18.8 us
  other arithmetic: 7.84 us -> 5.1 us
    all_to_all x1 -> x0, blocking collectives: 16.4 us -> none  [local(): lax.all_to_all(own_mixture.reshape(head_count * tile_count, per_video, gr...]
    all_to_all x0 -> x1, waiting for transfers between devices: none -> 11.4 us  [local(): lax.all_to_all(own_mixture.reshape(head_count * tile_count, per_video, gr...]
    all_to_all x0 -> x1, starting transfers between devices: none -> 4.59 us  [local(): lax.all_to_all(own_mixture.reshape(head_count * tile_count, per_video, gr...]
    unnamed x18 -> x20, local copies, waits for them, and re-layouts: 0.05 us -> 3.46 us
    another operation x1 -> x0, local copies, waits for them, and re-layouts: 2.52 us -> none  [local(): packed.reshape(head_count * videos, per_video, 3 * group_width)]
    transpose x0 -> x1, local copies, waits for them, and re-layouts: none -> 1.77 us  [pack_projected(): return jnp.transpose(packed, (0, 2, 1, 3))]
  transfers between devices with their start and end apart: 2 -> 3, of which waited for: 2 -> 3; matrix products, arithmetic and copies ran while one was open for 1% -> 1% of each run, Pallas kernels for 0% -> 0%
where the time goes in v9:
time: 153 us; the launch traced here: 152 us
  waiting for transfers between devices  59.4 us (39%)
  blocking collectives  31.9 us (21%)
  local copies, waits for them, and re-layouts  18.8 us (12%)
  Pallas kernels  17.3 us (11%)
  starting transfers between devices  14.1 us (9%)
  other arithmetic  5.1 us (3%)
  matrix products  4.26 us (3%)
    all_to_all x1, blocking collectives, local(): lax.all_to_all(packed.reshape(head_count * videos, per_video, 3 * group_w...  31.9 us
    all_to_all x1, waiting for transfers between devices, local(): lax.all_to_all(partial.reshape(head_count * tile_count, per_video, model_...  24.5 us
    all_to_all x1, waiting for transfers between devices, local(): lax.all_to_all(copies, ('head', 'tile'), split_axis=0, concat_axis=0, til...  23.6 us
    all_to_all x1, waiting for transfers between devices, local(): lax.all_to_all(own_mixture.reshape(head_count * tile_count, per_video, gr...  11.4 us
    pallas_call x1, Pallas kernels, pack_projected(): pl.pallas_call(_qkv_kernel, grid=(head_count,), in_specs=[pl.BlockSpec(hi...  9.07 us
    pallas_call x1, Pallas kernels, cross_partial(): pl.pallas_call(_cross_kernel, in_specs=[pl.BlockSpec(memory_space=pltpu.S...  5.47 us
    all_to_all x1, starting transfers between devices, local(): lax.all_to_all(partial.reshape(head_count * tile_count, per_video, model_...  4.8 us
    all_to_all x1, starting transfers between devices, local(): lax.all_to_all(copies, ('head', 'tile'), split_axis=0, concat_axis=0, til...  4.75 us
  transfers between devices with their start and end apart: 3, of which 3 were waited for; matrix products, arithmetic and copies ran while one was open for 1% of the time, Pallas kernels for 0%

profile of v9, /device:TPU:1, one launch (start us, length us, event | category | flops | bytes accessed | tf_op | source)
XLA Modules:
  0.0 152.4 jit_solution(1007589830625144245)
XLA Ops:
  0.7 0.8 fusion.20
  1.7 2.4 %copy.33.modulation_ref = f32[32,3,1536]{2,1,0:T(4,128)} copy(f32[32,3,1536]{2,0,1:T(8,128)} %param.22) | data formatting | bytes 1179648 | tf_op args[4]
  4.1 1.0 copy.32.hidden_ref
  5.2 0.6 pad_maximum_fusion.3.gain_ref
  5.9 0.3 fusion.26
  6.2 0.7 pad_maximum_fusion.1
  7.0 9.1 %shard_map.185 = bf16[4,96,1152]{2,1,0:T(8,128)(2,1)} custom-call(bf16[32,3,1536]{2,1,0:T(4,128)(2,1)} %copy.32.hidden_ref, f32[32,3,1536]{2,1,0:T(4,128)} %copy.33.modulation_ref, bf16[1536,4608]{1,0:T(8,128)(2,1)} %wv_ref.1, bf16[1536,4608]{1,0:T(8,128)(2,1)} %wv_ref.1, bf16[1536,4608]{1,0:T(8,128)(2,1)} %wv_ref.1, f32[96,128]{1,0:T(8,128)} %get-tuple-element.16.cos_ref, ...), custom_call_target="tpu_custom_call" | custom-call | flops 1358954496 | bytes 15925248 | tf_op jit(solution)/shard_map/pallas_call | solution.py:202
  16.0 1.8 %copy.34 = bf16[4,32,3,1152]{3,2,1,0:T(4,128)(2,1)S(1)} copy(bf16[4,32,3,1152]{3,1,2,0:T(8,128)(2,1)} %bitcast.68) | data formatting | bytes 1769472 | tf_op jit(solution)/shard_map/transpose | solution.py:225
  17.8 31.9 %all_to_all.20 = bf16[128,3,1152]{2,1,0:T(4,128)(2,1)S(1)} all-to-all(bf16[128,3,1152]{2,1,0:T(4,128)(2,1)S(1)} %bitcast.67), channel_id=1, replica_groups=mesh['head'=4,'tile'=32] {'head','tile'}, dimensions={0} | all-to-all | bytes 1769472 | tf_op jit(solution)/shard_map/all_to_all | solution.py:258
  49.7 1.5 %reshape.96.x_ref = bf16[384,1152]{1,0:T(8,128)(2,1)} reshape(bf16[128,3,1152]{2,1,0:T(4,128)(2,1)S(1)} %all_to_all.20) | data formatting | bytes 1769472 | tf_op jit(solution)/shard_map/reshape | solution.py:265
  51.2 2.7 %shard_map.186 = bf16[384,384]{1,0:T(8,128)(2,1)} custom-call(bf16[384,1152]{1,0:T(8,128)(2,1)} %reshape.96.x_ref), custom_call_target="tpu_custom_call" | custom-call | flops 226492416 | bytes 1179648 | tf_op jit(solution)/shard_map/pallas_call | solution.py:91
  53.9 1.8 %reshape.97 = bf16[128,3,384]{2,1,0:T(4,128)(2,1)} reshape(bf16[384,384]{1,0:T(8,128)(2,1)} %shard_map.186) | data formatting | bytes 589824 | tf_op jit(solution)/shard_map/reshape | solution.py:267
  55.8 4.6 %all-to-all-start.1 = ((bf16[128,3,384]{2,1,0:T(4,128)(2,1)}), bf16[128,3,384]{2,1,0:T(4,128)(2,1)S(1)}, u32[]{:S(2)}, u32[]{:S(2)}) async-start(bf16[128,3,384]{2,1,0:T(4,128)(2,1)} %reshape.97), calls=%async_computation.1 | async-start | bytes 786432 | tf_op jit(solution)/shard_map/all_to_all | solution.py:266
  60.4 0.9 slice_bitcast_fusion
  61.3 11.4 %all-to-all-done.1 = bf16[128,3,384]{2,1,0:T(4,128)(2,1)S(1)} async-done(((bf16[128,3,384]{2,1,0:T(4,128)(2,1)}), bf16[128,3,384]{2,1,0:T(4,128)(2,1)S(1)}, u32[]{:S(2)}, u32[]{:S(2)}) %all-to-all-start.1) | async-done | bytes 294944 | tf_op jit(solution)/shard_map/all_to_all | solution.py:266
  72.7 0.3 copy.57
  73.1 3.3 %fusion.29 = (f32[32,3]{0,1:T(4,128)S(1)}, f32[32,3,1536]{2,0,1:T(8,128)S(1)}) fusion(bf16[32,3,1536]{2,0,1:T(8,128)(2,1)S(1)} %dot_general.8, bf16[1536,1536]{1,0:T(8,128)(2,1)} %param.28, f32[32,1536]{1,0:T(8,128)S(1)} %slice_bitcast_fusion, bf16[32,3,1536]{2,0,1:T(8,128)(2,1)S(1)} %copy-done.1), kind=kOutput, calls=%fused_computation.58 | convolution fusion | flops 453574560 | bytes 6095232 | tf_op jit(solution)/shard_map/dot_general | solution.py:278
  76.4 0.2 multiply_reduce_fusion.1
  76.8 0.3 copy.36
  77.1 1.6 %broadcast_in_dim.2 = bf16[4,32,3,1536]{3,2,1,0:T(4,128)(2,1)} broadcast(bf16[32,3,1536]{2,1,0:T(4,128)(2,1)S(1)} %copy.36), dimensions={1,2,3} | broadcast | bytes 1474560 | tf_op jit(solution)/shard_map/broadcast_in_dim | solution.py:283
  78.6 4.8 %all-to-all-start.2 = ((bf16[128,3,1536]{2,1,0:T(4,128)(2,1)}), bf16[128,3,1536]{2,1,0:T(4,128)(2,1)S(1)}, u32[]{:S(2)}, u32[]{:S(2)}) async-start(bf16[128,3,1536]{2,1,0:T(4,128)(2,1)} %bitcast.66), calls=%async_computation.2 | async-start | bytes 3145728 | tf_op jit(solution)/shard_map/all_to_all | solution.py:286
  83.4 0.6 reshape.101.gain_ref
  84.6 23.6 %all-to-all-done.2 = bf16[128,3,1536]{2,1,0:T(4,128)(2,1)S(1)} async-done(((bf16[128,3,1536]{2,1,0:T(4,128)(2,1)}), bf16[128,3,1536]{2,1,0:T(4,128)(2,1)S(1)}, u32[]{:S(2)}, u32[]{:S(2)}) %all-to-all-start.2) | async-done | bytes 1179680 | tf_op jit(solution)/shard_map/all_to_all | solution.py:286
  108.2 2.2 %reshape.100.x_ref = bf16[384,1536]{1,0:T(8,128)(2,1)} reshape(bf16[128,3,1536]{2,1,0:T(4,128)(2,1)S(1)} %all-to-all-done.2) | data formatting | bytes 2359296 | tf_op jit(solution)/shard_map/reshape | solution.py:287
  110.4 5.5 %shard_map.187 = bf16[384,1536]{1,0:T(8,128)(2,1)} custom-call(s32[1]{0:T(128)S(6)} %copy.58.length_ref, bf16[384,1536]{1,0:T(8,128)(2,1)} %reshape.100.x_ref, bf16[1536,384]{1,0:T(8,128)(2,1)} %wq_ref.3, f32[1,384]{1,0:T(1,128)} %reshape.101.gain_ref, bf16[512,384]{1,0:T(8,128)(2,1)} %bitcast.71, bf16[512,384]{1,0:T(8,128)(2,1)} %bitcast.72, ...), custom_call_target="tpu_custom_call" | custom-call | flops 1207959552 | bytes 5505024 | tf_op jit(solution)/shard_map/pallas_call | solution.py:137
  115.9 3.8 %reshape.102 = bf16[128,3,1536]{2,1,0:T(4,128)(2,1)} reshape(bf16[384,1536]{1,0:T(8,128)(2,1)} %shard_map.187) | data formatting | bytes 2359296 | tf_op jit(solution)/shard_map/reshape | solution.py:292
  119.7 4.8 %all-to-all-start.3 = ((bf16[128,3,1536]{2,1,0:T(4,128)(2,1)}), bf16[128,3,1536]{2,1,0:T(4,128)(2,1)S(1)}, u32[]{:S(2)}, u32[]{:S(2)}) async-start(bf16[128,3,1536]{2,1,0:T(4,128)(2,1)} %reshape.102), calls=%async_computation.3 | async-start | bytes 3145728 | tf_op jit(solution)/shard_map/all_to_all | solution.py:291
  124.5 0.3 fusion.28
  124.8 24.5 %all-to-all-done.3 = bf16[128,3,1536]{2,1,0:T(4,128)(2,1)S(1)} async-done(((bf16[128,3,1536]{2,1,0:T(4,128)(2,1)}), bf16[128,3,1536]{2,1,0:T(4,128)(2,1)S(1)}, u32[]{:S(2)}, u32[]{:S(2)}) %all-to-all-start.3) | async-done | bytes 1179680 | tf_op jit(solution)/shard_map/all_to_all | solution.py:291
  149.3 1.1 reduce_sum.50
  150.6 0.9 multiply_reduce_fusion
  151.5 0.9 fusion.8
  (35 shorter events, 1.0 us)
Async XLA Ops:
  0.6 150.8 %copy-start = (bf16[1536,64]{0,1:T(8,128)(2,1)S(1)}, bf16[1536,64]{0,1:T(8,128)(2,1)}, u32[]{:S(2)}) copy-start(bf16[1536,64]{0,1:T(8,128)(2,1)} %param.35) | copy-start | bytes 589828
  0.6 3.5 %copy-start.1 = (bf16[32,3,1536]{2,0,1:T(8,128)(2,1)S(1)}, bf16[32,3,1536]{2,0,1:T(8,128)(2,1)}, u32[]{:S(2)}) copy-start(bf16[32,3,1536]{2,0,1:T(8,128)(2,1)} %param.18) | copy-start | bytes 884740
  0.7 4.5 %copy-start.5 = (f32[1536]{0:T(1024)S(1)}, f32[1536]{0:T(1024)}, u32[]{:S(2)}) copy-start(f32[1536]{0:T(1024)} %param.27) | copy-start | bytes 18436
  0.7 4.5 %copy-start.6 = (f32[1536]{0:T(1024)S(1)}, f32[1536]{0:T(1024)}, u32[]{:S(2)}) copy-start(f32[1536]{0:T(1024)} %param.26) | copy-start | bytes 18436
  55.8 16.9 %all-to-all-start.1 = ((bf16[128,3,384]{2,1,0:T(4,128)(2,1)}), bf16[128,3,384]{2,1,0:T(4,128)(2,1)S(1)}, u32[]{:S(2)}, u32[]{:S(2)}) async-start(bf16[128,3,384]{2,1,0:T(4,128)(2,1)} %reshape.97), calls=%async_computation.1 | async-start | bytes 786432 | tf_op jit(solution)/shard_map/all_to_all | solution.py:266
  73.1 3.6 %copy-start.4 = (f32[1536]{0:T(1024)S(1)}, f32[1536]{0:T(1024)}, u32[]{:S(2)}) copy-start(f32[1536]{0:T(1024)} %param.29) | copy-start | bytes 18436
  78.6 4.8 %copy-start.7 = (f32[384]{0:T(512)S(1)}, f32[384]{0:T(512)}, u32[]{:S(2)}) copy-start(f32[384]{0:T(512)} %param.31) | copy-start | bytes 4612
  78.6 29.6 %all-to-all-start.2 = ((bf16[128,3,1536]{2,1,0:T(4,128)(2,1)}), bf16[128,3,1536]{2,1,0:T(4,128)(2,1)S(1)}, u32[]{:S(2)}, u32[]{:S(2)}) async-start(bf16[128,3,1536]{2,1,0:T(4,128)(2,1)} %bitcast.66), calls=%async_computation.2 | async-start | bytes 3145728 | tf_op jit(solution)/shard_map/all_to_all | solution.py:286
  119.7 4.8 %copy-start.2 = (f32[32,2,1536]{2,1,0:T(2,128)S(1)}, f32[32,2,1536]{2,1,0:T(2,128)}, u32[]{:S(2)}) copy-start(f32[32,2,1536]{2,1,0:T(2,128)} %param.23) | copy-start | bytes 1179652
  119.7 29.6 %all-to-all-start.3 = ((bf16[128,3,1536]{2,1,0:T(4,128)(2,1)}), bf16[128,3,1536]{2,1,0:T(4,128)(2,1)S(1)}, u32[]{:S(2)}, u32[]{:S(2)}) async-start(bf16[128,3,1536]{2,1,0:T(4,128)(2,1)} %reshape.102), calls=%async_computation.3 | async-start | bytes 3145728 | tf_op jit(solution)/shard_map/all_to_all | solution.py:291
  150.4 1.1 copy-start.3
  150.4 1.1 copy-start.8

commit v10 on v7

--- a/solution.py
+++ b/solution.py
@@ -99,47 +99,58 @@
     )(arrived)
 
 
-def _cross_kernel(length_ref, x_ref, wq_ref, gain_ref, keys_ref, values_ref, wo_ref, o_ref, mixed_ref):
+def _cross_kernel(length_ref, x_ref, wq_ref, gain_ref, keys_ref, values_ref, wo_ref, o_ref, total_ref):
+    head = pl.program_id(0)
     factor = 1.0 / math.sqrt(HEAD_DIM)
-    group_width = wq_ref.shape[1]
     text = keys_ref.shape[0]
-    projected = jnp.dot(x_ref[...], wq_ref[...], preferred_element_type=jnp.float32)
-    gains = gain_ref[...]
+    piece = jnp.dot(x_ref[...], wq_ref[...], preferred_element_type=jnp.float32)
+    mean_square = jnp.mean(piece * piece, axis=-1, keepdims=True)
+    queries = (piece * lax.rsqrt(mean_square + EPSILON) * gain_ref[...]).astype(jnp.bfloat16)
     live = (lax.broadcasted_iota(jnp.int32, (1, text), 1) < length_ref[0]).astype(jnp.float32)
-    for head in range(group_width // HEAD_DIM):
-        lanes = slice(head * HEAD_DIM, (head + 1) * HEAD_DIM)
-        piece = projected[:, lanes]
-        mean_square = jnp.mean(piece * piece, axis=-1, keepdims=True)
-        queries = (piece * lax.rsqrt(mean_square + EPSILON) * gains[:, lanes]).astype(jnp.bfloat16)
-        scores = (
-            lax.dot_general(
-                queries, keys_ref[:, lanes], (((1,), (1,)), ((), ())),
-                preferred_element_type=jnp.float32,
-            )
-            * factor
+    scores = (
+        lax.dot_general(
+            queries, keys_ref[...], (((1,), (1,)), ((), ())), preferred_element_type=jnp.float32
         )
-        weights = jnp.exp(scores) * live
-        totals = jnp.sum(weights, axis=-1, keepdims=True)
-        mixture = jnp.dot(
-            weights.astype(jnp.bfloat16), values_ref[:, lanes], preferred_element_type=jnp.float32
-        )
-        mixed_ref[:, lanes] = (mixture / totals).astype(mixed_ref.dtype)
-    o_ref[...] = jnp.dot(mixed_ref[...], wo_ref[...], preferred_element_type=jnp.float32).astype(
-        o_ref.dtype
-    )
+        * factor
+    )
+    weights = jnp.exp(scores) * live
+    totals = jnp.sum(weights, axis=-1, keepdims=True)
+    mixture = jnp.dot(weights.astype(jnp.bfloat16), values_ref[...], preferred_element_type=jnp.float32)
+    mixed = (mixture / totals).astype(jnp.bfloat16)
+    contribution = jnp.dot(mixed, wo_ref[...], preferred_element_type=jnp.float32)
+
+    @pl.when(head == 0)
+    def _():
+        total_ref[...] = contribution
+
+    @pl.when(head > 0)
+    def _():
+        total_ref[...] += contribution
+
+    @pl.when(head == pl.num_programs(0) - 1)
+    def _():
+        o_ref[...] = total_ref[...].astype(o_ref.dtype)
 
 
 def cross_partial(owner_cross, cross_wq, cross_q_gain, keys_own, values_own, length, cross_wo):
     token_total, model_width = owner_cross.shape
     group_width = cross_wq.shape[1]
     text = keys_own.shape[0]
-    vmem = pl.BlockSpec(memory_space=pltpu.VMEM)
     return pl.pallas_call(
         _cross_kernel,
-        in_specs=[pl.BlockSpec(memory_space=pltpu.SMEM)] + [vmem] * 6,
-        out_specs=vmem,
+        grid=(group_width // HEAD_DIM,),
+        in_specs=[
+            pl.BlockSpec(memory_space=pltpu.SMEM),
+            pl.BlockSpec((token_total, model_width), lambda h: (0, 0)),
+            pl.BlockSpec((model_width, HEAD_DIM), lambda h: (0, h)),
+            pl.BlockSpec((1, HEAD_DIM), lambda h: (0, h)),
+            pl.BlockSpec((text, HEAD_DIM), lambda h: (0, h)),
+            pl.BlockSpec((text, HEAD_DIM), lambda h: (0, h)),
+            pl.BlockSpec((HEAD_DIM, model_width), lambda h: (h, 0)),
+        ],
+        out_specs=pl.BlockSpec((token_total, model_width), lambda h: (0, 0)),
         out_shape=jax.ShapeDtypeStruct((token_total, model_width), jnp.bfloat16),
-        scratch_shapes=[pltpu.VMEM((token_total, group_width), jnp.bfloat16)],
+        scratch_shapes=[pltpu.VMEM((token_total, model_width), jnp.float32)],
         cost_estimate=pl.CostEstimate(
             flops=4 * token_total * model_width * group_width + 4 * token_total * text * group_width,
             bytes_accessed=4 * model_width * group_width + 4 * text * group_width

time: 153 us -> 156 us (1.020)
  Pallas kernels: 16.4 us -> 19.7 us
    pallas_call x1, Pallas kernels: 5.43 us -> 8.77 us  [cross_partial(): pl.pallas_call(_cross_kernel, grid=(group_width // HEAD_DIM,), in_specs=[...]
where the time goes in v10:
time: 156 us; the launch traced here: 155 us
  blocking collectives  48.3 us (31%)
  waiting for transfers between devices  48.1 us (31%)
  Pallas kernels  19.7 us (13%)
  local copies, waits for them, and re-layouts  16.1 us (10%)
  starting transfers between devices  9.56 us (6%)
  other arithmetic  7.84 us (5%)
  matrix products  4.26 us (3%)
    all_to_all x1, blocking collectives, local(): lax.all_to_all(packed.reshape(head_count * videos, per_video, 3 * group_w...  31.9 us
    all_to_all x1, waiting for transfers between devices, local(): lax.all_to_all(partial.reshape(head_count * tile_count, per_video, model_...  24.5 us
    all_to_all x1, waiting for transfers between devices, local(): lax.all_to_all(copies, ('head', 'tile'), split_axis=0, concat_axis=0, til...  23.6 us
    all_to_all x1, blocking collectives, local(): lax.all_to_all(own_mixture.reshape(head_count * tile_count, per_video, gr...  16.4 us
    pallas_call x1, Pallas kernels, cross_partial(): pl.pallas_call(_cross_kernel, grid=(group_width // HEAD_DIM,), in_specs=[...  8.77 us
    pallas_call x1, Pallas kernels, pack_projected(): pl.pallas_call(_qkv_kernel, grid=(head_count,), in_specs=[pl.BlockSpec((t...  8.22 us
    all_to_all x1, starting transfers between devices, local(): lax.all_to_all(partial.reshape(head_count * tile_count, per_video, model_...  4.8 us
    all_to_all x1, starting transfers between devices, local(): lax.all_to_all(copies, ('head', 'tile'), split_axis=0, concat_axis=0, til...  4.76 us
  transfers between devices with their start and end apart: 2, of which 2 were waited for; matrix products, arithmetic and copies ran while one was open for 1% of the time, Pallas kernels for 0%

profile of v10, /device:TPU:1, one launch (start us, length us, event | category | flops | bytes accessed | tf_op | source)
XLA Modules:
  0.0 155.3 jit_solution(17150798332784898630)
XLA Ops:
  0.7 0.8 fusion.24
  2.0 1.2 slice_bitcast_fusion.1
  3.2 1.1 convert_reduce_fusion
  4.6 0.2 fusion.14
  4.8 0.3 copy.35
  5.1 1.0 reshape.103.x_ref
  6.2 0.6 pad_maximum_fusion.3.gain_ref
  6.9 0.3 fusion.30
  7.2 0.7 pad_maximum_fusion.1
  7.9 8.2 %shard_map.185 = bf16[4,96,1152]{2,1,0:T(8,128)(2,1)} custom-call(bf16[96,1536]{1,0:T(8,128)(2,1)} %reshape.103.x_ref, bf16[1536,4608]{1,0:T(8,128)(2,1)} %wv_ref.1, bf16[1536,4608]{1,0:T(8,128)(2,1)} %wv_ref.1, bf16[1536,4608]{1,0:T(8,128)(2,1)} %wv_ref.1, f32[96,128]{1,0:T(8,128)} %get-tuple-element.19.cos_ref, f32[96,128]{1,0:T(8,128)} %get-tuple-element.20.sin_ref, ...), custom_call_target="tpu_custom_call" | custom-call | flops 1358954496 | bytes 15925248 | tf_op jit(solution)/shard_map/pallas_call | solution.py:198
  16.1 2.5 %reshape_reshape.3 = bf16[128,3,1152]{2,1,0:T(4,128)(2,1)S(1)} reshape(bf16[4,96,1152]{2,1,0:T(8,128)(2,1)} %shard_map.185) | data formatting | bytes 1769472 | tf_op jit(solution)/shard_map/reshape;reshape | solution.py:253
  18.6 31.9 %all_to_all.20 = bf16[128,3,1152]{2,1,0:T(4,128)(2,1)S(1)} all-to-all(bf16[128,3,1152]{2,1,0:T(4,128)(2,1)S(1)} %reshape_reshape.3), channel_id=1, replica_groups=mesh['head'=4,'tile'=32] {'head','tile'}, dimensions={0} | all-to-all | bytes 1769472 | tf_op jit(solution)/shard_map/all_to_all | solution.py:252
  50.5 1.5 reshape.104.x_ref
  52.0 2.7 %shard_map.186 = bf16[384,384]{1,0:T(8,128)(2,1)} custom-call(bf16[384,1152]{1,0:T(8,128)(2,1)} %reshape.104.x_ref), custom_call_target="tpu_custom_call" | custom-call | flops 226492416 | bytes 1179648 | tf_op jit(solution)/shard_map/pallas_call | solution.py:91
  54.7 1.1 reshape.105
  55.8 16.4 %all_to_all.21 = bf16[128,3,384]{2,1,0:T(4,128)(2,1)S(1)} all-to-all(bf16[128,3,384]{2,1,0:T(4,128)(2,1)S(1)} %reshape.105), channel_id=1, replica_groups=mesh['head'=4,'tile'=32] {'head','tile'}, dimensions={0} | all-to-all | bytes 589824 | tf_op jit(solution)/shard_map/all_to_all | solution.py:260
  72.2 0.3 copy.61
  72.7 3.3 %fusion.33 = (f32[32,3]{0,1:T(4,128)S(1)}, f32[32,3,1536]{2,0,1:T(8,128)S(1)}) fusion(bf16[32,3,1536]{2,0,1:T(8,128)(2,1)S(1)} %dot_general.8, bf16[1536,1536]{1,0:T(8,128)(2,1)} %param.28, f32[32,1536]{1,0:T(8,128)S(1)} %get-tuple-element.6, bf16[32,3,1536]{2,0,1:T(8,128)(2,1)S(1)} %copy-done.1), kind=kOutput, calls=%fused_computation.67 | convolution fusion | flops 453574560 | bytes 6095232 | tf_op jit(solution)/shard_map/dot_general | solution.py:272
  76.4 0.3 copy.40
  76.6 1.6 %broadcast_in_dim.2 = bf16[4,32,3,1536]{3,2,1,0:T(4,128)(2,1)} broadcast(bf16[32,3,1536]{2,1,0:T(4,128)(2,1)S(1)} %copy.40), dimensions={1,2,3} | broadcast | bytes 1474560 | tf_op jit(solution)/shard_map/broadcast_in_dim | solution.py:277
  78.2 4.8 %all-to-all-start.2 = ((bf16[128,3,1536]{2,1,0:T(4,128)(2,1)}), bf16[128,3,1536]{2,1,0:T(4,128)(2,1)S(1)}, u32[]{:S(2)}, u32[]{:S(2)}) async-start(bf16[128,3,1536]{2,1,0:T(4,128)(2,1)} %bitcast.34), calls=%async_computation.2 | async-start | bytes 3145728 | tf_op jit(solution)/shard_map/all_to_all | solution.py:280
  83.0 0.6 reshape.109.gain_ref
  84.2 23.6 %all-to-all-done.2 = bf16[128,3,1536]{2,1,0:T(4,128)(2,1)S(1)} async-done(((bf16[128,3,1536]{2,1,0:T(4,128)(2,1)}), bf16[128,3,1536]{2,1,0:T(4,128)(2,1)S(1)}, u32[]{:S(2)}, u32[]{:S(2)}) %all-to-all-start.2) | async-done | bytes 1179680 | tf_op jit(solution)/shard_map/all_to_all | solution.py:280
  107.8 2.2 %reshape.108.x_ref = bf16[384,1536]{1,0:T(8,128)(2,1)} reshape(bf16[128,3,1536]{2,1,0:T(4,128)(2,1)S(1)} %all-to-all-done.2) | data formatting | bytes 2359296 | tf_op jit(solution)/shard_map/reshape | solution.py:281
  110.0 8.8 %shard_map.187 = bf16[384,1536]{1,0:T(8,128)(2,1)} custom-call(s32[1]{0:T(128)S(6)} %copy.62.length_ref, bf16[384,1536]{1,0:T(8,128)(2,1)} %reshape.108.x_ref, bf16[1536,384]{1,0:T(8,128)(2,1)} %wq_ref.3, f32[1,384]{1,0:T(1,128)} %reshape.109.gain_ref, bf16[512,384]{1,0:T(8,128)(2,1)} %bitcast.37, bf16[512,384]{1,0:T(8,128)(2,1)} %bitcast.38, ...), custom_call_target="tpu_custom_call" | custom-call | flops 1207959552 | bytes 5505024 | tf_op jit(solution)/shard_map/pallas_call | solution.py:139
  118.7 3.8 %reshape.110 = bf16[128,3,1536]{2,1,0:T(4,128)(2,1)} reshape(bf16[384,1536]{1,0:T(8,128)(2,1)} %shard_map.187) | data formatting | bytes 2359296 | tf_op jit(solution)/shard_map/reshape | solution.py:286
  122.5 4.8 %all-to-all-start.3 = ((bf16[128,3,1536]{2,1,0:T(4,128)(2,1)}), bf16[128,3,1536]{2,1,0:T(4,128)(2,1)S(1)}, u32[]{:S(2)}, u32[]{:S(2)}) async-start(bf16[128,3,1536]{2,1,0:T(4,128)(2,1)} %reshape.110), calls=%async_computation.3 | async-start | bytes 3145728 | tf_op jit(solution)/shard_map/all_to_all | solution.py:285
  127.3 0.3 fusion.32
  127.7 24.5 %all-to-all-done.3 = bf16[128,3,1536]{2,1,0:T(4,128)(2,1)S(1)} async-done(((bf16[128,3,1536]{2,1,0:T(4,128)(2,1)}), bf16[128,3,1536]{2,1,0:T(4,128)(2,1)S(1)}, u32[]{:S(2)}, u32[]{:S(2)}) %all-to-all-start.3) | async-done | bytes 1179680 | tf_op jit(solution)/shard_map/all_to_all | solution.py:285
  152.1 1.1 reduce_sum.70
  153.4 0.9 multiply_reduce_fusion
  154.3 0.9 fusion.8
  (42 shorter events, 1.8 us)
Async XLA Ops:
  0.6 153.7 %copy-start = (bf16[1536,64]{0,1:T(8,128)(2,1)S(1)}, bf16[1536,64]{0,1:T(8,128)(2,1)}, u32[]{:S(2)}) copy-start(bf16[1536,64]{0,1:T(8,128)(2,1)} %param.35) | copy-start | bytes 589828
  0.6 3.7 %copy-start.1 = (bf16[32,3,1536]{2,0,1:T(8,128)(2,1)S(1)}, bf16[32,3,1536]{2,0,1:T(8,128)(2,1)}, u32[]{:S(2)}) copy-start(bf16[32,3,1536]{2,0,1:T(8,128)(2,1)} %param.18) | copy-start | bytes 884740
  3.2 2.8 %copy-start.5 = (f32[1536]{0:T(1024)S(1)}, f32[1536]{0:T(1024)}, u32[]{:S(2)}) copy-start(f32[1536]{0:T(1024)} %param.27) | copy-start | bytes 18436
  3.2 2.8 %copy-start.6 = (f32[1536]{0:T(1024)S(1)}, f32[1536]{0:T(1024)}, u32[]{:S(2)}) copy-start(f32[1536]{0:T(1024)} %param.26) | copy-start | bytes 18436
  72.6 3.6 %copy-start.4 = (f32[1536]{0:T(1024)S(1)}, f32[1536]{0:T(1024)}, u32[]{:S(2)}) copy-start(f32[1536]{0:T(1024)} %param.29) | copy-start | bytes 18436
  78.2 4.8 %copy-start.7 = (f32[384]{0:T(512)S(1)}, f32[384]{0:T(512)}, u32[]{:S(2)}) copy-start(f32[384]{0:T(512)} %param.31) | copy-start | bytes 4612
  78.2 29.6 %all-to-all-start.2 = ((bf16[128,3,1536]{2,1,0:T(4,128)(2,1)}), bf16[128,3,1536]{2,1,0:T(4,128)(2,1)S(1)}, u32[]{:S(2)}, u32[]{:S(2)}) async-start(bf16[128,3,1536]{2,1,0:T(4,128)(2,1)} %bitcast.34), calls=%async_computation.2 | async-start | bytes 3145728 | tf_op jit(solution)/shard_map/all_to_all | solution.py:280
  122.5 4.8 %copy-start.2 = (f32[32,2,1536]{2,1,0:T(2,128)S(1)}, f32[32,2,1536]{2,1,0:T(2,128)}, u32[]{:S(2)}) copy-start(f32[32,2,1536]{2,1,0:T(2,128)} %param.23) | copy-start | bytes 1179652
  122.5 29.6 %all-to-all-start.3 = ((bf16[128,3,1536]{2,1,0:T(4,128)(2,1)}), bf16[128,3,1536]{2,1,0:T(4,128)(2,1)S(1)}, u32[]{:S(2)}, u32[]{:S(2)}) async-start(bf16[128,3,1536]{2,1,0:T(4,128)(2,1)} %reshape.110), calls=%async_computation.3 | async-start | bytes 3145728 | tf_op jit(solution)/shard_map/all_to_all | solution.py:285
  153.2 1.1 copy-start.3
  153.2 1.1 copy-start.8

commit v11 on v9

--- a/solution.py
+++ b/solution.py
@@ -150,15 +150,16 @@
 
 
 def _qkv_kernel(
-    hidden_ref, modulation_ref, wq_ref, wk_ref, wv_ref, cos_ref, sin_ref, gain_ref, o_ref, normed_ref
+    hidden_ref, shift_ref, scale_ref, wq_ref, wk_ref, wv_ref, cos_ref, sin_ref, gain_ref, o_ref,
+    normed_ref,
 ):
     group = pl.program_id(0)
     videos, per_video, _ = hidden_ref.shape
 
     @pl.when(group == 0)
     def _():
-        shift = modulation_ref[:, 0, :]
-        scale = 1.0 + modulation_ref[:, 1, :]
+        shift = shift_ref[...]
+        scale = 1.0 + scale_ref[...]
         for slot in range(per_video):
             stream = hidden_ref[:, slot, :].astype(jnp.float32)
             normed_ref[slot * videos : (slot + 1) * videos, :] = (
@@ -204,7 +205,8 @@
         grid=(head_count,),
         in_specs=[
             pl.BlockSpec(hidden.shape, whole3),
-            pl.BlockSpec(block_modulation.shape, whole3),
+            pl.BlockSpec((videos, model_width), whole2),
+            pl.BlockSpec((videos, model_width), whole2),
             pl.BlockSpec((model_width, group_width), lambda g: (0, g)),
             pl.BlockSpec((model_width, group_width), lambda g: (0, head_count + g)),
             pl.BlockSpec((model_width, group_width), lambda g: (0, 2 * head_count + g)),
@@ -220,7 +222,10 @@
             bytes_accessed=2 * model_width * 3 * model_width + 4 * token_total * 3 * model_width,
             transcendentals=0,
         ),
-    )(hidden, block_modulation, w_qkv, w_qkv, w_qkv, cos_full, sin_signed, gains)
+    )(
+        hidden, block_modulation[:, 0], block_modulation[:, 1], w_qkv, w_qkv, w_qkv,
+        cos_full, sin_signed, gains,
+    )
     packed = packed.reshape(head_count, per_video, videos, 3 * group_width)
     return jnp.transpose(packed, (0, 2, 1, 3))
 

time: 153 us -> 152 us (level)
  blocking collectives: 31.9 us -> 48.3 us
  waiting for transfers between devices: 59.4 us -> 48.1 us
  starting transfers between devices: 14.1 us -> 9.57 us
    all_to_all x0 -> x1, blocking collectives: none -> 16.4 us  [local(): lax.all_to_all(own_mixture.reshape(head_count * tile_count, per_video, gr...]
    all_to_all x1 -> x0, waiting for transfers between devices: 11.4 us -> none  [local(): lax.all_to_all(own_mixture.reshape(head_count * tile_count, per_video, gr...]
    all_to_all x1 -> x0, starting transfers between devices: 4.59 us -> none  [local(): lax.all_to_all(own_mixture.reshape(head_count * tile_count, per_video, gr...]
    unnamed x20 -> x19, local copies, waits for them, and re-layouts: 3.46 us -> 2.01 us
  transfers between devices with their start and end apart: 3 -> 2, of which waited for: 3 -> 2; matrix products, arithmetic and copies ran while one was open for 1% -> 1% of each run, Pallas kernels for 0% -> 0%
where the time goes in v11:
time: 152 us; the launch traced here: 151 us
  blocking collectives  48.3 us (32%)
  waiting for transfers between devices  48.1 us (32%)
  local copies, waits for them, and re-layouts  17.6 us (12%)
  Pallas kernels  17.1 us (11%)
  starting transfers between devices  9.57 us (6%)
  other arithmetic  5.08 us (3%)
  matrix products  4.25 us (3%)
    all_to_all x1, blocking collectives, local(): lax.all_to_all(packed.reshape(head_count * videos, per_video, 3 * group_w...  31.9 us
    all_to_all x1, waiting for transfers between devices, local(): lax.all_to_all(partial.reshape(head_count * tile_count, per_video, model_...  24.5 us
    all_to_all x1, waiting for transfers between devices, local(): lax.all_to_all(copies, ('head', 'tile'), split_axis=0, concat_axis=0, til...  23.6 us
    all_to_all x1, blocking collectives, local(): lax.all_to_all(own_mixture.reshape(head_count * tile_count, per_video, gr...  16.4 us
    pallas_call x1, Pallas kernels, pack_projected(): pl.pallas_call(_qkv_kernel, grid=(head_count,), in_specs=[pl.BlockSpec(hi...  8.9 us
    pallas_call x1, Pallas kernels, cross_partial(): pl.pallas_call(_cross_kernel, in_specs=[pl.BlockSpec(memory_space=pltpu.S...  5.45 us
    all_to_all x1, starting transfers between devices, local(): lax.all_to_all(partial.reshape(head_count * tile_count, per_video, model_...  4.81 us
    all_to_all x1, starting transfers between devices, local(): lax.all_to_all(copies, ('head', 'tile'), split_axis=0, concat_axis=0, til...  4.76 us
  transfers between devices with their start and end apart: 2, of which 2 were waited for; matrix products, arithmetic and copies ran while one was open for 1% of the time, Pallas kernels for 0%

profile of v11, /device:TPU:1, one launch (start us, length us, event | category | flops | bytes accessed | tf_op | source)
XLA Modules:
  0.0 151.4 jit_solution(1869733287559831668)
XLA Ops:
  0.7 0.7 fusion.20
  1.7 1.9 %slice_bitcast_fusion.2 = (f32[32,1536]{1,0:T(8,128)S(1)}, f32[32,1536]{1,0:T(8,128)}, f32[32,1536]{1,0:T(8,128)}) fusion(f32[32,3,1536]{2,0,1:T(8,128)} %param.22), kind=kLoop, calls=%fused_computation.22 | loop fusion | bytes 1179648 | tf_op jit(solution)/shard_map/mul | solution.py:286
  3.6 2.0 %copy.30.hidden_ref = bf16[32,3,1536]{2,1,0:T(4,128)(2,1)} copy(bf16[32,3,1536]{2,0,1:T(8,128)(2,1)} %param.18) | data formatting | bytes 589824 | tf_op args[0]
  5.7 0.6 pad_maximum_fusion.3.gain_ref
  6.4 0.3 fusion.26
  6.6 0.7 pad_maximum_fusion.1
  7.4 8.9 %shard_map.185 = bf16[4,96,1152]{2,1,0:T(8,128)(2,1)} custom-call(bf16[32,3,1536]{2,1,0:T(4,128)(2,1)} %copy.30.hidden_ref, f32[32,1536]{1,0:T(8,128)} %get-tuple-element.8.shift_ref, f32[32,1536]{1,0:T(8,128)} %get-tuple-element.7.scale_ref, bf16[1536,4608]{1,0:T(8,128)(2,1)} %wv_ref.1, bf16[1536,4608]{1,0:T(8,128)(2,1)} %wv_ref.1, ...), custom_call_target="tpu_custom_call" | custom-call | flops 1358954496 | bytes 15925248 | tf_op jit(solution)/shard_map/pallas_call | solution.py:203
  16.3 1.8 %copy.31 = bf16[4,32,3,1152]{3,2,1,0:T(4,128)(2,1)S(1)} copy(bf16[4,32,3,1152]{3,1,2,0:T(8,128)(2,1)} %bitcast.72) | data formatting | bytes 1769472 | tf_op jit(solution)/shard_map/transpose | solution.py:230
  18.1 31.9 %all_to_all.20 = bf16[128,3,1152]{2,1,0:T(4,128)(2,1)S(1)} all-to-all(bf16[128,3,1152]{2,1,0:T(4,128)(2,1)S(1)} %bitcast.71), channel_id=1, replica_groups=mesh['head'=4,'tile'=32] {'head','tile'}, dimensions={0} | all-to-all | bytes 1769472 | tf_op jit(solution)/shard_map/all_to_all | solution.py:263
  49.9 1.5 reshape.96.x_ref
  51.4 2.7 %shard_map.186 = bf16[384,384]{1,0:T(8,128)(2,1)} custom-call(bf16[384,1152]{1,0:T(8,128)(2,1)} %reshape.96.x_ref), custom_call_target="tpu_custom_call" | custom-call | flops 226492416 | bytes 1179648 | tf_op jit(solution)/shard_map/pallas_call | solution.py:91
  54.1 1.1 reshape.97
  55.3 16.4 %all_to_all.21 = bf16[128,3,384]{2,1,0:T(4,128)(2,1)S(1)} all-to-all(bf16[128,3,384]{2,1,0:T(4,128)(2,1)S(1)} %reshape.97), channel_id=1, replica_groups=mesh['head'=4,'tile'=32] {'head','tile'}, dimensions={0} | all-to-all | bytes 589824 | tf_op jit(solution)/shard_map/all_to_all | solution.py:271
  71.7 0.3 copy.54
  72.1 3.3 %fusion.29 = (f32[32,3]{0,1:T(4,128)S(1)}, f32[32,3,1536]{2,0,1:T(8,128)S(1)}) fusion(bf16[32,3,1536]{2,0,1:T(8,128)(2,1)S(1)} %dot_general.8, bf16[1536,1536]{1,0:T(8,128)(2,1)} %param.28, f32[32,1536]{1,0:T(8,128)S(1)} %get-tuple-element.6, bf16[32,3,1536]{2,0,1:T(8,128)(2,1)S(1)} %copy-done.1), kind=kOutput, calls=%fused_computation.60 | convolution fusion | flops 453574560 | bytes 6095232 | tf_op jit(solution)/shard_map/dot_general | solution.py:283
  75.4 0.2 multiply_reduce_fusion.1
  75.7 0.2 multiply_convert_fusion
  75.8 0.3 copy.33
  76.1 1.6 %broadcast_in_dim.2 = bf16[4,32,3,1536]{3,2,1,0:T(4,128)(2,1)} broadcast(bf16[32,3,1536]{2,1,0:T(4,128)(2,1)S(1)} %copy.33), dimensions={1,2,3} | broadcast | bytes 1474560 | tf_op jit(solution)/shard_map/broadcast_in_dim | solution.py:288
  77.6 4.8 %all-to-all-start.2 = ((bf16[128,3,1536]{2,1,0:T(4,128)(2,1)}), bf16[128,3,1536]{2,1,0:T(4,128)(2,1)S(1)}, u32[]{:S(2)}, u32[]{:S(2)}) async-start(bf16[128,3,1536]{2,1,0:T(4,128)(2,1)} %bitcast.70), calls=%async_computation.2 | async-start | bytes 3145728 | tf_op jit(solution)/shard_map/all_to_all | solution.py:291
  82.4 0.6 reshape.101.gain_ref
  83.6 23.6 %all-to-all-done.2 = bf16[128,3,1536]{2,1,0:T(4,128)(2,1)S(1)} async-done(((bf16[128,3,1536]{2,1,0:T(4,128)(2,1)}), bf16[128,3,1536]{2,1,0:T(4,128)(2,1)S(1)}, u32[]{:S(2)}, u32[]{:S(2)}) %all-to-all-start.2) | async-done | bytes 1179680 | tf_op jit(solution)/shard_map/all_to_all | solution.py:291
  107.2 2.2 %reshape.100.x_ref = bf16[384,1536]{1,0:T(8,128)(2,1)} reshape(bf16[128,3,1536]{2,1,0:T(4,128)(2,1)S(1)} %all-to-all-done.2) | data formatting | bytes 2359296 | tf_op jit(solution)/shard_map/reshape | solution.py:292
  109.4 5.5 %shard_map.187 = bf16[384,1536]{1,0:T(8,128)(2,1)} custom-call(s32[1]{0:T(128)S(6)} %copy.55.length_ref, bf16[384,1536]{1,0:T(8,128)(2,1)} %reshape.100.x_ref, bf16[1536,384]{1,0:T(8,128)(2,1)} %wq_ref.3, f32[1,384]{1,0:T(1,128)} %reshape.101.gain_ref, bf16[512,384]{1,0:T(8,128)(2,1)} %bitcast.75, bf16[512,384]{1,0:T(8,128)(2,1)} %bitcast.76, ...), custom_call_target="tpu_custom_call" | custom-call | flops 1207959552 | bytes 5505024 | tf_op jit(solution)/shard_map/pallas_call | solution.py:137
  114.9 3.8 %reshape.102 = bf16[128,3,1536]{2,1,0:T(4,128)(2,1)} reshape(bf16[384,1536]{1,0:T(8,128)(2,1)} %shard_map.187) | data formatting | bytes 2359296 | tf_op jit(solution)/shard_map/reshape | solution.py:297
  118.6 4.8 %all-to-all-start.3 = ((bf16[128,3,1536]{2,1,0:T(4,128)(2,1)}), bf16[128,3,1536]{2,1,0:T(4,128)(2,1)S(1)}, u32[]{:S(2)}, u32[]{:S(2)}) async-start(bf16[128,3,1536]{2,1,0:T(4,128)(2,1)} %reshape.102), calls=%async_computation.3 | async-start | bytes 3145728 | tf_op jit(solution)/shard_map/all_to_all | solution.py:296
  123.5 0.3 fusion.28
  123.8 24.5 %all-to-all-done.3 = bf16[128,3,1536]{2,1,0:T(4,128)(2,1)S(1)} async-done(((bf16[128,3,1536]{2,1,0:T(4,128)(2,1)}), bf16[128,3,1536]{2,1,0:T(4,128)(2,1)S(1)}, u32[]{:S(2)}, u32[]{:S(2)}) %all-to-all-start.3) | async-done | bytes 1179680 | tf_op jit(solution)/shard_map/all_to_all | solution.py:296
  148.3 1.1 reduce_sum.50
  149.4 0.2 fusion.24
  149.6 0.9 multiply_reduce_fusion
  150.5 0.9 fusion.8
  (33 shorter events, 0.7 us)
Async XLA Ops:
  0.6 149.8 %copy-start = (bf16[1536,64]{0,1:T(8,128)(2,1)S(1)}, bf16[1536,64]{0,1:T(8,128)(2,1)}, u32[]{:S(2)}) copy-start(bf16[1536,64]{0,1:T(8,128)(2,1)} %param.35) | copy-start | bytes 589828
  0.6 4.9 %copy-start.5 = (f32[1536]{0:T(1024)S(1)}, f32[1536]{0:T(1024)}, u32[]{:S(2)}) copy-start(f32[1536]{0:T(1024)} %param.27) | copy-start | bytes 18436
  0.7 4.9 %copy-start.6 = (f32[1536]{0:T(1024)S(1)}, f32[1536]{0:T(1024)}, u32[]{:S(2)}) copy-start(f32[1536]{0:T(1024)} %param.26) | copy-start | bytes 18436
  54.1 17.9 %copy-start.1 = (bf16[32,3,1536]{2,0,1:T(8,128)(2,1)S(1)}, bf16[32,3,1536]{2,0,1:T(8,128)(2,1)}, u32[]{:S(2)}) copy-start(bf16[32,3,1536]{2,0,1:T(8,128)(2,1)} %param.18) | copy-start | bytes 884740
  72.1 3.6 %copy-start.4 = (f32[1536]{0:T(1024)S(1)}, f32[1536]{0:T(1024)}, u32[]{:S(2)}) copy-start(f32[1536]{0:T(1024)} %param.29) | copy-start | bytes 18436
  77.6 4.8 %copy-start.7 = (f32[384]{0:T(512)S(1)}, f32[384]{0:T(512)}, u32[]{:S(2)}) copy-start(f32[384]{0:T(512)} %param.31) | copy-start | bytes 4612
  77.6 29.6 %all-to-all-start.2 = ((bf16[128,3,1536]{2,1,0:T(4,128)(2,1)}), bf16[128,3,1536]{2,1,0:T(4,128)(2,1)S(1)}, u32[]{:S(2)}, u32[]{:S(2)}) async-start(bf16[128,3,1536]{2,1,0:T(4,128)(2,1)} %bitcast.70), calls=%async_computation.2 | async-start | bytes 3145728 | tf_op jit(solution)/shard_map/all_to_all | solution.py:291
  118.6 4.8 %copy-start.2 = (f32[32,2,1536]{2,1,0:T(2,128)S(1)}, f32[32,2,1536]{2,1,0:T(2,128)}, u32[]{:S(2)}) copy-start(f32[32,2,1536]{2,1,0:T(2,128)} %param.23) | copy-start | bytes 1179652
  118.6 29.6 %all-to-all-start.3 = ((bf16[128,3,1536]{2,1,0:T(4,128)(2,1)}), bf16[128,3,1536]{2,1,0:T(4,128)(2,1)S(1)}, u32[]{:S(2)}, u32[]{:S(2)}) async-start(bf16[128,3,1536]{2,1,0:T(4,128)(2,1)} %reshape.102), calls=%async_computation.3 | async-start | bytes 3145728 | tf_op jit(solution)/shard_map/all_to_all | solution.py:296
  149.4 1.1 copy-start.3
  149.4 1.1 copy-start.8

commit v12 on v7

--- a/solution.py
+++ b/solution.py
@@ -264,7 +264,7 @@
     after_self = stream + block_gate * self_update
     cross_in = (layer_norm(after_self) * cross_gain).astype(jnp.bfloat16)
     copies = jnp.broadcast_to(cross_in[None], (head_count,) + cross_in.shape).reshape(
-        head_count * videos, per_video, model_width
+        head_count * videos, 2, per_video * model_width // 2
     )
     owner_cross = lax.all_to_all(copies, ("head", "tile"), split_axis=0, concat_axis=0, tiled=True)
     owner_cross = owner_cross.reshape(-1, model_width)
@@ -272,7 +272,7 @@
         owner_cross, cross_wq, cross_q_gain, text_keys[0], text_values[0], text_lengths, cross_wo
     )
     returned_partials = lax.all_to_all(
-        partial.reshape(head_count * tile_count, per_video, model_width),
+        partial.reshape(head_count * tile_count, 2, per_video * model_width // 2),
         ("head", "tile"),
         split_axis=0,
         concat_axis=0,

time: 153 us -> 148 us (0.967)
  waiting for transfers between devices: 48.1 us -> 39.5 us
  local copies, waits for them, and re-layouts: 16 us -> 19.7 us
    reshape x1 -> x3, local copies, waits for them, and re-layouts: 3.78 us -> 9.12 us  [the longest x1 4.01 us: local(): returned_partials = lax.all_to_all(partial.reshape(head_count * tile_coun...]
    all_to_all x1, waiting for transfers between devices: 24.5 us -> 20 us  [local(): lax.all_to_all(partial.reshape(head_count * tile_count, 2, per_video * mo...]
    all_to_all x1, waiting for transfers between devices: 23.6 us -> 19.5 us  [local(): lax.all_to_all(copies, ('head', 'tile'), split_axis=0, concat_axis=0, til...]
where the time goes in v12:
time: 148 us; the launch traced here: 147 us
  blocking collectives  48.2 us (33%)
  waiting for transfers between devices  39.5 us (27%)
  local copies, waits for them, and re-layouts  19.7 us (13%)
  Pallas kernels  16.4 us (11%)
  starting transfers between devices  10.7 us (7%)
  other arithmetic  6.86 us (5%)
  matrix products  4.26 us (3%)
  between operations  1.56 us (1%)
    all_to_all x1, blocking collectives, local(): lax.all_to_all(packed.reshape(head_count * videos, per_video, 3 * group_w...  31.9 us
    all_to_all x1, waiting for transfers between devices, local(): lax.all_to_all(partial.reshape(head_count * tile_count, 2, per_video * mo...  20 us
    all_to_all x1, waiting for transfers between devices, local(): lax.all_to_all(copies, ('head', 'tile'), split_axis=0, concat_axis=0, til...  19.5 us
    all_to_all x1, blocking collectives, local(): lax.all_to_all(own_mixture.reshape(head_count * tile_count, per_video, gr...  16.4 us
    pallas_call x1, Pallas kernels, pack_projected(): pl.pallas_call(_qkv_kernel, grid=(head_count,), in_specs=[pl.BlockSpec((t...  8.22 us
    all_to_all x1, starting transfers between devices, local(): lax.all_to_all(partial.reshape(head_count * tile_count, 2, per_video * mo...  5.92 us
    pallas_call x1, Pallas kernels, cross_partial(): pl.pallas_call(_cross_kernel, in_specs=[pl.BlockSpec(memory_space=pltpu.S...  5.43 us
    all_to_all x1, starting transfers between devices, local(): lax.all_to_all(copies, ('head', 'tile'), split_axis=0, concat_axis=0, til...  4.75 us
  transfers between devices with their start and end apart: 2, of which 2 were waited for; matrix products, arithmetic and copies ran while one was open for 1% of the time, Pallas kernels for 0%

profile of v12, /device:TPU:1, one launch (start us, length us, event | category | flops | bytes accessed | tf_op | source)
XLA Modules:
  0.0 147.1 jit_solution(10978327572862215418)
XLA Ops:
  0.7 0.8 fusion.24
  2.0 1.2 slice_bitcast_fusion.1
  3.8 0.3 copy.35
  4.1 1.0 reshape.103.x_ref
  5.2 0.6 pad_maximum_fusion.3.gain_ref
  5.9 0.3 fusion.30
  6.2 0.7 pad_maximum_fusion.1
  6.9 8.2 %shard_map.185 = bf16[4,96,1152]{2,1,0:T(8,128)(2,1)} custom-call(bf16[96,1536]{1,0:T(8,128)(2,1)} %reshape.103.x_ref, bf16[1536,4608]{1,0:T(8,128)(2,1)} %wv_ref.1, bf16[1536,4608]{1,0:T(8,128)(2,1)} %wv_ref.1, bf16[1536,4608]{1,0:T(8,128)(2,1)} %wv_ref.1, f32[96,128]{1,0:T(8,128)} %get-tuple-element.19.cos_ref, f32[96,128]{1,0:T(8,128)} %get-tuple-element.20.sin_ref, ...), custom_call_target="tpu_custom_call" | custom-call | flops 1358954496 | bytes 15925248 | tf_op jit(solution)/shard_map/pallas_call | solution.py:187
  15.1 2.5 %reshape_reshape.3 = bf16[128,3,1152]{2,1,0:T(4,128)(2,1)S(1)} reshape(bf16[4,96,1152]{2,1,0:T(8,128)(2,1)} %shard_map.185) | data formatting | bytes 1769472 | tf_op jit(solution)/shard_map/reshape;reshape | solution.py:242
  17.7 31.9 %all_to_all.20 = bf16[128,3,1152]{2,1,0:T(4,128)(2,1)S(1)} all-to-all(bf16[128,3,1152]{2,1,0:T(4,128)(2,1)S(1)} %reshape_reshape.3), channel_id=1, replica_groups=mesh['head'=4,'tile'=32] {'head','tile'}, dimensions={0} | all-to-all | bytes 1769472 | tf_op jit(solution)/shard_map/all_to_all | solution.py:241
  49.5 1.5 %reshape.104.x_ref = bf16[384,1152]{1,0:T(8,128)(2,1)} reshape(bf16[128,3,1152]{2,1,0:T(4,128)(2,1)S(1)} %all_to_all.20) | data formatting | bytes 1769472 | tf_op jit(solution)/shard_map/reshape | solution.py:248
  51.0 2.7 %shard_map.186 = bf16[384,384]{1,0:T(8,128)(2,1)} custom-call(bf16[384,1152]{1,0:T(8,128)(2,1)} %reshape.104.x_ref), custom_call_target="tpu_custom_call" | custom-call | flops 226492416 | bytes 1179648 | tf_op jit(solution)/shard_map/pallas_call | solution.py:91
  53.8 1.1 reshape.105
  54.9 16.4 %all_to_all.21 = bf16[128,3,384]{2,1,0:T(4,128)(2,1)S(1)} all-to-all(bf16[128,3,384]{2,1,0:T(4,128)(2,1)S(1)} %reshape.105), channel_id=1, replica_groups=mesh['head'=4,'tile'=32] {'head','tile'}, dimensions={0} | all-to-all | bytes 589824 | tf_op jit(solution)/shard_map/all_to_all | solution.py:249
  71.2 0.3 copy.61
  71.7 3.3 %fusion.33 = (f32[32,3]{0,1:T(4,128)S(1)}, f32[32,3,1536]{2,0,1:T(8,128)S(1)}) fusion(bf16[32,3,1536]{2,0,1:T(8,128)(2,1)S(1)} %dot_general.8, bf16[1536,1536]{1,0:T(8,128)(2,1)} %param.28, f32[32,1536]{1,0:T(8,128)S(1)} %get-tuple-element.6, bf16[32,3,1536]{2,0,1:T(8,128)(2,1)S(1)} %copy-done.1), kind=kOutput, calls=%fused_computation.67 | convolution fusion | flops 453574560 | bytes 6095232 | tf_op jit(solution)/shard_map/dot_general | solution.py:261
  75.4 0.3 copy.40
  75.6 0.4 broadcast_in_dim.2
  76.1 2.4 %reshape.107 = bf16[128,2,2304]{2,1,0:T(2,128)(2,1)} reshape(bf16[4,32,3,1536]{3,2,1,0:T(4,128)(2,1)S(1)} %broadcast_in_dim.2) | data formatting | bytes 2359296 | tf_op jit(solution)/shard_map/reshape | solution.py:266
  78.5 4.8 %all-to-all-start.2 = ((bf16[128,2,2304]{2,1,0:T(2,128)(2,1)}), bf16[128,2,2304]{2,1,0:T(2,128)(2,1)S(1)}, u32[]{:S(2)}, u32[]{:S(2)}) async-start(bf16[128,2,2304]{2,1,0:T(2,128)(2,1)} %reshape.107), calls=%async_computation.2 | async-start | bytes 2359296 | tf_op jit(solution)/shard_map/all_to_all | solution.py:269
  83.3 0.6 reshape.109.gain_ref
  84.5 19.5 %all-to-all-done.2 = bf16[128,2,2304]{2,1,0:T(2,128)(2,1)S(1)} async-done(((bf16[128,2,2304]{2,1,0:T(2,128)(2,1)}), bf16[128,2,2304]{2,1,0:T(2,128)(2,1)S(1)}, u32[]{:S(2)}, u32[]{:S(2)}) %all-to-all-start.2) | async-done | bytes 1179680 | tf_op jit(solution)/shard_map/all_to_all | solution.py:269
  104.0 1.6 %reshape.108.x_ref = bf16[384,1536]{1,0:T(8,128)(2,1)} reshape(bf16[128,2,2304]{2,1,0:T(2,128)(2,1)S(1)} %all-to-all-done.2) | data formatting | bytes 2359296 | tf_op jit(solution)/shard_map/reshape | solution.py:270
  105.6 5.4 %shard_map.187 = bf16[384,1536]{1,0:T(8,128)(2,1)} custom-call(s32[1]{0:T(128)S(6)} %copy.62.length_ref, bf16[384,1536]{1,0:T(8,128)(2,1)} %reshape.108.x_ref, bf16[1536,384]{1,0:T(8,128)(2,1)} %wq_ref.3, f32[1,384]{1,0:T(1,128)} %reshape.109.gain_ref, bf16[512,384]{1,0:T(8,128)(2,1)} %bitcast.33, bf16[512,384]{1,0:T(8,128)(2,1)} %bitcast.34, ...), custom_call_target="tpu_custom_call" | custom-call | flops 1207959552 | bytes 5505024 | tf_op jit(solution)/shard_map/pallas_call | solution.py:137
  111.0 2.7 %reshape.110 = bf16[128,2,2304]{2,1,0:T(2,128)(2,1)} reshape(bf16[384,1536]{1,0:T(8,128)(2,1)} %shard_map.187) | data formatting | bytes 2359296 | tf_op jit(solution)/shard_map/reshape | solution.py:275
  113.6 5.9 %all-to-all-start.3 = ((bf16[128,2,2304]{2,1,0:T(2,128)(2,1)}), bf16[128,2,2304]{2,1,0:T(2,128)(2,1)}, u32[]{:S(2)}, u32[]{:S(2)}) async-start(bf16[128,2,2304]{2,1,0:T(2,128)(2,1)} %reshape.110), calls=%async_computation.3 | async-start | bytes 2359296 | tf_op jit(solution)/shard_map/all_to_all | solution.py:274
  119.6 0.3 fusion.32
  119.9 20.0 %all-to-all-done.3 = bf16[128,2,2304]{2,1,0:T(2,128)(2,1)} async-done(((bf16[128,2,2304]{2,1,0:T(2,128)(2,1)}), bf16[128,2,2304]{2,1,0:T(2,128)(2,1)}, u32[]{:S(2)}, u32[]{:S(2)}) %all-to-all-start.3) | async-done | bytes 1179680 | tf_op jit(solution)/shard_map/all_to_all | solution.py:274
  140.0 4.0 %reshape.111 = bf16[4,32,3,1536]{3,2,1,0:T(4,128)(2,1)S(1)} reshape(bf16[128,2,2304]{2,1,0:T(2,128)(2,1)} %all-to-all-done.3) | data formatting | bytes 2359296 | tf_op jit(solution)/shard_map/reshape | solution.py:280
  144.0 1.1 reduce_sum.70
  145.3 0.9 multiply_reduce_fusion
  146.2 0.9 fusion.8
  (44 shorter events, 2.1 us)
Async XLA Ops:
  0.6 145.5 %copy-start = (bf16[1536,64]{0,1:T(8,128)(2,1)S(1)}, bf16[1536,64]{0,1:T(8,128)(2,1)}, u32[]{:S(2)}) copy-start(bf16[1536,64]{0,1:T(8,128)(2,1)} %param.35) | copy-start | bytes 589828
  0.6 2.6 %copy-start.1 = (bf16[32,3,1536]{2,0,1:T(8,128)(2,1)S(1)}, bf16[32,3,1536]{2,0,1:T(8,128)(2,1)}, u32[]{:S(2)}) copy-start(bf16[32,3,1536]{2,0,1:T(8,128)(2,1)} %param.18) | copy-start | bytes 884740
  3.6 1.5 %copy-start.5 = (f32[1536]{0:T(1024)S(1)}, f32[1536]{0:T(1024)}, u32[]{:S(2)}) copy-start(f32[1536]{0:T(1024)} %param.27) | copy-start | bytes 18436
  3.6 1.5 %copy-start.6 = (f32[1536]{0:T(1024)S(1)}, f32[1536]{0:T(1024)}, u32[]{:S(2)}) copy-start(f32[1536]{0:T(1024)} %param.26) | copy-start | bytes 18436
  71.7 3.6 %copy-start.4 = (f32[1536]{0:T(1024)S(1)}, f32[1536]{0:T(1024)}, u32[]{:S(2)}) copy-start(f32[1536]{0:T(1024)} %param.29) | copy-start | bytes 18436
  78.5 4.8 %copy-start.7 = (f32[384]{0:T(512)S(1)}, f32[384]{0:T(512)}, u32[]{:S(2)}) copy-start(f32[384]{0:T(512)} %param.31) | copy-start | bytes 4612
  78.5 25.5 %all-to-all-start.2 = ((bf16[128,2,2304]{2,1,0:T(2,128)(2,1)}), bf16[128,2,2304]{2,1,0:T(2,128)(2,1)S(1)}, u32[]{:S(2)}, u32[]{:S(2)}) async-start(bf16[128,2,2304]{2,1,0:T(2,128)(2,1)} %reshape.107), calls=%async_computation.2 | async-start | bytes 2359296 | tf_op jit(solution)/shard_map/all_to_all | solution.py:269
  113.6 5.9 %copy-start.2 = (f32[32,2,1536]{2,1,0:T(2,128)S(1)}, f32[32,2,1536]{2,1,0:T(2,128)}, u32[]{:S(2)}) copy-start(f32[32,2,1536]{2,1,0:T(2,128)} %param.23) | copy-start | bytes 1179652
  113.6 26.3 %all-to-all-start.3 = ((bf16[128,2,2304]{2,1,0:T(2,128)(2,1)}), bf16[128,2,2304]{2,1,0:T(2,128)(2,1)}, u32[]{:S(2)}, u32[]{:S(2)}) async-start(bf16[128,2,2304]{2,1,0:T(2,128)(2,1)} %reshape.110), calls=%async_computation.3 | async-start | bytes 2359296 | tf_op jit(solution)/shard_map/all_to_all | solution.py:274
  145.1 1.1 copy-start.3
  145.1 1.1 copy-start.8

commit v13 on v12

--- a/solution.py
+++ b/solution.py
@@ -239,7 +239,7 @@
     block_in = (layer_norm(stream) * (1.0 + block_scale) + block_shift).astype(jnp.bfloat16)
     packed = pack_projected(block_in, cell_map, w_qkv, self_q_gain, self_k_gain, head_count)
     arrived = lax.all_to_all(
-        packed.reshape(head_count * videos, per_video, 3 * group_width),
+        packed.reshape(head_count * videos, 2, per_video * 3 * group_width // 2),
         ("head", "tile"),
         split_axis=0,
         concat_axis=0,
@@ -247,7 +247,7 @@
     )
     own_mixture = attend_self(arrived.reshape(-1, 3 * group_width), group_width)
     returned = lax.all_to_all(
-        own_mixture.reshape(head_count * tile_count, per_video, group_width),
+        own_mixture.reshape(head_count * tile_count, 2, per_video * group_width // 2),
         ("head", "tile"),
         split_axis=0,
         concat_axis=0,
@@ -277,8 +277,12 @@
         split_axis=0,
         concat_axis=0,
         tiled=True,
-    ).reshape(head_count, videos, per_video, model_width)
-    returned_cross = jnp.sum(returned_partials.astype(jnp.float32), axis=0).astype(jnp.bfloat16)
+    ).reshape(head_count, videos, 2, per_video * model_width // 2)
+    returned_cross = (
+        jnp.sum(returned_partials.astype(jnp.float32), axis=0)
+        .astype(jnp.bfloat16)
+        .reshape(videos, per_video, model_width)
+    )
     after_cross = after_self + returned_cross.astype(jnp.float32)
     hidden_next = after_cross.astype(jnp.bfloat16)
     head_shift = head_modulation[:, 0][:, None, :]

time: 148 us -> 142 us (0.959)
  blocking collectives: 48.2 us -> 44.9 us
  local copies, waits for them, and re-layouts: 19.7 us -> 17.9 us
    reshape x2 -> x1, local copies, waits for them, and re-layouts: 5.11 us -> 1.35 us  [local(): own_mixture.reshape(head_count * tile_count, 2, per_video * group_width /...]
    all_to_all x2, blocking collectives: 48.2 us -> 44.9 us  [the longest x1 29.1 us: local(): lax.all_to_all(packed.reshape(head_count * videos, 2, per_video * 3 * gro...]
where the time goes in v13:
time: 142 us
  blocking collectives  44.9 us (32%)
  waiting for transfers between devices  39.8 us (28%)
  local copies, waits for them, and re-layouts  17.9 us (13%)
  Pallas kernels  16.4 us (12%)
  starting transfers between devices  9.48 us (7%)
  other arithmetic  7.53 us (5%)
  matrix products  4.24 us (3%)
  between operations  1.57 us (1%)
    all_to_all x1, blocking collectives, local(): lax.all_to_all(packed.reshape(head_count * videos, 2, per_video * 3 * gro...  29.1 us
    all_to_all x1, waiting for transfers between devices, local(): lax.all_to_all(partial.reshape(head_count * tile_count, 2, per_video * mo...  20.3 us
    all_to_all x1, waiting for transfers between devices, local(): lax.all_to_all(copies, ('head', 'tile'), split_axis=0, concat_axis=0, til...  19.5 us
    all_to_all x1, blocking collectives, local(): lax.all_to_all(own_mixture.reshape(head_count * tile_count, 2, per_video...  15.8 us
    pallas_call x1, Pallas kernels, pack_projected(): pl.pallas_call(_qkv_kernel, grid=(head_count,), in_specs=[pl.BlockSpec((t...  8.22 us
    pallas_call x1, Pallas kernels, cross_partial(): pl.pallas_call(_cross_kernel, in_specs=[pl.BlockSpec(memory_space=pltpu.S...  5.44 us
    all_to_all x1, starting transfers between devices, local(): lax.all_to_all(partial.reshape(head_count * tile_count, 2, per_video * mo...  4.75 us
    all_to_all x1, starting transfers between devices, local(): lax.all_to_all(copies, ('head', 'tile'), split_axis=0, concat_axis=0, til...  4.73 us
  transfers between devices with their start and end apart: 2, of which 2 were waited for; matrix products, arithmetic and copies ran while one was open for 1% of the time, Pallas kernels for 0%

profile of v13, /device:TPU:1, one launch (start us, length us, event | category | flops | bytes accessed | tf_op | source)
XLA Modules:
  0.0 141.7 jit_solution(3591362276394399779)
XLA Ops:
  0.7 0.8 fusion.24
  2.0 1.2 slice_bitcast_fusion.1
  4.1 1.0 reshape.106.x_ref
  5.2 0.6 pad_maximum_fusion.3.gain_ref
  5.9 0.3 fusion.29
  6.2 0.7 pad_maximum_fusion.1
  6.9 8.2 %shard_map.185 = bf16[4,96,1152]{2,1,0:T(8,128)(2,1)} custom-call(bf16[96,1536]{1,0:T(8,128)(2,1)} %reshape.106.x_ref, bf16[1536,4608]{1,0:T(8,128)(2,1)} %wv_ref.1, bf16[1536,4608]{1,0:T(8,128)(2,1)} %wv_ref.1, bf16[1536,4608]{1,0:T(8,128)(2,1)} %wv_ref.1, f32[96,128]{1,0:T(8,128)} %get-tuple-element.21.cos_ref, f32[96,128]{1,0:T(8,128)} %get-tuple-element.22.sin_ref, ...), custom_call_target="tpu_custom_call" | custom-call | flops 1358954496 | bytes 15925248 | tf_op jit(solution)/shard_map/pallas_call | solution.py:187
  15.1 3.1 %reshape_reshape.3 = bf16[128,2,1728]{2,1,0:T(2,128)(2,1)S(1)} reshape(bf16[4,96,1152]{2,1,0:T(8,128)(2,1)} %shard_map.185) | data formatting | bytes 1769472 | tf_op jit(solution)/shard_map/reshape;reshape | solution.py:242
  18.2 29.1 %all_to_all.20 = bf16[128,2,1728]{2,1,0:T(2,128)(2,1)S(1)} all-to-all(bf16[128,2,1728]{2,1,0:T(2,128)(2,1)S(1)} %reshape_reshape.3), channel_id=1, replica_groups=mesh['head'=4,'tile'=32] {'head','tile'}, dimensions={0} | all-to-all | bytes 1769472 | tf_op jit(solution)/shard_map/all_to_all | solution.py:241
  47.3 2.2 %reshape.107.x_ref = bf16[384,1152]{1,0:T(8,128)(2,1)} reshape(bf16[128,2,1728]{2,1,0:T(2,128)(2,1)S(1)} %all_to_all.20) | data formatting | bytes 1769472 | tf_op jit(solution)/shard_map/reshape | solution.py:248
  49.5 2.7 %shard_map.186 = bf16[384,384]{1,0:T(8,128)(2,1)} custom-call(bf16[384,1152]{1,0:T(8,128)(2,1)} %reshape.107.x_ref), custom_call_target="tpu_custom_call" | custom-call | flops 226492416 | bytes 1179648 | tf_op jit(solution)/shard_map/pallas_call | solution.py:91
  52.2 1.4 reshape.108
  53.5 15.8 %all_to_all.21 = bf16[128,2,576]{2,1,0:T(2,128)(2,1)S(1)} all-to-all(bf16[128,2,576]{2,1,0:T(2,128)(2,1)S(1)} %reshape.108), channel_id=1, replica_groups=mesh['head'=4,'tile'=32] {'head','tile'}, dimensions={0} | all-to-all | bytes 589824 | tf_op jit(solution)/shard_map/all_to_all | solution.py:249
  69.3 0.5 reshape.109
  69.8 0.3 copy.31
  70.2 3.3 %fusion.32 = (f32[32,3]{0,1:T(4,128)S(1)}, f32[32,3,1536]{2,0,1:T(8,128)S(1)}) fusion(bf16[32,3,1536]{2,0,1:T(8,128)(2,1)S(1)} %dot_general.8, bf16[1536,1536]{1,0:T(8,128)(2,1)} %param.28, f32[32,1536]{1,0:T(8,128)S(1)} %get-tuple-element.8, bf16[32,3,1536]{2,0,1:T(8,128)(2,1)S(1)} %copy-done.1), kind=kOutput, calls=%fused_computation.65 | convolution fusion | flops 453574560 | bytes 6095232 | tf_op jit(solution)/shard_map/dot_general | solution.py:261
  74.2 0.4 broadcast_in_dim.2
  74.6 2.4 %reshape.110 = bf16[128,2,2304]{2,1,0:T(2,128)(2,1)} reshape(bf16[4,32,3,1536]{3,2,1,0:T(4,128)(2,1)S(1)} %broadcast_in_dim.2) | data formatting | bytes 2359296 | tf_op jit(solution)/shard_map/reshape | solution.py:266
  77.1 4.7 %all-to-all-start.2 = ((bf16[128,2,2304]{2,1,0:T(2,128)(2,1)}), bf16[128,2,2304]{2,1,0:T(2,128)(2,1)S(1)}, u32[]{:S(2)}, u32[]{:S(2)}) async-start(bf16[128,2,2304]{2,1,0:T(2,128)(2,1)} %reshape.110), calls=%async_computation.2 | async-start | bytes 2359296 | tf_op jit(solution)/shard_map/all_to_all | solution.py:269
  81.8 0.6 reshape.112.gain_ref
  83.0 19.5 %all-to-all-done.2 = bf16[128,2,2304]{2,1,0:T(2,128)(2,1)S(1)} async-done(((bf16[128,2,2304]{2,1,0:T(2,128)(2,1)}), bf16[128,2,2304]{2,1,0:T(2,128)(2,1)S(1)}, u32[]{:S(2)}, u32[]{:S(2)}) %all-to-all-start.2) | async-done | bytes 1179680 | tf_op jit(solution)/shard_map/all_to_all | solution.py:269
  102.5 1.6 %reshape.111.x_ref = bf16[384,1536]{1,0:T(8,128)(2,1)} reshape(bf16[128,2,2304]{2,1,0:T(2,128)(2,1)S(1)} %all-to-all-done.2) | data formatting | bytes 2359296 | tf_op jit(solution)/shard_map/reshape | solution.py:270
  104.1 5.4 %shard_map.187 = bf16[384,1536]{1,0:T(8,128)(2,1)} custom-call(s32[1]{0:T(128)S(6)} %copy.44.length_ref, bf16[384,1536]{1,0:T(8,128)(2,1)} %reshape.111.x_ref, bf16[1536,384]{1,0:T(8,128)(2,1)} %wq_ref.3, f32[1,384]{1,0:T(1,128)} %reshape.112.gain_ref, bf16[512,384]{1,0:T(8,128)(2,1)} %bitcast.31, bf16[512,384]{1,0:T(8,128)(2,1)} %bitcast.32, ...), custom_call_target="tpu_custom_call" | custom-call | flops 1207959552 | bytes 5505024 | tf_op jit(solution)/shard_map/pallas_call | solution.py:137
  109.5 2.7 %reshape.113 = bf16[128,2,2304]{2,1,0:T(2,128)(2,1)} reshape(bf16[384,1536]{1,0:T(8,128)(2,1)} %shard_map.187) | data formatting | bytes 2359296 | tf_op jit(solution)/shard_map/reshape | solution.py:275
  112.2 4.8 %all-to-all-start.3 = ((bf16[128,2,2304]{2,1,0:T(2,128)(2,1)}), bf16[128,2,2304]{2,1,0:T(2,128)(2,1)S(1)}, u32[]{:S(2)}, u32[]{:S(2)}) async-start(bf16[128,2,2304]{2,1,0:T(2,128)(2,1)} %reshape.113), calls=%async_computation.3 | async-start | bytes 2359296 | tf_op jit(solution)/shard_map/all_to_all | solution.py:274
  117.0 0.3 fusion.31
  117.3 20.3 %all-to-all-done.3 = bf16[128,2,2304]{2,1,0:T(2,128)(2,1)S(1)} async-done(((bf16[128,2,2304]{2,1,0:T(2,128)(2,1)}), bf16[128,2,2304]{2,1,0:T(2,128)(2,1)S(1)}, u32[]{:S(2)}, u32[]{:S(2)}) %all-to-all-start.3) | async-done | bytes 1179680 | tf_op jit(solution)/shard_map/all_to_all | solution.py:274
  137.7 1.6 %reduce_sum.70 = bf16[32,2,2304]{2,1,0:T(2,128)(2,1)S(1)} reduce(bf16[4,32,2,2304]{3,2,1,0:T(2,128)(2,1)S(1)} %bitcast.29, bf16[]{:T(256)} %constant.66.clone.1), dimensions={0}, to_apply=%region_4.5 | reduce | flops 442368 | bytes 1474562 | tf_op jit(solution)/shard_map/reduce_sum | solution.py:282
  139.3 0.3 reshape.115
  139.6 0.3 fusion.28
  139.9 0.9 multiply_reduce_fusion
  140.8 0.9 fusion.8
  (45 shorter events, 2.5 us)
Async XLA Ops:
  0.6 140.2 %copy-start = (bf16[1536,64]{0,1:T(8,128)(2,1)S(1)}, bf16[1536,64]{0,1:T(8,128)(2,1)}, u32[]{:S(2)}) copy-start(bf16[1536,64]{0,1:T(8,128)(2,1)} %param.35) | copy-start | bytes 589828
  0.6 2.6 %copy-start.1 = (bf16[32,3,1536]{2,0,1:T(8,128)(2,1)S(1)}, bf16[32,3,1536]{2,0,1:T(8,128)(2,1)}, u32[]{:S(2)}) copy-start(bf16[32,3,1536]{2,0,1:T(8,128)(2,1)} %param.18) | copy-start | bytes 884740
  3.6 1.5 %copy-start.5 = (f32[1536]{0:T(1024)S(1)}, f32[1536]{0:T(1024)}, u32[]{:S(2)}) copy-start(f32[1536]{0:T(1024)} %param.27) | copy-start | bytes 18436
  3.6 1.5 %copy-start.6 = (f32[1536]{0:T(1024)S(1)}, f32[1536]{0:T(1024)}, u32[]{:S(2)}) copy-start(f32[1536]{0:T(1024)} %param.26) | copy-start | bytes 18436
  70.2 3.6 %copy-start.4 = (f32[1536]{0:T(1024)S(1)}, f32[1536]{0:T(1024)}, u32[]{:S(2)}) copy-start(f32[1536]{0:T(1024)} %param.29) | copy-start | bytes 18436
  77.1 4.7 %copy-start.7 = (f32[384]{0:T(512)S(1)}, f32[384]{0:T(512)}, u32[]{:S(2)}) copy-start(f32[384]{0:T(512)} %param.31) | copy-start | bytes 4612
  77.1 25.4 %all-to-all-start.2 = ((bf16[128,2,2304]{2,1,0:T(2,128)(2,1)}), bf16[128,2,2304]{2,1,0:T(2,128)(2,1)S(1)}, u32[]{:S(2)}, u32[]{:S(2)}) async-start(bf16[128,2,2304]{2,1,0:T(2,128)(2,1)} %reshape.110), calls=%async_computation.2 | async-start | bytes 2359296 | tf_op jit(solution)/shard_map/all_to_all | solution.py:269
  112.2 4.8 %copy-start.2 = (f32[32,2,1536]{2,1,0:T(2,128)S(1)}, f32[32,2,1536]{2,1,0:T(2,128)}, u32[]{:S(2)}) copy-start(f32[32,2,1536]{2,1,0:T(2,128)} %param.23) | copy-start | bytes 1179652
  112.2 25.5 %all-to-all-start.3 = ((bf16[128,2,2304]{2,1,0:T(2,128)(2,1)}), bf16[128,2,2304]{2,1,0:T(2,128)(2,1)S(1)}, u32[]{:S(2)}, u32[]{:S(2)}) async-start(bf16[128,2,2304]{2,1,0:T(2,128)(2,1)} %reshape.113), calls=%async_computation.3 | async-start | bytes 2359296 | tf_op jit(solution)/shard_map/all_to_all | solution.py:274
  139.6 1.2 copy-start.3
  139.6 1.2 copy-start.8

commit v14 on v13

--- a/solution.py
+++ b/solution.py
@@ -263,7 +263,8 @@
     )
     after_self = stream + block_gate * self_update
     cross_in = (layer_norm(after_self) * cross_gain).astype(jnp.bfloat16)
-    copies = jnp.broadcast_to(cross_in[None], (head_count,) + cross_in.shape).reshape(
+    cross_rows = cross_in.reshape(videos, 2, per_video * model_width // 2)
+    copies = jnp.broadcast_to(cross_rows[None], (head_count,) + cross_rows.shape).reshape(
         head_count * videos, 2, per_video * model_width // 2
     )
     owner_cross = lax.all_to_all(copies, ("head", "tile"), split_axis=0, concat_axis=0, tiled=True)

time: 142 us -> 141 us (level)
    reshape x1 -> x0, local copies, waits for them, and re-layouts: 2.45 us -> none  [local(): jnp.broadcast_to(cross_in[None], (head_count,) + cross_in.shape)]
    broadcast_in_dim x1 -> x2, local copies, waits for them, and re-layouts: 0.41 us -> 1.97 us  [local(): jnp.broadcast_to(cross_rows[None], (head_count,) + cross_rows.shape)]
where the time goes in v14:
time: 141 us
  blocking collectives  44.9 us (32%)
  waiting for transfers between devices  39.8 us (28%)
  local copies, waits for them, and re-layouts  17 us (12%)
  Pallas kernels  16.4 us (12%)
  starting transfers between devices  9.65 us (7%)
  other arithmetic  7.53 us (5%)
  matrix products  4.24 us (3%)
  between operations  1.57 us (1%)
    all_to_all x1, blocking collectives, local(): lax.all_to_all(packed.reshape(head_count * videos, 2, per_video * 3 * gro...  29.1 us
    all_to_all x1, waiting for transfers between devices, local(): lax.all_to_all(partial.reshape(head_count * tile_count, 2, per_video * mo...  20.3 us
    all_to_all x1, waiting for transfers between devices, local(): lax.all_to_all(copies, ('head', 'tile'), split_axis=0, concat_axis=0, til...  19.5 us
    all_to_all x1, blocking collectives, local(): lax.all_to_all(own_mixture.reshape(head_count * tile_count, 2, per_video...  15.8 us
    pallas_call x1, Pallas kernels, pack_projected(): pl.pallas_call(_qkv_kernel, grid=(head_count,), in_specs=[pl.BlockSpec((t...  8.22 us
    pallas_call x1, Pallas kernels, cross_partial(): pl.pallas_call(_cross_kernel, in_specs=[pl.BlockSpec(memory_space=pltpu.S...  5.44 us
    all_to_all x1, starting transfers between devices, local(): lax.all_to_all(copies, ('head', 'tile'), split_axis=0, concat_axis=0, til...  4.9 us
    all_to_all x1, starting transfers between devices, local(): lax.all_to_all(partial.reshape(head_count * tile_count, 2, per_video * mo...  4.75 us
  transfers between devices with their start and end apart: 2, of which 2 were waited for; matrix products, arithmetic and copies ran while one was open for 1% of the time, Pallas kernels for 0%

profile of v14, /device:TPU:1, one launch (start us, length us, event | category | flops | bytes accessed | tf_op | source)
XLA Modules:
  0.0 141.0 jit_solution(17706797085601383203)
XLA Ops:
  0.7 0.8 fusion.24
  2.0 1.2 slice_bitcast_fusion.1
  4.1 1.0 reshape.106.x_ref
  5.2 0.6 pad_maximum_fusion.3.gain_ref
  5.9 0.3 fusion.29
  6.2 0.7 pad_maximum_fusion.1
  6.9 8.2 %shard_map.185 = bf16[4,96,1152]{2,1,0:T(8,128)(2,1)} custom-call(bf16[96,1536]{1,0:T(8,128)(2,1)} %reshape.106.x_ref, bf16[1536,4608]{1,0:T(8,128)(2,1)} %wv_ref.1, bf16[1536,4608]{1,0:T(8,128)(2,1)} %wv_ref.1, bf16[1536,4608]{1,0:T(8,128)(2,1)} %wv_ref.1, f32[96,128]{1,0:T(8,128)} %get-tuple-element.21.cos_ref, f32[96,128]{1,0:T(8,128)} %get-tuple-element.22.sin_ref, ...), custom_call_target="tpu_custom_call" | custom-call | flops 1358954496 | bytes 15925248 | tf_op jit(solution)/shard_map/pallas_call | solution.py:187
  15.1 3.1 %reshape_reshape.3 = bf16[128,2,1728]{2,1,0:T(2,128)(2,1)S(1)} reshape(bf16[4,96,1152]{2,1,0:T(8,128)(2,1)} %shard_map.185) | data formatting | bytes 1769472 | tf_op jit(solution)/shard_map/reshape;reshape | solution.py:242
  18.2 29.1 %all_to_all.20 = bf16[128,2,1728]{2,1,0:T(2,128)(2,1)S(1)} all-to-all(bf16[128,2,1728]{2,1,0:T(2,128)(2,1)S(1)} %reshape_reshape.3), channel_id=1, replica_groups=mesh['head'=4,'tile'=32] {'head','tile'}, dimensions={0} | all-to-all | bytes 1769472 | tf_op jit(solution)/shard_map/all_to_all | solution.py:241
  47.3 2.2 %reshape.107.x_ref = bf16[384,1152]{1,0:T(8,128)(2,1)} reshape(bf16[128,2,1728]{2,1,0:T(2,128)(2,1)S(1)} %all_to_all.20) | data formatting | bytes 1769472 | tf_op jit(solution)/shard_map/reshape | solution.py:248
  49.5 2.7 %shard_map.186 = bf16[384,384]{1,0:T(8,128)(2,1)} custom-call(bf16[384,1152]{1,0:T(8,128)(2,1)} %reshape.107.x_ref), custom_call_target="tpu_custom_call" | custom-call | flops 226492416 | bytes 1179648 | tf_op jit(solution)/shard_map/pallas_call | solution.py:91
  52.2 1.4 reshape.108
  53.5 15.8 %all_to_all.21 = bf16[128,2,576]{2,1,0:T(2,128)(2,1)S(1)} all-to-all(bf16[128,2,576]{2,1,0:T(2,128)(2,1)S(1)} %reshape.108), channel_id=1, replica_groups=mesh['head'=4,'tile'=32] {'head','tile'}, dimensions={0} | all-to-all | bytes 589824 | tf_op jit(solution)/shard_map/all_to_all | solution.py:249
  69.3 0.5 reshape.109
  69.8 0.3 copy.30
  70.2 3.3 %fusion.32 = (f32[32,3]{0,1:T(4,128)S(1)}, f32[32,3,1536]{2,0,1:T(8,128)S(1)}) fusion(bf16[32,3,1536]{2,0,1:T(8,128)(2,1)S(1)} %dot_general.8, bf16[1536,1536]{1,0:T(8,128)(2,1)} %param.28, f32[32,1536]{1,0:T(8,128)S(1)} %get-tuple-element.8, bf16[32,3,1536]{2,0,1:T(8,128)(2,1)S(1)} %copy-done.1), kind=kOutput, calls=%fused_computation.65 | convolution fusion | flops 453574560 | bytes 6095232 | tf_op jit(solution)/shard_map/dot_general | solution.py:261
  74.2 0.3 broadcast_in_dim.4
  74.5 1.6 %broadcast_in_dim.5 = bf16[4,32,2,2304]{3,2,1,0:T(2,128)(2,1)} broadcast(bf16[32,2,2304]{2,1,0:T(2,128)(2,1)S(1)} %broadcast_in_dim.4), dimensions={1,2,3} | broadcast | bytes 1474560 | tf_op jit(solution)/shard_map/broadcast_in_dim | solution.py:267
  76.2 4.9 %all-to-all-start.2 = ((bf16[128,2,2304]{2,1,0:T(2,128)(2,1)}), bf16[128,2,2304]{2,1,0:T(2,128)(2,1)S(1)}, u32[]{:S(2)}, u32[]{:S(2)}) async-start(bf16[128,2,2304]{2,1,0:T(2,128)(2,1)} %bitcast.5), calls=%async_computation.2 | async-start | bytes 2359296 | tf_op jit(solution)/shard_map/all_to_all | solution.py:270
  81.1 0.6 reshape.112.gain_ref
  82.3 19.5 %all-to-all-done.2 = bf16[128,2,2304]{2,1,0:T(2,128)(2,1)S(1)} async-done(((bf16[128,2,2304]{2,1,0:T(2,128)(2,1)}), bf16[128,2,2304]{2,1,0:T(2,128)(2,1)S(1)}, u32[]{:S(2)}, u32[]{:S(2)}) %all-to-all-start.2) | async-done | bytes 1179680 | tf_op jit(solution)/shard_map/all_to_all | solution.py:270
  101.8 1.6 %reshape.111.x_ref = bf16[384,1536]{1,0:T(8,128)(2,1)} reshape(bf16[128,2,2304]{2,1,0:T(2,128)(2,1)S(1)} %all-to-all-done.2) | data formatting | bytes 2359296 | tf_op jit(solution)/shard_map/reshape | solution.py:271
  103.4 5.4 %shard_map.187 = bf16[384,1536]{1,0:T(8,128)(2,1)} custom-call(s32[1]{0:T(128)S(6)} %copy.43.length_ref, bf16[384,1536]{1,0:T(8,128)(2,1)} %reshape.111.x_ref, bf16[1536,384]{1,0:T(8,128)(2,1)} %wq_ref.3, f32[1,384]{1,0:T(1,128)} %reshape.112.gain_ref, bf16[512,384]{1,0:T(8,128)(2,1)} %bitcast.32, bf16[512,384]{1,0:T(8,128)(2,1)} %bitcast.33, ...), custom_call_target="tpu_custom_call" | custom-call | flops 1207959552 | bytes 5505024 | tf_op jit(solution)/shard_map/pallas_call | solution.py:137
  108.8 2.7 %reshape.113 = bf16[128,2,2304]{2,1,0:T(2,128)(2,1)} reshape(bf16[384,1536]{1,0:T(8,128)(2,1)} %shard_map.187) | data formatting | bytes 2359296 | tf_op jit(solution)/shard_map/reshape | solution.py:276
  111.5 4.7 %all-to-all-start.3 = ((bf16[128,2,2304]{2,1,0:T(2,128)(2,1)}), bf16[128,2,2304]{2,1,0:T(2,128)(2,1)S(1)}, u32[]{:S(2)}, u32[]{:S(2)}) async-start(bf16[128,2,2304]{2,1,0:T(2,128)(2,1)} %reshape.113), calls=%async_computation.3 | async-start | bytes 2359296 | tf_op jit(solution)/shard_map/all_to_all | solution.py:275
  116.2 0.3 fusion.31
  116.6 20.3 %all-to-all-done.3 = bf16[128,2,2304]{2,1,0:T(2,128)(2,1)S(1)} async-done(((bf16[128,2,2304]{2,1,0:T(2,128)(2,1)}), bf16[128,2,2304]{2,1,0:T(2,128)(2,1)S(1)}, u32[]{:S(2)}, u32[]{:S(2)}) %all-to-all-start.3) | async-done | bytes 1179680 | tf_op jit(solution)/shard_map/all_to_all | solution.py:275
  136.9 1.6 %reduce_sum.70 = bf16[32,2,2304]{2,1,0:T(2,128)(2,1)S(1)} reduce(bf16[4,32,2,2304]{3,2,1,0:T(2,128)(2,1)S(1)} %bitcast.30, bf16[]{:T(256)} %constant.66.clone.1), dimensions={0}, to_apply=%region_4.5 | reduce | flops 442368 | bytes 1474562 | tf_op jit(solution)/shard_map/reduce_sum | solution.py:283
  138.6 0.3 reshape.115
  138.9 0.3 fusion.28
  139.2 0.9 multiply_reduce_fusion
  140.1 0.9 fusion.8
  (45 shorter events, 2.5 us)
Async XLA Ops:
  0.6 139.4 %copy-start = (bf16[1536,64]{0,1:T(8,128)(2,1)S(1)}, bf16[1536,64]{0,1:T(8,128)(2,1)}, u32[]{:S(2)}) copy-start(bf16[1536,64]{0,1:T(8,128)(2,1)} %param.35) | copy-start | bytes 589828
  0.6 2.6 %copy-start.1 = (bf16[32,3,1536]{2,0,1:T(8,128)(2,1)S(1)}, bf16[32,3,1536]{2,0,1:T(8,128)(2,1)}, u32[]{:S(2)}) copy-start(bf16[32,3,1536]{2,0,1:T(8,128)(2,1)} %param.18) | copy-start | bytes 884740
  3.6 1.5 %copy-start.5 = (f32[1536]{0:T(1024)S(1)}, f32[1536]{0:T(1024)}, u32[]{:S(2)}) copy-start(f32[1536]{0:T(1024)} %param.27) | copy-start | bytes 18436
  3.6 1.5 %copy-start.6 = (f32[1536]{0:T(1024)S(1)}, f32[1536]{0:T(1024)}, u32[]{:S(2)}) copy-start(f32[1536]{0:T(1024)} %param.26) | copy-start | bytes 18436
  70.2 3.6 %copy-start.4 = (f32[1536]{0:T(1024)S(1)}, f32[1536]{0:T(1024)}, u32[]{:S(2)}) copy-start(f32[1536]{0:T(1024)} %param.29) | copy-start | bytes 18436
  76.2 4.9 %copy-start.7 = (f32[384]{0:T(512)S(1)}, f32[384]{0:T(512)}, u32[]{:S(2)}) copy-start(f32[384]{0:T(512)} %param.31) | copy-start | bytes 4612
  76.2 25.6 %all-to-all-start.2 = ((bf16[128,2,2304]{2,1,0:T(2,128)(2,1)}), bf16[128,2,2304]{2,1,0:T(2,128)(2,1)S(1)}, u32[]{:S(2)}, u32[]{:S(2)}) async-start(bf16[128,2,2304]{2,1,0:T(2,128)(2,1)} %bitcast.5), calls=%async_computation.2 | async-start | bytes 2359296 | tf_op jit(solution)/shard_map/all_to_all | solution.py:270
  111.5 4.8 %copy-start.2 = (f32[32,2,1536]{2,1,0:T(2,128)S(1)}, f32[32,2,1536]{2,1,0:T(2,128)}, u32[]{:S(2)}) copy-start(f32[32,2,1536]{2,1,0:T(2,128)} %param.23) | copy-start | bytes 1179652
  111.5 25.5 %all-to-all-start.3 = ((bf16[128,2,2304]{2,1,0:T(2,128)(2,1)}), bf16[128,2,2304]{2,1,0:T(2,128)(2,1)S(1)}, u32[]{:S(2)}, u32[]{:S(2)}) async-start(bf16[128,2,2304]{2,1,0:T(2,128)(2,1)} %reshape.113), calls=%async_computation.3 | async-start | bytes 2359296 | tf_op jit(solution)/shard_map/all_to_all | solution.py:275
  138.9 1.2 copy-start.3
  138.9 1.2 copy-start.8

commit v15 on v14

--- a/solution.py
+++ b/solution.py
@@ -99,13 +99,26 @@
     )(arrived)
 
 
-def _cross_kernel(length_ref, x_ref, wq_ref, gain_ref, keys_ref, values_ref, wo_ref, o_ref, mixed_ref):
+def _cross_kernel(
+    length_ref, x_ref, wq_ref, gain_ref, keys_hbm, values_hbm, wo_hbm, o_ref,
+    mixed_ref, keys_ref, values_ref, wo_ref, copy_sems,
+):
     factor = 1.0 / math.sqrt(HEAD_DIM)
     group_width = wq_ref.shape[1]
     text = keys_ref.shape[0]
+    copies = [
+        pltpu.make_async_copy(source, target, copy_sems.at[index])
+        for index, (source, target) in enumerate(
+            ((keys_hbm, keys_ref), (values_hbm, values_ref), (wo_hbm, wo_ref))
+        )
+    ]
+    for copy in copies:
+        copy.start()
     projected = jnp.dot(x_ref[...], wq_ref[...], preferred_element_type=jnp.float32)
     gains = gain_ref[...]
     live = (lax.broadcasted_iota(jnp.int32, (1, text), 1) < length_ref[0]).astype(jnp.float32)
+    copies[0].wait()
+    copies[1].wait()
     for head in range(group_width // HEAD_DIM):
         lanes = slice(head * HEAD_DIM, (head + 1) * HEAD_DIM)
         piece = projected[:, lanes]
@@ -124,6 +137,7 @@
             weights.astype(jnp.bfloat16), values_ref[:, lanes], preferred_element_type=jnp.float32
         )
         mixed_ref[:, lanes] = (mixture / totals).astype(mixed_ref.dtype)
+    copies[2].wait()
     o_ref[...] = jnp.dot(mixed_ref[...], wo_ref[...], preferred_element_type=jnp.float32).astype(
         o_ref.dtype
     )
@@ -134,12 +148,19 @@
     group_width = cross_wq.shape[1]
     text = keys_own.shape[0]
     vmem = pl.BlockSpec(memory_space=pltpu.VMEM)
+    hbm = pl.BlockSpec(memory_space=pl.ANY)
     return pl.pallas_call(
         _cross_kernel,
-        in_specs=[pl.BlockSpec(memory_space=pltpu.SMEM)] + [vmem] * 6,
+        in_specs=[pl.BlockSpec(memory_space=pltpu.SMEM), vmem, vmem, vmem, hbm, hbm, hbm],
         out_specs=vmem,
         out_shape=jax.ShapeDtypeStruct((token_total, model_width), jnp.bfloat16),
-        scratch_shapes=[pltpu.VMEM((token_total, group_width), jnp.bfloat16)],
+        scratch_shapes=[
+            pltpu.VMEM((token_total, group_width), jnp.bfloat16),
+            pltpu.VMEM((text, group_width), jnp.bfloat16),
+            pltpu.VMEM((text, group_width), jnp.bfloat16),
+            pltpu.VMEM((group_width, model_width), jnp.bfloat16),
+            pltpu.SemaphoreType.DMA((3,)),
+        ],
         cost_estimate=pl.CostEstimate(
             flops=4 * token_total * model_width * group_width + 4 * token_total * text * group_width,
             bytes_accessed=4 * model_width * group_width + 4 * text * group_width

time: 141 us -> 142 us (level)
  no operation moved by 1% of the time
where the time goes in v15:
time: 142 us; the launch traced here: 141 us
  blocking collectives  44.9 us (32%)
  waiting for transfers between devices  39.8 us (28%)
  local copies, waits for them, and re-layouts  17 us (12%)
  Pallas kernels  16.5 us (12%)
  starting transfers between devices  9.66 us (7%)
  other arithmetic  7.53 us (5%)
  matrix products  4.24 us (3%)
  between operations  1.58 us (1%)
    all_to_all x1, blocking collectives, local(): lax.all_to_all(packed.reshape(head_count * videos, 2, per_video * 3 * gro...  29.1 us
    all_to_all x1, waiting for transfers between devices, local(): lax.all_to_all(partial.reshape(head_count * tile_count, 2, per_video * mo...  20.3 us
    all_to_all x1, waiting for transfers between devices, local(): lax.all_to_all(copies, ('head', 'tile'), split_axis=0, concat_axis=0, til...  19.5 us
    all_to_all x1, blocking collectives, local(): lax.all_to_all(own_mixture.reshape(head_count * tile_count, 2, per_video...  15.8 us
    pallas_call x1, Pallas kernels, pack_projected(): pl.pallas_call(_qkv_kernel, grid=(head_count,), in_specs=[pl.BlockSpec((t...  8.22 us
    pallas_call x1, Pallas kernels, cross_partial(): pl.pallas_call(_cross_kernel, in_specs=[pl.BlockSpec(memory_space=pltpu.S...  5.6 us
    all_to_all x1, starting transfers between devices, local(): lax.all_to_all(copies, ('head', 'tile'), split_axis=0, concat_axis=0, til...  4.9 us
    all_to_all x1, starting transfers between devices, local(): lax.all_to_all(partial.reshape(head_count * tile_count, 2, per_video * mo...  4.75 us
  transfers between devices with their start and end apart: 2, of which 2 were waited for; matrix products, arithmetic and copies ran while one was open for 1% of the time, Pallas kernels for 0%

profile of v15, /device:TPU:1, one launch (start us, length us, event | category | flops | bytes accessed | tf_op | source)
XLA Modules:
  0.0 141.2 jit_solution(11585766161623087034)
XLA Ops:
  0.7 0.8 fusion.24
  2.0 1.2 slice_bitcast_fusion.1
  4.1 1.0 reshape.106.x_ref
  5.2 0.6 pad_maximum_fusion.3.gain_ref
  5.9 0.3 fusion.29
  6.2 0.7 pad_maximum_fusion.1
  6.9 8.2 %shard_map.185 = bf16[4,96,1152]{2,1,0:T(8,128)(2,1)} custom-call(bf16[96,1536]{1,0:T(8,128)(2,1)} %reshape.106.x_ref, bf16[1536,4608]{1,0:T(8,128)(2,1)} %wv_ref.1, bf16[1536,4608]{1,0:T(8,128)(2,1)} %wv_ref.1, bf16[1536,4608]{1,0:T(8,128)(2,1)} %wv_ref.1, f32[96,128]{1,0:T(8,128)} %get-tuple-element.21.cos_ref, f32[96,128]{1,0:T(8,128)} %get-tuple-element.22.sin_ref, ...), custom_call_target="tpu_custom_call" | custom-call | flops 1358954496 | bytes 15925248 | tf_op jit(solution)/shard_map/pallas_call | solution.py:208
  15.1 3.1 %reshape_reshape.3 = bf16[128,2,1728]{2,1,0:T(2,128)(2,1)S(1)} reshape(bf16[4,96,1152]{2,1,0:T(8,128)(2,1)} %shard_map.185) | data formatting | bytes 1769472 | tf_op jit(solution)/shard_map/reshape;reshape | solution.py:263
  18.2 29.1 %all_to_all.20 = bf16[128,2,1728]{2,1,0:T(2,128)(2,1)S(1)} all-to-all(bf16[128,2,1728]{2,1,0:T(2,128)(2,1)S(1)} %reshape_reshape.3), channel_id=1, replica_groups=mesh['head'=4,'tile'=32] {'head','tile'}, dimensions={0} | all-to-all | bytes 1769472 | tf_op jit(solution)/shard_map/all_to_all | solution.py:262
  47.3 2.2 %reshape.107.x_ref = bf16[384,1152]{1,0:T(8,128)(2,1)} reshape(bf16[128,2,1728]{2,1,0:T(2,128)(2,1)S(1)} %all_to_all.20) | data formatting | bytes 1769472 | tf_op jit(solution)/shard_map/reshape | solution.py:269
  49.5 2.7 %shard_map.186 = bf16[384,384]{1,0:T(8,128)(2,1)} custom-call(bf16[384,1152]{1,0:T(8,128)(2,1)} %reshape.107.x_ref), custom_call_target="tpu_custom_call" | custom-call | flops 226492416 | bytes 1179648 | tf_op jit(solution)/shard_map/pallas_call | solution.py:91
  52.2 1.4 reshape.108
  53.5 15.8 %all_to_all.21 = bf16[128,2,576]{2,1,0:T(2,128)(2,1)S(1)} all-to-all(bf16[128,2,576]{2,1,0:T(2,128)(2,1)S(1)} %reshape.108), channel_id=1, replica_groups=mesh['head'=4,'tile'=32] {'head','tile'}, dimensions={0} | all-to-all | bytes 589824 | tf_op jit(solution)/shard_map/all_to_all | solution.py:270
  69.3 0.5 reshape.109
  69.8 0.3 copy.30
  70.2 3.3 %fusion.32 = (f32[32,3]{0,1:T(4,128)S(1)}, f32[32,3,1536]{2,0,1:T(8,128)S(1)}) fusion(bf16[32,3,1536]{2,0,1:T(8,128)(2,1)S(1)} %dot_general.8, bf16[1536,1536]{1,0:T(8,128)(2,1)} %param.28, f32[32,1536]{1,0:T(8,128)S(1)} %get-tuple-element.8, bf16[32,3,1536]{2,0,1:T(8,128)(2,1)S(1)} %copy-done.1), kind=kOutput, calls=%fused_computation.65 | convolution fusion | flops 453574560 | bytes 6095232 | tf_op jit(solution)/shard_map/dot_general | solution.py:282
  74.2 0.3 broadcast_in_dim.4
  74.5 1.6 %broadcast_in_dim.5 = bf16[4,32,2,2304]{3,2,1,0:T(2,128)(2,1)} broadcast(bf16[32,2,2304]{2,1,0:T(2,128)(2,1)S(1)} %broadcast_in_dim.4), dimensions={1,2,3} | broadcast | bytes 1474560 | tf_op jit(solution)/shard_map/broadcast_in_dim | solution.py:288
  76.2 4.9 %all-to-all-start.2 = ((bf16[128,2,2304]{2,1,0:T(2,128)(2,1)}), bf16[128,2,2304]{2,1,0:T(2,128)(2,1)S(1)}, u32[]{:S(2)}, u32[]{:S(2)}) async-start(bf16[128,2,2304]{2,1,0:T(2,128)(2,1)} %bitcast.5), calls=%async_computation.2 | async-start | bytes 2359296 | tf_op jit(solution)/shard_map/all_to_all | solution.py:291
  81.1 0.6 reshape.112.gain_ref
  82.3 19.5 %all-to-all-done.2 = bf16[128,2,2304]{2,1,0:T(2,128)(2,1)S(1)} async-done(((bf16[128,2,2304]{2,1,0:T(2,128)(2,1)}), bf16[128,2,2304]{2,1,0:T(2,128)(2,1)S(1)}, u32[]{:S(2)}, u32[]{:S(2)}) %all-to-all-start.2) | async-done | bytes 1179680 | tf_op jit(solution)/shard_map/all_to_all | solution.py:291
  101.8 1.6 %reshape.111.x_ref = bf16[384,1536]{1,0:T(8,128)(2,1)} reshape(bf16[128,2,2304]{2,1,0:T(2,128)(2,1)S(1)} %all-to-all-done.2) | data formatting | bytes 2359296 | tf_op jit(solution)/shard_map/reshape | solution.py:292
  103.4 5.6 %shard_map.187 = bf16[384,1536]{1,0:T(8,128)(2,1)} custom-call(s32[1]{0:T(128)S(6)} %copy.43.length_ref, bf16[384,1536]{1,0:T(8,128)(2,1)} %reshape.111.x_ref, bf16[1536,384]{1,0:T(8,128)(2,1)} %wq_ref.3, f32[1,384]{1,0:T(1,128)} %reshape.112.gain_ref, bf16[512,384]{1,0:T(8,128)(2,1)} %bitcast.32, bf16[512,384]{1,0:T(8,128)(2,1)} %bitcast.33, ...), custom_call_target="tpu_custom_call" | custom-call | flops 1207959552 | bytes 5505024 | tf_op jit(solution)/shard_map/pallas_call | solution.py:152
  109.0 2.7 %reshape.113 = bf16[128,2,2304]{2,1,0:T(2,128)(2,1)} reshape(bf16[384,1536]{1,0:T(8,128)(2,1)} %shard_map.187) | data formatting | bytes 2359296 | tf_op jit(solution)/shard_map/reshape | solution.py:297
  111.7 4.8 %all-to-all-start.3 = ((bf16[128,2,2304]{2,1,0:T(2,128)(2,1)}), bf16[128,2,2304]{2,1,0:T(2,128)(2,1)S(1)}, u32[]{:S(2)}, u32[]{:S(2)}) async-start(bf16[128,2,2304]{2,1,0:T(2,128)(2,1)} %reshape.113), calls=%async_computation.3 | async-start | bytes 2359296 | tf_op jit(solution)/shard_map/all_to_all | solution.py:296
  116.4 0.3 fusion.31
  116.8 20.3 %all-to-all-done.3 = bf16[128,2,2304]{2,1,0:T(2,128)(2,1)S(1)} async-done(((bf16[128,2,2304]{2,1,0:T(2,128)(2,1)}), bf16[128,2,2304]{2,1,0:T(2,128)(2,1)S(1)}, u32[]{:S(2)}, u32[]{:S(2)}) %all-to-all-start.3) | async-done | bytes 1179680 | tf_op jit(solution)/shard_map/all_to_all | solution.py:296
  137.1 1.6 %reduce_sum.70 = bf16[32,2,2304]{2,1,0:T(2,128)(2,1)S(1)} reduce(bf16[4,32,2,2304]{3,2,1,0:T(2,128)(2,1)S(1)} %bitcast.30, bf16[]{:T(256)} %constant.66.clone.1), dimensions={0}, to_apply=%region_4.5 | reduce | flops 442368 | bytes 1474562 | tf_op jit(solution)/shard_map/reduce_sum | solution.py:304
  138.7 0.3 reshape.115
  139.1 0.3 fusion.28
  139.4 0.9 multiply_reduce_fusion
  140.3 0.9 fusion.8
  (45 shorter events, 2.5 us)
Async XLA Ops:
  0.6 139.6 %copy-start = (bf16[1536,64]{0,1:T(8,128)(2,1)S(1)}, bf16[1536,64]{0,1:T(8,128)(2,1)}, u32[]{:S(2)}) copy-start(bf16[1536,64]{0,1:T(8,128)(2,1)} %param.35) | copy-start | bytes 589828
  0.6 2.6 %copy-start.1 = (bf16[32,3,1536]{2,0,1:T(8,128)(2,1)S(1)}, bf16[32,3,1536]{2,0,1:T(8,128)(2,1)}, u32[]{:S(2)}) copy-start(bf16[32,3,1536]{2,0,1:T(8,128)(2,1)} %param.18) | copy-start | bytes 884740
  3.6 1.5 %copy-start.5 = (f32[1536]{0:T(1024)S(1)}, f32[1536]{0:T(1024)}, u32[]{:S(2)}) copy-start(f32[1536]{0:T(1024)} %param.27) | copy-start | bytes 18436
  3.6 1.5 %copy-start.6 = (f32[1536]{0:T(1024)S(1)}, f32[1536]{0:T(1024)}, u32[]{:S(2)}) copy-start(f32[1536]{0:T(1024)} %param.26) | copy-start | bytes 18436
  70.2 3.6 %copy-start.4 = (f32[1536]{0:T(1024)S(1)}, f32[1536]{0:T(1024)}, u32[]{:S(2)}) copy-start(f32[1536]{0:T(1024)} %param.29) | copy-start | bytes 18436
  76.2 4.9 %copy-start.7 = (f32[384]{0:T(512)S(1)}, f32[384]{0:T(512)}, u32[]{:S(2)}) copy-start(f32[384]{0:T(512)} %param.31) | copy-start | bytes 4612
  76.2 25.6 %all-to-all-start.2 = ((bf16[128,2,2304]{2,1,0:T(2,128)(2,1)}), bf16[128,2,2304]{2,1,0:T(2,128)(2,1)S(1)}, u32[]{:S(2)}, u32[]{:S(2)}) async-start(bf16[128,2,2304]{2,1,0:T(2,128)(2,1)} %bitcast.5), calls=%async_computation.2 | async-start | bytes 2359296 | tf_op jit(solution)/shard_map/all_to_all | solution.py:291
  111.7 4.8 %copy-start.2 = (f32[32,2,1536]{2,1,0:T(2,128)S(1)}, f32[32,2,1536]{2,1,0:T(2,128)}, u32[]{:S(2)}) copy-start(f32[32,2,1536]{2,1,0:T(2,128)} %param.23) | copy-start | bytes 1179652
  111.7 25.5 %all-to-all-start.3 = ((bf16[128,2,2304]{2,1,0:T(2,128)(2,1)}), bf16[128,2,2304]{2,1,0:T(2,128)(2,1)S(1)}, u32[]{:S(2)}, u32[]{:S(2)}) async-start(bf16[128,2,2304]{2,1,0:T(2,128)(2,1)} %reshape.113), calls=%async_computation.3 | async-start | bytes 2359296 | tf_op jit(solution)/shard_map/all_to_all | solution.py:296
  139.0 1.2 copy-start.3
  139.1 1.2 copy-start.8

commit v16 on v14

--- a/solution.py
+++ b/solution.py
@@ -149,15 +149,19 @@
     )(length, owner_cross, cross_wq, cross_q_gain.reshape(1, group_width), keys_own, values_own, cross_wo)
 
 
-def _qkv_kernel(x_ref, wq_ref, wk_ref, wv_ref, cos_ref, sin_ref, gain_ref, o_ref):
+def _qkv_kernel(x_ref, wq_ref, wk_ref, wv_ref, angle_ref, qgain_ref, kgain_ref, o_ref):
     block_in = x_ref[...]
-    cosine = cos_ref[...]
-    sine_signed = sin_ref[...]
+    angles = angle_ref[...]
+    lane = lax.broadcasted_iota(jnp.int32, angles.shape, 1)
+    cosine = jnp.cos(angles)
+    sine = jnp.sin(angles)
+    sine_signed = jnp.where(lane < HEAD_DIM // 2, -sine, sine)
     group_width = wq_ref.shape[1]
+    gain_refs = (qgain_ref, kgain_ref)
     for section, w_ref in enumerate((wq_ref, wk_ref, wv_ref)):
         projected = jnp.dot(block_in, w_ref[...], preferred_element_type=jnp.float32)
         if section < 2:
-            gains = gain_ref[section : section + 1, :]
+            gains = gain_refs[section][...]
             parts = []
             for head in range(group_width // HEAD_DIM):
                 lanes = slice(head * HEAD_DIM, (head + 1) * HEAD_DIM)
@@ -178,11 +182,7 @@
     token_total = rows.shape[0]
     group_width = model_width // head_count
     angles = rope_angles(cell_map).reshape(token_total, HEAD_DIM // 2)
-    cosine = jnp.cos(angles)
-    sine = jnp.sin(angles)
-    cos_full = jnp.concatenate([cosine, cosine], axis=-1)
-    sin_signed = jnp.concatenate([-sine, sine], axis=-1)
-    gains = jnp.stack([self_q_gain, self_k_gain])
+    angles_full = jnp.concatenate([angles, angles], axis=-1)
     whole = lambda g: (0, 0)
     packed = pl.pallas_call(
         _qkv_kernel,
@@ -193,8 +193,8 @@
             pl.BlockSpec((model_width, group_width), lambda g: (0, head_count + g)),
             pl.BlockSpec((model_width, group_width), lambda g: (0, 2 * head_count + g)),
             pl.BlockSpec((token_total, HEAD_DIM), whole),
-            pl.BlockSpec((token_total, HEAD_DIM), whole),
-            pl.BlockSpec((2, group_width), lambda g: (0, g)),
+            pl.BlockSpec((1, group_width), lambda g: (0, g)),
+            pl.BlockSpec((1, group_width), lambda g: (0, g)),
         ],
         out_specs=pl.BlockSpec((1, token_total, 3 * group_width), lambda g: (g, 0, 0)),
         out_shape=jax.ShapeDtypeStruct((head_count, token_total, 3 * group_width), jnp.bfloat16),
@@ -203,7 +203,10 @@
             bytes_accessed=2 * model_width * 3 * model_width + 4 * token_total * 3 * model_width,
             transcendentals=0,
         ),
-    )(rows, w_qkv, w_qkv, w_qkv, cos_full, sin_signed, gains)
+    )(
+        rows, w_qkv, w_qkv, w_qkv, angles_full,
+        self_q_gain.reshape(1, model_width), self_k_gain.reshape(1, model_width),
+    )
     return packed.reshape(head_count, videos, per_video, 3 * group_width)
 
 

time: 141 us -> 142 us (level)
  local copies, waits for them, and re-layouts: 17 us -> 18.9 us
  other arithmetic: 7.53 us -> 5.92 us
where the time goes in v16:
time: 142 us; the launch traced here: 141 us
  blocking collectives  44.9 us (32%)
  waiting for transfers between devices  39.8 us (28%)
  local copies, waits for them, and re-layouts  18.9 us (13%)
  Pallas kernels  16.5 us (12%)
  starting transfers between devices  9.49 us (7%)
  other arithmetic  5.92 us (4%)
  matrix products  4.23 us (3%)
  between operations  1.54 us (1%)
    all_to_all x1, blocking collectives, local(): lax.all_to_all(packed.reshape(head_count * videos, 2, per_video * 3 * gro...  29.1 us
    all_to_all x1, waiting for transfers between devices, local(): lax.all_to_all(partial.reshape(head_count * tile_count, 2, per_video * mo...  20.3 us
    all_to_all x1, waiting for transfers between devices, local(): lax.all_to_all(copies, ('head', 'tile'), split_axis=0, concat_axis=0, til...  19.5 us
    all_to_all x1, blocking collectives, local(): lax.all_to_all(own_mixture.reshape(head_count * tile_count, 2, per_video...  15.8 us
    pallas_call x1, Pallas kernels, pack_projected(): pl.pallas_call(_qkv_kernel, grid=(head_count,), in_specs=[pl.BlockSpec((t...  8.32 us
    pallas_call x1, Pallas kernels, cross_partial(): pl.pallas_call(_cross_kernel, in_specs=[pl.BlockSpec(memory_space=pltpu.S...  5.43 us
    all_to_all x1, starting transfers between devices, local(): lax.all_to_all(partial.reshape(head_count * tile_count, 2, per_video * mo...  4.75 us
    all_to_all x1, starting transfers between devices, local(): lax.all_to_all(copies, ('head', 'tile'), split_axis=0, concat_axis=0, til...  4.74 us
  transfers between devices with their start and end apart: 2, of which 2 were waited for; matrix products, arithmetic and copies ran while one was open for 1% of the time, Pallas kernels for 0%

profile of v16, /device:TPU:1, one launch (start us, length us, event | category | flops | bytes accessed | tf_op | source)
XLA Modules:
  0.0 141.2 jit_solution(3012137351569768092)
XLA Ops:
  0.7 0.8 fusion.23
  2.0 1.2 slice_bitcast_fusion.1
  4.1 1.0 reshape.112.x_ref
  5.1 0.6 reshape.113.qgain_ref
  5.7 0.6 reshape.114.kgain_ref
  6.5 0.8 concatenate.6.angle_ref
  7.2 8.3 %shard_map.185 = bf16[4,96,1152]{2,1,0:T(8,128)(2,1)} custom-call(bf16[96,1536]{1,0:T(8,128)(2,1)} %reshape.112.x_ref, bf16[1536,4608]{1,0:T(8,128)(2,1)} %wv_ref.1, bf16[1536,4608]{1,0:T(8,128)(2,1)} %wv_ref.1, bf16[1536,4608]{1,0:T(8,128)(2,1)} %wv_ref.1, f32[96,128]{1,0:T(8,128)} %concatenate.6.angle_ref, f32[1,1536]{1,0:T(1,128)} %reshape.113.qgain_ref, ...), custom_call_target="tpu_custom_call" | custom-call | flops 1358954496 | bytes 15925248 | tf_op jit(solution)/shard_map/pallas_call | solution.py:187
  15.5 3.1 %reshape_reshape.3 = bf16[128,2,1728]{2,1,0:T(2,128)(2,1)S(1)} reshape(bf16[4,96,1152]{2,1,0:T(8,128)(2,1)} %shard_map.185) | data formatting | bytes 1769472 | tf_op jit(solution)/shard_map/reshape;reshape | solution.py:245
  18.6 29.1 %all_to_all.20 = bf16[128,2,1728]{2,1,0:T(2,128)(2,1)S(1)} all-to-all(bf16[128,2,1728]{2,1,0:T(2,128)(2,1)S(1)} %reshape_reshape.3), channel_id=1, replica_groups=mesh['head'=4,'tile'=32] {'head','tile'}, dimensions={0} | all-to-all | bytes 1769472 | tf_op jit(solution)/shard_map/all_to_all | solution.py:244
  47.6 2.2 %reshape.115.x_ref = bf16[384,1152]{1,0:T(8,128)(2,1)} reshape(bf16[128,2,1728]{2,1,0:T(2,128)(2,1)S(1)} %all_to_all.20) | data formatting | bytes 1769472 | tf_op jit(solution)/shard_map/reshape | solution.py:251
  49.8 2.7 %shard_map.186 = bf16[384,384]{1,0:T(8,128)(2,1)} custom-call(bf16[384,1152]{1,0:T(8,128)(2,1)} %reshape.115.x_ref), custom_call_target="tpu_custom_call" | custom-call | flops 226492416 | bytes 1179648 | tf_op jit(solution)/shard_map/pallas_call | solution.py:91
  52.6 1.4 reshape.116
  53.9 15.8 %all_to_all.21 = bf16[128,2,576]{2,1,0:T(2,128)(2,1)S(1)} all-to-all(bf16[128,2,576]{2,1,0:T(2,128)(2,1)S(1)} %reshape.116), channel_id=1, replica_groups=mesh['head'=4,'tile'=32] {'head','tile'}, dimensions={0} | all-to-all | bytes 589824 | tf_op jit(solution)/shard_map/all_to_all | solution.py:252
  69.7 0.5 reshape.117
  70.2 0.3 copy.30
  70.6 3.3 %fusion.28 = (f32[32,3]{0,1:T(4,128)S(1)}, f32[32,3,1536]{2,0,1:T(8,128)S(1)}) fusion(bf16[32,3,1536]{2,0,1:T(8,128)(2,1)S(1)} %dot_general.8, bf16[1536,1536]{1,0:T(8,128)(2,1)} %param.28, f32[32,1536]{1,0:T(8,128)S(1)} %get-tuple-element.6, bf16[32,3,1536]{2,0,1:T(8,128)(2,1)S(1)} %copy-done.1), kind=kOutput, calls=%fused_computation.58 | convolution fusion | flops 453574560 | bytes 6095232 | tf_op jit(solution)/shard_map/dot_general | solution.py:264
  74.6 0.3 broadcast_in_dim.4
  74.9 1.6 %broadcast_in_dim.5 = bf16[4,32,2,2304]{3,2,1,0:T(2,128)(2,1)} broadcast(bf16[32,2,2304]{2,1,0:T(2,128)(2,1)S(1)} %broadcast_in_dim.4), dimensions={1,2,3} | broadcast | bytes 1474560 | tf_op jit(solution)/shard_map/broadcast_in_dim | solution.py:270
  76.6 4.7 %all-to-all-start.2 = ((bf16[128,2,2304]{2,1,0:T(2,128)(2,1)}), bf16[128,2,2304]{2,1,0:T(2,128)(2,1)S(1)}, u32[]{:S(2)}, u32[]{:S(2)}) async-start(bf16[128,2,2304]{2,1,0:T(2,128)(2,1)} %bitcast.5), calls=%async_computation.2 | async-start | bytes 2359296 | tf_op jit(solution)/shard_map/all_to_all | solution.py:273
  81.3 0.6 reshape.120.gain_ref
  82.5 19.5 %all-to-all-done.2 = bf16[128,2,2304]{2,1,0:T(2,128)(2,1)S(1)} async-done(((bf16[128,2,2304]{2,1,0:T(2,128)(2,1)}), bf16[128,2,2304]{2,1,0:T(2,128)(2,1)S(1)}, u32[]{:S(2)}, u32[]{:S(2)}) %all-to-all-start.2) | async-done | bytes 1179680 | tf_op jit(solution)/shard_map/all_to_all | solution.py:273
  102.0 1.6 %reshape.119.x_ref = bf16[384,1536]{1,0:T(8,128)(2,1)} reshape(bf16[128,2,2304]{2,1,0:T(2,128)(2,1)S(1)} %all-to-all-done.2) | data formatting | bytes 2359296 | tf_op jit(solution)/shard_map/reshape | solution.py:274
  103.6 5.4 %shard_map.187 = bf16[384,1536]{1,0:T(8,128)(2,1)} custom-call(s32[1]{0:T(128)S(6)} %copy.43.length_ref, bf16[384,1536]{1,0:T(8,128)(2,1)} %reshape.119.x_ref, bf16[1536,384]{1,0:T(8,128)(2,1)} %wq_ref.3, f32[1,384]{1,0:T(1,128)} %reshape.120.gain_ref, bf16[512,384]{1,0:T(8,128)(2,1)} %bitcast.32, bf16[512,384]{1,0:T(8,128)(2,1)} %bitcast.33, ...), custom_call_target="tpu_custom_call" | custom-call | flops 1207959552 | bytes 5505024 | tf_op jit(solution)/shard_map/pallas_call | solution.py:137
  109.0 2.7 %reshape.121 = bf16[128,2,2304]{2,1,0:T(2,128)(2,1)} reshape(bf16[384,1536]{1,0:T(8,128)(2,1)} %shard_map.187) | data formatting | bytes 2359296 | tf_op jit(solution)/shard_map/reshape | solution.py:279
  111.7 4.8 %all-to-all-start.3 = ((bf16[128,2,2304]{2,1,0:T(2,128)(2,1)}), bf16[128,2,2304]{2,1,0:T(2,128)(2,1)S(1)}, u32[]{:S(2)}, u32[]{:S(2)}) async-start(bf16[128,2,2304]{2,1,0:T(2,128)(2,1)} %reshape.121), calls=%async_computation.3 | async-start | bytes 2359296 | tf_op jit(solution)/shard_map/all_to_all | solution.py:278
  116.5 0.3 fusion.27
  116.8 20.3 %all-to-all-done.3 = bf16[128,2,2304]{2,1,0:T(2,128)(2,1)S(1)} async-done(((bf16[128,2,2304]{2,1,0:T(2,128)(2,1)}), bf16[128,2,2304]{2,1,0:T(2,128)(2,1)S(1)}, u32[]{:S(2)}, u32[]{:S(2)}) %all-to-all-start.3) | async-done | bytes 1179680 | tf_op jit(solution)/shard_map/all_to_all | solution.py:278
  137.2 1.6 %reduce_sum.70 = bf16[32,2,2304]{2,1,0:T(2,128)(2,1)S(1)} reduce(bf16[4,32,2,2304]{3,2,1,0:T(2,128)(2,1)S(1)} %bitcast.30, bf16[]{:T(256)} %constant.66.clone.1), dimensions={0}, to_apply=%region_4.5 | reduce | flops 442368 | bytes 1474562 | tf_op jit(solution)/shard_map/reduce_sum | solution.py:286
  138.8 0.3 reshape.123
  139.1 0.3 fusion.26
  139.4 0.9 multiply_reduce_fusion
  140.3 0.9 fusion.8
  (43 shorter events, 2.5 us)
Async XLA Ops:
  0.6 139.7 %copy-start = (bf16[1536,64]{0,1:T(8,128)(2,1)S(1)}, bf16[1536,64]{0,1:T(8,128)(2,1)}, u32[]{:S(2)}) copy-start(bf16[1536,64]{0,1:T(8,128)(2,1)} %param.35) | copy-start | bytes 589828
  0.6 2.6 %copy-start.1 = (bf16[32,3,1536]{2,0,1:T(8,128)(2,1)S(1)}, bf16[32,3,1536]{2,0,1:T(8,128)(2,1)}, u32[]{:S(2)}) copy-start(bf16[32,3,1536]{2,0,1:T(8,128)(2,1)} %param.18) | copy-start | bytes 884740
  3.6 1.5 %copy-start.5 = (f32[1536]{0:T(1024)S(1)}, f32[1536]{0:T(1024)}, u32[]{:S(2)}) copy-start(f32[1536]{0:T(1024)} %param.26) | copy-start | bytes 18436
  3.6 2.1 %copy-start.6 = (f32[1536]{0:T(1024)S(1)}, f32[1536]{0:T(1024)}, u32[]{:S(2)}) copy-start(f32[1536]{0:T(1024)} %param.27) | copy-start | bytes 18436
  70.6 3.6 %copy-start.4 = (f32[1536]{0:T(1024)S(1)}, f32[1536]{0:T(1024)}, u32[]{:S(2)}) copy-start(f32[1536]{0:T(1024)} %param.29) | copy-start | bytes 18436
  76.6 4.8 %copy-start.7 = (f32[384]{0:T(512)S(1)}, f32[384]{0:T(512)}, u32[]{:S(2)}) copy-start(f32[384]{0:T(512)} %param.31) | copy-start | bytes 4612
  76.6 25.4 %all-to-all-start.2 = ((bf16[128,2,2304]{2,1,0:T(2,128)(2,1)}), bf16[128,2,2304]{2,1,0:T(2,128)(2,1)S(1)}, u32[]{:S(2)}, u32[]{:S(2)}) async-start(bf16[128,2,2304]{2,1,0:T(2,128)(2,1)} %bitcast.5), calls=%async_computation.2 | async-start | bytes 2359296 | tf_op jit(solution)/shard_map/all_to_all | solution.py:273
  111.7 4.8 %copy-start.2 = (f32[32,2,1536]{2,1,0:T(2,128)S(1)}, f32[32,2,1536]{2,1,0:T(2,128)}, u32[]{:S(2)}) copy-start(f32[32,2,1536]{2,1,0:T(2,128)} %param.23) | copy-start | bytes 1179652
  111.7 25.5 %all-to-all-start.3 = ((bf16[128,2,2304]{2,1,0:T(2,128)(2,1)}), bf16[128,2,2304]{2,1,0:T(2,128)(2,1)S(1)}, u32[]{:S(2)}, u32[]{:S(2)}) async-start(bf16[128,2,2304]{2,1,0:T(2,128)(2,1)} %reshape.121), calls=%async_computation.3 | async-start | bytes 2359296 | tf_op jit(solution)/shard_map/all_to_all | solution.py:278
  139.1 1.2 copy-start.3
  139.1 1.2 copy-start.8

commit v17 on v14

--- a/solution.py
+++ b/solution.py
@@ -106,24 +106,30 @@
     projected = jnp.dot(x_ref[...], wq_ref[...], preferred_element_type=jnp.float32)
     gains = gain_ref[...]
     live = (lax.broadcasted_iota(jnp.int32, (1, text), 1) < length_ref[0]).astype(jnp.float32)
-    for head in range(group_width // HEAD_DIM):
-        lanes = slice(head * HEAD_DIM, (head + 1) * HEAD_DIM)
-        piece = projected[:, lanes]
-        mean_square = jnp.mean(piece * piece, axis=-1, keepdims=True)
-        queries = (piece * lax.rsqrt(mean_square + EPSILON) * gains[:, lanes]).astype(jnp.bfloat16)
-        scores = (
-            lax.dot_general(
-                queries, keys_ref[:, lanes], (((1,), (1,)), ((), ())),
+    block_rows = 128
+    for start in range(0, x_ref.shape[0], block_rows):
+        rows = slice(start, start + block_rows)
+        for head in range(group_width // HEAD_DIM):
+            lanes = slice(head * HEAD_DIM, (head + 1) * HEAD_DIM)
+            piece = projected[rows, lanes]
+            mean_square = jnp.mean(piece * piece, axis=-1, keepdims=True)
+            queries = (piece * lax.rsqrt(mean_square + EPSILON) * gains[:, lanes]).astype(
+                jnp.bfloat16
+            )
+            scores = (
+                lax.dot_general(
+                    queries, keys_ref[:, lanes], (((1,), (1,)), ((), ())),
+                    preferred_element_type=jnp.float32,
+                )
+                * factor
+            )
+            weights = jnp.exp(scores) * live
+            totals = jnp.sum(weights, axis=-1, keepdims=True)
+            mixture = jnp.dot(
+                weights.astype(jnp.bfloat16), values_ref[:, lanes],
                 preferred_element_type=jnp.float32,
             )
-            * factor
-        )
-        weights = jnp.exp(scores) * live
-        totals = jnp.sum(weights, axis=-1, keepdims=True)
-        mixture = jnp.dot(
-            weights.astype(jnp.bfloat16), values_ref[:, lanes], preferred_element_type=jnp.float32
-        )
-        mixed_ref[:, lanes] = (mixture / totals).astype(mixed_ref.dtype)
+            mixed_ref[rows, lanes] = (mixture / totals).astype(mixed_ref.dtype)
     o_ref[...] = jnp.dot(mixed_ref[...], wo_ref[...], preferred_element_type=jnp.float32).astype(
         o_ref.dtype
     )

time: 141 us -> 142 us (level)
  no operation moved by 1% of the time
where the time goes in v17:
time: 142 us
  blocking collectives  44.9 us (32%)
  waiting for transfers between devices  39.8 us (28%)
  Pallas kernels  17.4 us (12%)
  local copies, waits for them, and re-layouts  17 us (12%)
  starting transfers between devices  9.64 us (7%)
  other arithmetic  7.53 us (5%)
  matrix products  4.24 us (3%)
  between operations  1.57 us (1%)
    all_to_all x1, blocking collectives, local(): lax.all_to_all(packed.reshape(head_count * videos, 2, per_video * 3 * gro...  29.1 us
    all_to_all x1, waiting for transfers between devices, local(): lax.all_to_all(partial.reshape(head_count * tile_count, 2, per_video * mo...  20.3 us
    all_to_all x1, waiting for transfers between devices, local(): lax.all_to_all(copies, ('head', 'tile'), split_axis=0, concat_axis=0, til...  19.5 us
    all_to_all x1, blocking collectives, local(): lax.all_to_all(own_mixture.reshape(head_count * tile_count, 2, per_video...  15.8 us
    pallas_call x1, Pallas kernels, pack_projected(): pl.pallas_call(_qkv_kernel, grid=(head_count,), in_specs=[pl.BlockSpec((t...  8.22 us
    pallas_call x1, Pallas kernels, cross_partial(): pl.pallas_call(_cross_kernel, in_specs=[pl.BlockSpec(memory_space=pltpu.S...  6.47 us
    all_to_all x1, starting transfers between devices, local(): lax.all_to_all(copies, ('head', 'tile'), split_axis=0, concat_axis=0, til...  4.9 us
    all_to_all x1, starting transfers between devices, local(): lax.all_to_all(partial.reshape(head_count * tile_count, 2, per_video * mo...  4.73 us
  transfers between devices with their start and end apart: 2, of which 2 were waited for; matrix products, arithmetic and copies ran while one was open for 1% of the time, Pallas kernels for 0%

profile of v17, /device:TPU:1, one launch (start us, length us, event | category | flops | bytes accessed | tf_op | source)
XLA Modules:
  0.0 142.0 jit_solution(14690653882796243206)
XLA Ops:
  0.7 0.8 fusion.24
  2.0 1.2 slice_bitcast_fusion.1
  4.1 1.0 reshape.106.x_ref
  5.2 0.6 pad_maximum_fusion.3.gain_ref
  5.9 0.3 fusion.29
  6.2 0.7 pad_maximum_fusion.1
  6.9 8.2 %shard_map.185 = bf16[4,96,1152]{2,1,0:T(8,128)(2,1)} custom-call(bf16[96,1536]{1,0:T(8,128)(2,1)} %reshape.106.x_ref, bf16[1536,4608]{1,0:T(8,128)(2,1)} %wv_ref.1, bf16[1536,4608]{1,0:T(8,128)(2,1)} %wv_ref.1, bf16[1536,4608]{1,0:T(8,128)(2,1)} %wv_ref.1, f32[96,128]{1,0:T(8,128)} %get-tuple-element.21.cos_ref, f32[96,128]{1,0:T(8,128)} %get-tuple-element.22.sin_ref, ...), custom_call_target="tpu_custom_call" | custom-call | flops 1358954496 | bytes 15925248 | tf_op jit(solution)/shard_map/pallas_call | solution.py:193
  15.1 3.1 %reshape_reshape.3 = bf16[128,2,1728]{2,1,0:T(2,128)(2,1)S(1)} reshape(bf16[4,96,1152]{2,1,0:T(8,128)(2,1)} %shard_map.185) | data formatting | bytes 1769472 | tf_op jit(solution)/shard_map/reshape;reshape | solution.py:248
  18.2 29.1 %all_to_all.20 = bf16[128,2,1728]{2,1,0:T(2,128)(2,1)S(1)} all-to-all(bf16[128,2,1728]{2,1,0:T(2,128)(2,1)S(1)} %reshape_reshape.3), channel_id=1, replica_groups=mesh['head'=4,'tile'=32] {'head','tile'}, dimensions={0} | all-to-all | bytes 1769472 | tf_op jit(solution)/shard_map/all_to_all | solution.py:247
  47.3 2.2 %reshape.107.x_ref = bf16[384,1152]{1,0:T(8,128)(2,1)} reshape(bf16[128,2,1728]{2,1,0:T(2,128)(2,1)S(1)} %all_to_all.20) | data formatting | bytes 1769472 | tf_op jit(solution)/shard_map/reshape | solution.py:254
  49.5 2.7 %shard_map.186 = bf16[384,384]{1,0:T(8,128)(2,1)} custom-call(bf16[384,1152]{1,0:T(8,128)(2,1)} %reshape.107.x_ref), custom_call_target="tpu_custom_call" | custom-call | flops 226492416 | bytes 1179648 | tf_op jit(solution)/shard_map/pallas_call | solution.py:91
  52.2 1.4 reshape.108
  53.5 15.8 %all_to_all.21 = bf16[128,2,576]{2,1,0:T(2,128)(2,1)S(1)} all-to-all(bf16[128,2,576]{2,1,0:T(2,128)(2,1)S(1)} %reshape.108), channel_id=1, replica_groups=mesh['head'=4,'tile'=32] {'head','tile'}, dimensions={0} | all-to-all | bytes 589824 | tf_op jit(solution)/shard_map/all_to_all | solution.py:255
  69.3 0.5 reshape.109
  69.8 0.3 copy.30
  70.2 3.3 %fusion.32 = (f32[32,3]{0,1:T(4,128)S(1)}, f32[32,3,1536]{2,0,1:T(8,128)S(1)}) fusion(bf16[32,3,1536]{2,0,1:T(8,128)(2,1)S(1)} %dot_general.8, bf16[1536,1536]{1,0:T(8,128)(2,1)} %param.28, f32[32,1536]{1,0:T(8,128)S(1)} %get-tuple-element.8, bf16[32,3,1536]{2,0,1:T(8,128)(2,1)S(1)} %copy-done.1), kind=kOutput, calls=%fused_computation.65 | convolution fusion | flops 453574560 | bytes 6095232 | tf_op jit(solution)/shard_map/dot_general | solution.py:267
  74.2 0.3 broadcast_in_dim.4
  74.5 1.6 %broadcast_in_dim.5 = bf16[4,32,2,2304]{3,2,1,0:T(2,128)(2,1)} broadcast(bf16[32,2,2304]{2,1,0:T(2,128)(2,1)S(1)} %broadcast_in_dim.4), dimensions={1,2,3} | broadcast | bytes 1474560 | tf_op jit(solution)/shard_map/broadcast_in_dim | solution.py:273
  76.2 4.9 %all-to-all-start.2 = ((bf16[128,2,2304]{2,1,0:T(2,128)(2,1)}), bf16[128,2,2304]{2,1,0:T(2,128)(2,1)S(1)}, u32[]{:S(2)}, u32[]{:S(2)}) async-start(bf16[128,2,2304]{2,1,0:T(2,128)(2,1)} %bitcast.5), calls=%async_computation.2 | async-start | bytes 2359296 | tf_op jit(solution)/shard_map/all_to_all | solution.py:276
  81.1 0.6 reshape.112.gain_ref
  82.3 19.5 %all-to-all-done.2 = bf16[128,2,2304]{2,1,0:T(2,128)(2,1)S(1)} async-done(((bf16[128,2,2304]{2,1,0:T(2,128)(2,1)}), bf16[128,2,2304]{2,1,0:T(2,128)(2,1)S(1)}, u32[]{:S(2)}, u32[]{:S(2)}) %all-to-all-start.2) | async-done | bytes 1179680 | tf_op jit(solution)/shard_map/all_to_all | solution.py:276
  101.8 1.6 %reshape.111.x_ref = bf16[384,1536]{1,0:T(8,128)(2,1)} reshape(bf16[128,2,2304]{2,1,0:T(2,128)(2,1)S(1)} %all-to-all-done.2) | data formatting | bytes 2359296 | tf_op jit(solution)/shard_map/reshape | solution.py:277
  103.4 6.5 %shard_map.187 = bf16[384,1536]{1,0:T(8,128)(2,1)} custom-call(s32[1]{0:T(128)S(6)} %copy.43.length_ref, bf16[384,1536]{1,0:T(8,128)(2,1)} %reshape.111.x_ref, bf16[1536,384]{1,0:T(8,128)(2,1)} %wq_ref.3, f32[1,384]{1,0:T(1,128)} %reshape.112.gain_ref, bf16[512,384]{1,0:T(8,128)(2,1)} %bitcast.32, bf16[512,384]{1,0:T(8,128)(2,1)} %bitcast.33, ...), custom_call_target="tpu_custom_call" | custom-call | flops 1207959552 | bytes 5505024 | tf_op jit(solution)/shard_map/pallas_call | solution.py:143
  109.8 2.7 %reshape.113 = bf16[128,2,2304]{2,1,0:T(2,128)(2,1)} reshape(bf16[384,1536]{1,0:T(8,128)(2,1)} %shard_map.187) | data formatting | bytes 2359296 | tf_op jit(solution)/shard_map/reshape | solution.py:282
  112.5 4.7 %all-to-all-start.3 = ((bf16[128,2,2304]{2,1,0:T(2,128)(2,1)}), bf16[128,2,2304]{2,1,0:T(2,128)(2,1)S(1)}, u32[]{:S(2)}, u32[]{:S(2)}) async-start(bf16[128,2,2304]{2,1,0:T(2,128)(2,1)} %reshape.113), calls=%async_computation.3 | async-start | bytes 2359296 | tf_op jit(solution)/shard_map/all_to_all | solution.py:281
  117.3 0.3 fusion.31
  117.6 20.3 %all-to-all-done.3 = bf16[128,2,2304]{2,1,0:T(2,128)(2,1)S(1)} async-done(((bf16[128,2,2304]{2,1,0:T(2,128)(2,1)}), bf16[128,2,2304]{2,1,0:T(2,128)(2,1)S(1)}, u32[]{:S(2)}, u32[]{:S(2)}) %all-to-all-start.3) | async-done | bytes 1179680 | tf_op jit(solution)/shard_map/all_to_all | solution.py:281
  137.9 1.6 %reduce_sum.70 = bf16[32,2,2304]{2,1,0:T(2,128)(2,1)S(1)} reduce(bf16[4,32,2,2304]{3,2,1,0:T(2,128)(2,1)S(1)} %bitcast.30, bf16[]{:T(256)} %constant.66.clone.1), dimensions={0}, to_apply=%region_4.5 | reduce | flops 442368 | bytes 1474562 | tf_op jit(solution)/shard_map/reduce_sum | solution.py:289
  139.6 0.3 reshape.115
  139.9 0.3 fusion.28
  140.2 0.9 multiply_reduce_fusion
  141.1 0.9 fusion.8
  (45 shorter events, 2.5 us)
Async XLA Ops:
  0.6 140.5 %copy-start = (bf16[1536,64]{0,1:T(8,128)(2,1)S(1)}, bf16[1536,64]{0,1:T(8,128)(2,1)}, u32[]{:S(2)}) copy-start(bf16[1536,64]{0,1:T(8,128)(2,1)} %param.35) | copy-start | bytes 589828
  0.6 2.6 %copy-start.1 = (bf16[32,3,1536]{2,0,1:T(8,128)(2,1)S(1)}, bf16[32,3,1536]{2,0,1:T(8,128)(2,1)}, u32[]{:S(2)}) copy-start(bf16[32,3,1536]{2,0,1:T(8,128)(2,1)} %param.18) | copy-start | bytes 884740
  3.6 1.5 %copy-start.5 = (f32[1536]{0:T(1024)S(1)}, f32[1536]{0:T(1024)}, u32[]{:S(2)}) copy-start(f32[1536]{0:T(1024)} %param.27) | copy-start | bytes 18436
  3.6 1.5 %copy-start.6 = (f32[1536]{0:T(1024)S(1)}, f32[1536]{0:T(1024)}, u32[]{:S(2)}) copy-start(f32[1536]{0:T(1024)} %param.26) | copy-start | bytes 18436
  70.2 3.6 %copy-start.4 = (f32[1536]{0:T(1024)S(1)}, f32[1536]{0:T(1024)}, u32[]{:S(2)}) copy-start(f32[1536]{0:T(1024)} %param.29) | copy-start | bytes 18436
  76.2 4.9 %copy-start.7 = (f32[384]{0:T(512)S(1)}, f32[384]{0:T(512)}, u32[]{:S(2)}) copy-start(f32[384]{0:T(512)} %param.31) | copy-start | bytes 4612
  76.2 25.6 %all-to-all-start.2 = ((bf16[128,2,2304]{2,1,0:T(2,128)(2,1)}), bf16[128,2,2304]{2,1,0:T(2,128)(2,1)S(1)}, u32[]{:S(2)}, u32[]{:S(2)}) async-start(bf16[128,2,2304]{2,1,0:T(2,128)(2,1)} %bitcast.5), calls=%async_computation.2 | async-start | bytes 2359296 | tf_op jit(solution)/shard_map/all_to_all | solution.py:276
  112.5 4.7 %copy-start.2 = (f32[32,2,1536]{2,1,0:T(2,128)S(1)}, f32[32,2,1536]{2,1,0:T(2,128)}, u32[]{:S(2)}) copy-start(f32[32,2,1536]{2,1,0:T(2,128)} %param.23) | copy-start | bytes 1179652
  112.5 25.4 %all-to-all-start.3 = ((bf16[128,2,2304]{2,1,0:T(2,128)(2,1)}), bf16[128,2,2304]{2,1,0:T(2,128)(2,1)S(1)}, u32[]{:S(2)}, u32[]{:S(2)}) async-start(bf16[128,2,2304]{2,1,0:T(2,128)(2,1)} %reshape.113), calls=%async_computation.3 | async-start | bytes 2359296 | tf_op jit(solution)/shard_map/all_to_all | solution.py:281
  139.9 1.2 copy-start.3
  139.9 1.2 copy-start.8

commit v18 on v14

--- a/solution.py
+++ b/solution.py
@@ -146,7 +146,15 @@
             + 4 * token_total * model_width,
             transcendentals=token_total * text * (group_width // HEAD_DIM),
         ),
-    )(length, owner_cross, cross_wq, cross_q_gain.reshape(1, group_width), keys_own, values_own, cross_wo)
+    )(
+        length,
+        owner_cross,
+        pltpu.with_memory_space_constraint(cross_wq, pltpu.VMEM),
+        cross_q_gain.reshape(1, group_width),
+        pltpu.with_memory_space_constraint(keys_own, pltpu.VMEM),
+        pltpu.with_memory_space_constraint(values_own, pltpu.VMEM),
+        pltpu.with_memory_space_constraint(cross_wo, pltpu.VMEM),
+    )
 
 
 def _qkv_kernel(x_ref, wq_ref, wk_ref, wv_ref, cos_ref, sin_ref, gain_ref, o_ref):

time: 141 us -> 143 us (1.014)
  local copies, waits for them, and re-layouts: 17 us -> 18.7 us
where the time goes in v18:
time: 143 us; the launch traced here: 142 us
  blocking collectives  44.9 us (31%)
  waiting for transfers between devices  39.5 us (28%)
  local copies, waits for them, and re-layouts  18.7 us (13%)
  Pallas kernels  15.5 us (11%)
  starting transfers between devices  10.7 us (7%)
  other arithmetic  7.5 us (5%)
  matrix products  4.24 us (3%)
  between operations  1.6 us (1%)
    all_to_all x1, blocking collectives, local(): lax.all_to_all(packed.reshape(head_count * videos, 2, per_video * 3 * gro...  29.1 us
    all_to_all x1, waiting for transfers between devices, local(): lax.all_to_all(partial.reshape(head_count * tile_count, 2, per_video * mo...  20.3 us
    all_to_all x1, waiting for transfers between devices, local(): lax.all_to_all(copies, ('head', 'tile'), split_axis=0, concat_axis=0, til...  19.1 us
    all_to_all x1, blocking collectives, local(): lax.all_to_all(own_mixture.reshape(head_count * tile_count, 2, per_video...  15.8 us
    pallas_call x1, Pallas kernels, pack_projected(): pl.pallas_call(_qkv_kernel, grid=(head_count,), in_specs=[pl.BlockSpec((t...  8.24 us
    all_to_all x1, starting transfers between devices, local(): lax.all_to_all(copies, ('head', 'tile'), split_axis=0, concat_axis=0, til...  5.9 us
    all_to_all x1, starting transfers between devices, local(): lax.all_to_all(partial.reshape(head_count * tile_count, 2, per_video * mo...  4.75 us
    pallas_call x1, Pallas kernels, cross_partial(): pl.pallas_call(_cross_kernel, in_specs=[pl.BlockSpec(memory_space=pltpu.S...  4.5 us
  transfers between devices with their start and end apart: 2, of which 2 were waited for; matrix products, arithmetic and copies ran while one was open for 1% of the time, Pallas kernels for 0%

profile of v18, /device:TPU:1, one launch (start us, length us, event | category | flops | bytes accessed | tf_op | source)
XLA Modules:
  0.0 142.5 jit_solution(32182621237145282)
XLA Ops:
  0.7 0.8 fusion.24
  2.0 1.2 slice_bitcast_fusion.1
  4.1 1.0 reshape.106.x_ref
  5.2 0.6 pad_maximum_fusion.3.gain_ref
  6.2 0.7 pad_maximum_fusion.1
  6.9 8.2 %shard_map.185 = bf16[4,96,1152]{2,1,0:T(8,128)(2,1)} custom-call(bf16[96,1536]{1,0:T(8,128)(2,1)} %reshape.106.x_ref, bf16[1536,4608]{1,0:T(8,128)(2,1)} %wv_ref.1, bf16[1536,4608]{1,0:T(8,128)(2,1)} %wv_ref.1, bf16[1536,4608]{1,0:T(8,128)(2,1)} %wv_ref.1, f32[96,128]{1,0:T(8,128)} %get-tuple-element.21.cos_ref, f32[96,128]{1,0:T(8,128)} %get-tuple-element.22.sin_ref, ...), custom_call_target="tpu_custom_call" | custom-call | flops 1358954496 | bytes 15925248 | tf_op jit(solution)/shard_map/pallas_call | solution.py:195
  15.1 3.1 %reshape_reshape.3 = bf16[128,2,1728]{2,1,0:T(2,128)(2,1)S(1)} reshape(bf16[4,96,1152]{2,1,0:T(8,128)(2,1)} %shard_map.185) | data formatting | bytes 1769472 | tf_op jit(solution)/shard_map/reshape;reshape | solution.py:250
  18.2 29.1 %all_to_all.20 = bf16[128,2,1728]{2,1,0:T(2,128)(2,1)S(1)} all-to-all(bf16[128,2,1728]{2,1,0:T(2,128)(2,1)S(1)} %reshape_reshape.3), channel_id=1, replica_groups=mesh['head'=4,'tile'=32] {'head','tile'}, dimensions={0} | all-to-all | bytes 1769472 | tf_op jit(solution)/shard_map/all_to_all | solution.py:249
  47.3 2.2 %reshape.107.x_ref = bf16[384,1152]{1,0:T(8,128)(2,1)} reshape(bf16[128,2,1728]{2,1,0:T(2,128)(2,1)S(1)} %all_to_all.20) | data formatting | bytes 1769472 | tf_op jit(solution)/shard_map/reshape | solution.py:256
  49.5 2.7 %shard_map.186 = bf16[384,384]{1,0:T(8,128)(2,1)} custom-call(bf16[384,1152]{1,0:T(8,128)(2,1)} %reshape.107.x_ref), custom_call_target="tpu_custom_call" | custom-call | flops 226492416 | bytes 1179648 | tf_op jit(solution)/shard_map/pallas_call | solution.py:91
  52.2 1.4 reshape.108
  53.5 15.8 %all_to_all.21 = bf16[128,2,576]{2,1,0:T(2,128)(2,1)S(1)} all-to-all(bf16[128,2,576]{2,1,0:T(2,128)(2,1)S(1)} %reshape.108), channel_id=1, replica_groups=mesh['head'=4,'tile'=32] {'head','tile'}, dimensions={0} | all-to-all | bytes 589824 | tf_op jit(solution)/shard_map/all_to_all | solution.py:257
  69.3 0.5 reshape.109
  69.8 0.3 copy.30
  70.3 3.3 %fusion.32 = (f32[32,3]{0,1:T(4,128)S(1)}, f32[32,3,1536]{2,0,1:T(8,128)S(1)}) fusion(bf16[32,3,1536]{2,0,1:T(8,128)(2,1)S(1)} %dot_general.8, bf16[1536,1536]{1,0:T(8,128)(2,1)} %param.28, f32[32,1536]{1,0:T(8,128)S(1)} %get-tuple-element.8, bf16[32,3,1536]{2,0,1:T(8,128)(2,1)S(1)} %copy-done.7), kind=kOutput, calls=%fused_computation.65 | convolution fusion | flops 453574560 | bytes 6095232 | tf_op jit(solution)/shard_map/dot_general | solution.py:269
  73.8 0.6 copy-done.5
  74.8 0.3 broadcast_in_dim.4
  75.2 1.7 %broadcast_in_dim.5 = bf16[4,32,2,2304]{3,2,1,0:T(2,128)(2,1)} broadcast(bf16[32,2,2304]{2,1,0:T(2,128)(2,1)S(1)} %broadcast_in_dim.4), dimensions={1,2,3} | broadcast | bytes 1474560 | tf_op jit(solution)/shard_map/broadcast_in_dim | solution.py:275
  76.8 5.9 %all-to-all-start.2 = ((bf16[128,2,2304]{2,1,0:T(2,128)(2,1)}), bf16[128,2,2304]{2,1,0:T(2,128)(2,1)}, u32[]{:S(2)}, u32[]{:S(2)}) async-start(bf16[128,2,2304]{2,1,0:T(2,128)(2,1)} %bitcast.5), calls=%async_computation.2 | async-start | bytes 2359296 | tf_op jit(solution)/shard_map/all_to_all | solution.py:278
  82.7 0.6 reshape.112.gain_ref
  84.0 19.1 %all-to-all-done.2 = bf16[128,2,2304]{2,1,0:T(2,128)(2,1)} async-done(((bf16[128,2,2304]{2,1,0:T(2,128)(2,1)}), bf16[128,2,2304]{2,1,0:T(2,128)(2,1)}, u32[]{:S(2)}, u32[]{:S(2)}) %all-to-all-start.2) | async-done | bytes 1179680 | tf_op jit(solution)/shard_map/all_to_all | solution.py:278
  103.1 2.6 %reshape.111.x_ref = bf16[384,1536]{1,0:T(8,128)(2,1)} reshape(bf16[128,2,2304]{2,1,0:T(2,128)(2,1)} %all-to-all-done.2) | data formatting | bytes 2359296 | tf_op jit(solution)/shard_map/reshape | solution.py:279
  105.8 4.5 %shard_map.187 = bf16[384,1536]{1,0:T(8,128)(2,1)} custom-call(s32[1]{0:T(128)S(6)} %copy.43.length_ref, bf16[384,1536]{1,0:T(8,128)(2,1)} %reshape.111.x_ref, bf16[1536,384]{1,0:T(8,128)(2,1)S(1)} %copy-done.1, f32[1,384]{1,0:T(1,128)} %reshape.112.gain_ref, bf16[512,384]{1,0:T(8,128)(2,1)S(1)} %bitcast.30, bf16[512,384]{1,0:T(8,128)(2,1)S(1)} %bitcast.31, ...), custom_call_target="tpu_custom_call" | custom-call | flops 1207959552 | bytes 5505024 | tf_op jit(solution)/shard_map/pallas_call | solution.py:137
  110.3 2.6 %reshape.113 = bf16[128,2,2304]{2,1,0:T(2,128)(2,1)} reshape(bf16[384,1536]{1,0:T(8,128)(2,1)} %shard_map.187) | data formatting | bytes 2359296 | tf_op jit(solution)/shard_map/reshape | solution.py:284
  112.9 4.8 %all-to-all-start.3 = ((bf16[128,2,2304]{2,1,0:T(2,128)(2,1)}), bf16[128,2,2304]{2,1,0:T(2,128)(2,1)S(1)}, u32[]{:S(2)}, u32[]{:S(2)}) async-start(bf16[128,2,2304]{2,1,0:T(2,128)(2,1)} %reshape.113), calls=%async_computation.3 | async-start | bytes 2359296 | tf_op jit(solution)/shard_map/all_to_all | solution.py:283
  117.7 0.3 fusion.31
  118.1 20.3 %all-to-all-done.3 = bf16[128,2,2304]{2,1,0:T(2,128)(2,1)S(1)} async-done(((bf16[128,2,2304]{2,1,0:T(2,128)(2,1)}), bf16[128,2,2304]{2,1,0:T(2,128)(2,1)S(1)}, u32[]{:S(2)}, u32[]{:S(2)}) %all-to-all-start.3) | async-done | bytes 1179680 | tf_op jit(solution)/shard_map/all_to_all | solution.py:283
  138.4 1.6 %reduce_sum.70 = bf16[32,2,2304]{2,1,0:T(2,128)(2,1)S(1)} reduce(bf16[4,32,2,2304]{3,2,1,0:T(2,128)(2,1)S(1)} %bitcast.32, bf16[]{:T(256)} %constant.66.clone.1), dimensions={0}, to_apply=%region_4.5 | reduce | flops 442368 | bytes 1474562 | tf_op jit(solution)/shard_map/reduce_sum | solution.py:291
  140.0 0.3 reshape.115
  140.4 0.3 fusion.28
  140.7 0.9 multiply_reduce_fusion
  141.6 0.9 fusion.8
  (57 shorter events, 2.7 us)
Async XLA Ops:
  0.6 140.9 %copy-start = (bf16[1536,64]{0,1:T(8,128)(2,1)S(1)}, bf16[1536,64]{0,1:T(8,128)(2,1)}, u32[]{:S(2)}) copy-start(bf16[1536,64]{0,1:T(8,128)(2,1)} %param.35) | copy-start | bytes 589828
  0.6 2.6 %copy-start.7 = (bf16[32,3,1536]{2,0,1:T(8,128)(2,1)S(1)}, bf16[32,3,1536]{2,0,1:T(8,128)(2,1)}, u32[]{:S(2)}) copy-start(bf16[32,3,1536]{2,0,1:T(8,128)(2,1)} %param.18) | copy-start | bytes 884740
  3.6 1.5 %copy-start.11 = (f32[1536]{0:T(1024)S(1)}, f32[1536]{0:T(1024)}, u32[]{:S(2)}) copy-start(f32[1536]{0:T(1024)} %param.27) | copy-start | bytes 18436
  3.6 1.5 %copy-start.12 = (f32[1536]{0:T(1024)S(1)}, f32[1536]{0:T(1024)}, u32[]{:S(2)}) copy-start(f32[1536]{0:T(1024)} %param.26) | copy-start | bytes 18436
  70.2 4.2 %copy-start.10 = (f32[1536]{0:T(1024)S(1)}, f32[1536]{0:T(1024)}, u32[]{:S(2)}) copy-start(f32[1536]{0:T(1024)} %param.29) | copy-start | bytes 18436
  73.6 0.8 copy-start.5
  76.8 5.9 %copy-start.13 = (f32[384]{0:T(512)S(1)}, f32[384]{0:T(512)}, u32[]{:S(2)}) copy-start(f32[384]{0:T(512)} %param.31) | copy-start | bytes 4612
  76.8 29.0 %copy-start.3 = (bf16[1,512,384]{2,1,0:T(8,128)(2,1)S(1)}, bf16[1,512,384]{2,1,0:T(8,128)(2,1)}, u32[]{:S(2)}) copy-start(bf16[1,512,384]{2,1,0:T(8,128)(2,1)} %param.32) | copy-start | bytes 1179652
  76.8 29.0 %copy-start.4 = (bf16[1,512,384]{2,1,0:T(8,128)(2,1)S(1)}, bf16[1,512,384]{2,1,0:T(8,128)(2,1)}, u32[]{:S(2)}) copy-start(bf16[1,512,384]{2,1,0:T(8,128)(2,1)} %param.33) | copy-start | bytes 1179652
  76.8 26.3 %all-to-all-start.2 = ((bf16[128,2,2304]{2,1,0:T(2,128)(2,1)}), bf16[128,2,2304]{2,1,0:T(2,128)(2,1)}, u32[]{:S(2)}, u32[]{:S(2)}) async-start(bf16[128,2,2304]{2,1,0:T(2,128)(2,1)} %bitcast.5), calls=%async_computation.2 | async-start | bytes 2359296 | tf_op jit(solution)/shard_map/all_to_all | solution.py:278
  84.0 21.8 %copy-start.1 = (bf16[1536,384]{1,0:T(8,128)(2,1)S(1)}, bf16[1536,384]{1,0:T(8,128)(2,1)}, u32[]{:S(2)}) copy-start(bf16[1536,384]{1,0:T(8,128)(2,1)} %wq_ref.3) | copy-start | bytes 3538948
  84.0 21.8 %copy-start.2 = (bf16[384,1536]{1,0:T(8,128)(2,1)S(1)}, bf16[384,1536]{1,0:T(8,128)(2,1)}, u32[]{:S(2)}) copy-start(bf16[384,1536]{1,0:T(8,128)(2,1)} %wo_ref.1) | copy-start | bytes 3538948
  112.9 4.8 %copy-start.8 = (f32[32,2,1536]{2,1,0:T(2,128)S(1)}, f32[32,2,1536]{2,1,0:T(2,128)}, u32[]{:S(2)}) copy-start(f32[32,2,1536]{2,1,0:T(2,128)} %param.23) | copy-start | bytes 1179652
  112.9 25.5 %all-to-all-start.3 = ((bf16[128,2,2304]{2,1,0:T(2,128)(2,1)}), bf16[128,2,2304]{2,1,0:T(2,128)(2,1)S(1)}, u32[]{:S(2)}, u32[]{:S(2)}) async-start(bf16[128,2,2304]{2,1,0:T(2,128)(2,1)} %reshape.113), calls=%async_computation.3 | async-start | bytes 2359296 | tf_op jit(solution)/shard_map/all_to_all | solution.py:283
  138.4 1.9 %copy-start.6 = (f32[32,3,1536]{2,0,1:T(8,128)S(1)}, f32[32,3,1536]{2,0,1:T(8,128)}, u32[]{:S(2)}) copy-start(f32[32,3,1536]{2,0,1:T(8,128)} %copy-done.5) | copy-start | bytes 1769476
  140.3 1.2 copy-start.9
  140.4 1.2 copy-start.14

commit v19 on v18

--- a/solution.py
+++ b/solution.py
@@ -149,11 +149,11 @@
     )(
         length,
         owner_cross,
-        pltpu.with_memory_space_constraint(cross_wq, pltpu.VMEM),
+        cross_wq,
         cross_q_gain.reshape(1, group_width),
         pltpu.with_memory_space_constraint(keys_own, pltpu.VMEM),
         pltpu.with_memory_space_constraint(values_own, pltpu.VMEM),
-        pltpu.with_memory_space_constraint(cross_wo, pltpu.VMEM),
+        cross_wo,
     )
 
 

time: 143 us -> 141 us (0.986)
  local copies, waits for them, and re-layouts: 18.7 us -> 17 us
where the time goes in v19:
time: 141 us
  blocking collectives  44.9 us (32%)
  waiting for transfers between devices  39.8 us (28%)
  local copies, waits for them, and re-layouts  17 us (12%)
  Pallas kernels  16.2 us (11%)
  starting transfers between devices  9.65 us (7%)
  other arithmetic  7.55 us (5%)
  matrix products  4.24 us (3%)
  between operations  1.59 us (1%)
    all_to_all x1, blocking collectives, local(): lax.all_to_all(packed.reshape(head_count * videos, 2, per_video * 3 * gro...  29.1 us
    all_to_all x1, waiting for transfers between devices, local(): lax.all_to_all(partial.reshape(head_count * tile_count, 2, per_video * mo...  20.3 us
    all_to_all x1, waiting for transfers between devices, local(): lax.all_to_all(copies, ('head', 'tile'), split_axis=0, concat_axis=0, til...  19.4 us
    all_to_all x1, blocking collectives, local(): lax.all_to_all(own_mixture.reshape(head_count * tile_count, 2, per_video...  15.8 us
    pallas_call x1, Pallas kernels, pack_projected(): pl.pallas_call(_qkv_kernel, grid=(head_count,), in_specs=[pl.BlockSpec((t...  8.21 us
    pallas_call x1, Pallas kernels, cross_partial(): pl.pallas_call(_cross_kernel, in_specs=[pl.BlockSpec(memory_space=pltpu.S...  5.22 us
    all_to_all x1, starting transfers between devices, local(): lax.all_to_all(copies, ('head', 'tile'), split_axis=0, concat_axis=0, til...  4.9 us
    all_to_all x1, starting transfers between devices, local(): lax.all_to_all(partial.reshape(head_count * tile_count, 2, per_video * mo...  4.75 us
  transfers between devices with their start and end apart: 2, of which 2 were waited for; matrix products, arithmetic and copies ran while one was open for 1% of the time, Pallas kernels for 0%

profile of v19, /device:TPU:1, one launch (start us, length us, event | category | flops | bytes accessed | tf_op | source)
XLA Modules:
  0.0 140.8 jit_solution(1901096020063801618)
XLA Ops:
  0.7 0.8 fusion.24
  2.0 1.2 slice_bitcast_fusion.1
  4.1 1.0 reshape.106.x_ref
  5.2 0.6 pad_maximum_fusion.3.gain_ref
  5.9 0.3 fusion.29
  6.2 0.7 pad_maximum_fusion.1
  6.9 8.2 %shard_map.185 = bf16[4,96,1152]{2,1,0:T(8,128)(2,1)} custom-call(bf16[96,1536]{1,0:T(8,128)(2,1)} %reshape.106.x_ref, bf16[1536,4608]{1,0:T(8,128)(2,1)} %wv_ref.1, bf16[1536,4608]{1,0:T(8,128)(2,1)} %wv_ref.1, bf16[1536,4608]{1,0:T(8,128)(2,1)} %wv_ref.1, f32[96,128]{1,0:T(8,128)} %get-tuple-element.21.cos_ref, f32[96,128]{1,0:T(8,128)} %get-tuple-element.22.sin_ref, ...), custom_call_target="tpu_custom_call" | custom-call | flops 1358954496 | bytes 15925248 | tf_op jit(solution)/shard_map/pallas_call | solution.py:195
  15.1 3.1 %reshape_reshape.3 = bf16[128,2,1728]{2,1,0:T(2,128)(2,1)S(1)} reshape(bf16[4,96,1152]{2,1,0:T(8,128)(2,1)} %shard_map.185) | data formatting | bytes 1769472 | tf_op jit(solution)/shard_map/reshape;reshape | solution.py:250
  18.2 29.1 %all_to_all.20 = bf16[128,2,1728]{2,1,0:T(2,128)(2,1)S(1)} all-to-all(bf16[128,2,1728]{2,1,0:T(2,128)(2,1)S(1)} %reshape_reshape.3), channel_id=1, replica_groups=mesh['head'=4,'tile'=32] {'head','tile'}, dimensions={0} | all-to-all | bytes 1769472 | tf_op jit(solution)/shard_map/all_to_all | solution.py:249
  47.3 2.2 %reshape.107.x_ref = bf16[384,1152]{1,0:T(8,128)(2,1)} reshape(bf16[128,2,1728]{2,1,0:T(2,128)(2,1)S(1)} %all_to_all.20) | data formatting | bytes 1769472 | tf_op jit(solution)/shard_map/reshape | solution.py:256
  49.5 2.7 %shard_map.186 = bf16[384,384]{1,0:T(8,128)(2,1)} custom-call(bf16[384,1152]{1,0:T(8,128)(2,1)} %reshape.107.x_ref), custom_call_target="tpu_custom_call" | custom-call | flops 226492416 | bytes 1179648 | tf_op jit(solution)/shard_map/pallas_call | solution.py:91
  52.2 1.4 reshape.108
  53.5 15.8 %all_to_all.21 = bf16[128,2,576]{2,1,0:T(2,128)(2,1)S(1)} all-to-all(bf16[128,2,576]{2,1,0:T(2,128)(2,1)S(1)} %reshape.108), channel_id=1, replica_groups=mesh['head'=4,'tile'=32] {'head','tile'}, dimensions={0} | all-to-all | bytes 589824 | tf_op jit(solution)/shard_map/all_to_all | solution.py:257
  69.3 0.5 reshape.109
  69.8 0.3 copy.30
  70.2 3.3 %fusion.32 = (f32[32,3]{0,1:T(4,128)S(1)}, f32[32,3,1536]{2,0,1:T(8,128)S(1)}) fusion(bf16[32,3,1536]{2,0,1:T(8,128)(2,1)S(1)} %dot_general.8, bf16[1536,1536]{1,0:T(8,128)(2,1)} %param.28, f32[32,1536]{1,0:T(8,128)S(1)} %get-tuple-element.8, bf16[32,3,1536]{2,0,1:T(8,128)(2,1)S(1)} %copy-done.3), kind=kOutput, calls=%fused_computation.65 | convolution fusion | flops 453574560 | bytes 6095232 | tf_op jit(solution)/shard_map/dot_general | solution.py:269
  74.2 0.3 broadcast_in_dim.4
  74.6 1.6 %broadcast_in_dim.5 = bf16[4,32,2,2304]{3,2,1,0:T(2,128)(2,1)} broadcast(bf16[32,2,2304]{2,1,0:T(2,128)(2,1)S(1)} %broadcast_in_dim.4), dimensions={1,2,3} | broadcast | bytes 1474560 | tf_op jit(solution)/shard_map/broadcast_in_dim | solution.py:275
  76.2 4.9 %all-to-all-start.2 = ((bf16[128,2,2304]{2,1,0:T(2,128)(2,1)}), bf16[128,2,2304]{2,1,0:T(2,128)(2,1)S(1)}, u32[]{:S(2)}, u32[]{:S(2)}) async-start(bf16[128,2,2304]{2,1,0:T(2,128)(2,1)} %bitcast.5), calls=%async_computation.2 | async-start | bytes 2359296 | tf_op jit(solution)/shard_map/all_to_all | solution.py:278
  81.1 0.6 reshape.112.gain_ref
  82.4 19.4 %all-to-all-done.2 = bf16[128,2,2304]{2,1,0:T(2,128)(2,1)S(1)} async-done(((bf16[128,2,2304]{2,1,0:T(2,128)(2,1)}), bf16[128,2,2304]{2,1,0:T(2,128)(2,1)S(1)}, u32[]{:S(2)}, u32[]{:S(2)}) %all-to-all-start.2) | async-done | bytes 1179680 | tf_op jit(solution)/shard_map/all_to_all | solution.py:278
  101.8 1.6 %reshape.111.x_ref = bf16[384,1536]{1,0:T(8,128)(2,1)} reshape(bf16[128,2,2304]{2,1,0:T(2,128)(2,1)S(1)} %all-to-all-done.2) | data formatting | bytes 2359296 | tf_op jit(solution)/shard_map/reshape | solution.py:279
  103.4 5.2 %shard_map.187 = bf16[384,1536]{1,0:T(8,128)(2,1)} custom-call(s32[1]{0:T(128)S(6)} %copy.43.length_ref, bf16[384,1536]{1,0:T(8,128)(2,1)} %reshape.111.x_ref, bf16[1536,384]{1,0:T(8,128)(2,1)} %wq_ref.3, f32[1,384]{1,0:T(1,128)} %reshape.112.gain_ref, bf16[512,384]{1,0:T(8,128)(2,1)S(1)} %bitcast.30, bf16[512,384]{1,0:T(8,128)(2,1)S(1)} %bitcast.31, ...), custom_call_target="tpu_custom_call" | custom-call | flops 1207959552 | bytes 5505024 | tf_op jit(solution)/shard_map/pallas_call | solution.py:137
  108.6 2.7 %reshape.113 = bf16[128,2,2304]{2,1,0:T(2,128)(2,1)} reshape(bf16[384,1536]{1,0:T(8,128)(2,1)} %shard_map.187) | data formatting | bytes 2359296 | tf_op jit(solution)/shard_map/reshape | solution.py:284
  111.3 4.8 %all-to-all-start.3 = ((bf16[128,2,2304]{2,1,0:T(2,128)(2,1)}), bf16[128,2,2304]{2,1,0:T(2,128)(2,1)S(1)}, u32[]{:S(2)}, u32[]{:S(2)}) async-start(bf16[128,2,2304]{2,1,0:T(2,128)(2,1)} %reshape.113), calls=%async_computation.3 | async-start | bytes 2359296 | tf_op jit(solution)/shard_map/all_to_all | solution.py:283
  116.1 0.3 fusion.31
  116.4 20.3 %all-to-all-done.3 = bf16[128,2,2304]{2,1,0:T(2,128)(2,1)S(1)} async-done(((bf16[128,2,2304]{2,1,0:T(2,128)(2,1)}), bf16[128,2,2304]{2,1,0:T(2,128)(2,1)S(1)}, u32[]{:S(2)}, u32[]{:S(2)}) %all-to-all-start.3) | async-done | bytes 1179680 | tf_op jit(solution)/shard_map/all_to_all | solution.py:283
  136.7 1.6 %reduce_sum.70 = bf16[32,2,2304]{2,1,0:T(2,128)(2,1)S(1)} reduce(bf16[4,32,2,2304]{3,2,1,0:T(2,128)(2,1)S(1)} %bitcast.32, bf16[]{:T(256)} %constant.66.clone.1), dimensions={0}, to_apply=%region_4.5 | reduce | flops 442368 | bytes 1474562 | tf_op jit(solution)/shard_map/reduce_sum | solution.py:291
  138.4 0.3 reshape.115
  138.7 0.3 fusion.28
  139.0 0.9 multiply_reduce_fusion
  139.9 0.9 fusion.8
  (49 shorter events, 2.5 us)
Async XLA Ops:
  0.6 139.3 %copy-start = (bf16[1536,64]{0,1:T(8,128)(2,1)S(1)}, bf16[1536,64]{0,1:T(8,128)(2,1)}, u32[]{:S(2)}) copy-start(bf16[1536,64]{0,1:T(8,128)(2,1)} %param.35) | copy-start | bytes 589828
  0.6 2.6 %copy-start.3 = (bf16[32,3,1536]{2,0,1:T(8,128)(2,1)S(1)}, bf16[32,3,1536]{2,0,1:T(8,128)(2,1)}, u32[]{:S(2)}) copy-start(bf16[32,3,1536]{2,0,1:T(8,128)(2,1)} %param.18) | copy-start | bytes 884740
  3.6 1.5 %copy-start.7 = (f32[1536]{0:T(1024)S(1)}, f32[1536]{0:T(1024)}, u32[]{:S(2)}) copy-start(f32[1536]{0:T(1024)} %param.27) | copy-start | bytes 18436
  3.6 1.5 %copy-start.8 = (f32[1536]{0:T(1024)S(1)}, f32[1536]{0:T(1024)}, u32[]{:S(2)}) copy-start(f32[1536]{0:T(1024)} %param.26) | copy-start | bytes 18436
  70.2 3.6 %copy-start.6 = (f32[1536]{0:T(1024)S(1)}, f32[1536]{0:T(1024)}, u32[]{:S(2)}) copy-start(f32[1536]{0:T(1024)} %param.29) | copy-start | bytes 18436
  76.2 4.9 %copy-start.9 = (f32[384]{0:T(512)S(1)}, f32[384]{0:T(512)}, u32[]{:S(2)}) copy-start(f32[384]{0:T(512)} %param.31) | copy-start | bytes 4612
  76.2 25.6 %all-to-all-start.2 = ((bf16[128,2,2304]{2,1,0:T(2,128)(2,1)}), bf16[128,2,2304]{2,1,0:T(2,128)(2,1)S(1)}, u32[]{:S(2)}, u32[]{:S(2)}) async-start(bf16[128,2,2304]{2,1,0:T(2,128)(2,1)} %bitcast.5), calls=%async_computation.2 | async-start | bytes 2359296 | tf_op jit(solution)/shard_map/all_to_all | solution.py:278
  82.3 21.1 %copy-start.1 = (bf16[1,512,384]{2,1,0:T(8,128)(2,1)S(1)}, bf16[1,512,384]{2,1,0:T(8,128)(2,1)}, u32[]{:S(2)}) copy-start(bf16[1,512,384]{2,1,0:T(8,128)(2,1)} %param.32) | copy-start | bytes 1179652
  82.3 21.1 %copy-start.2 = (bf16[1,512,384]{2,1,0:T(8,128)(2,1)S(1)}, bf16[1,512,384]{2,1,0:T(8,128)(2,1)}, u32[]{:S(2)}) copy-start(bf16[1,512,384]{2,1,0:T(8,128)(2,1)} %param.33) | copy-start | bytes 1179652
  111.3 4.8 %copy-start.4 = (f32[32,2,1536]{2,1,0:T(2,128)S(1)}, f32[32,2,1536]{2,1,0:T(2,128)}, u32[]{:S(2)}) copy-start(f32[32,2,1536]{2,1,0:T(2,128)} %param.23) | copy-start | bytes 1179652
  111.3 25.5 %all-to-all-start.3 = ((bf16[128,2,2304]{2,1,0:T(2,128)(2,1)}), bf16[128,2,2304]{2,1,0:T(2,128)(2,1)S(1)}, u32[]{:S(2)}, u32[]{:S(2)}) async-start(bf16[128,2,2304]{2,1,0:T(2,128)(2,1)} %reshape.113), calls=%async_computation.3 | async-start | bytes 2359296 | tf_op jit(solution)/shard_map/all_to_all | solution.py:283
  138.7 1.2 copy-start.5
  138.7 1.2 copy-start.10

commit v20 on v19

--- a/solution.py
+++ b/solution.py
@@ -153,7 +153,7 @@
         cross_q_gain.reshape(1, group_width),
         pltpu.with_memory_space_constraint(keys_own, pltpu.VMEM),
         pltpu.with_memory_space_constraint(values_own, pltpu.VMEM),
-        cross_wo,
+        pltpu.with_memory_space_constraint(cross_wo, pltpu.VMEM),
     )
 
 

time: 141 us -> 143 us (1.014)
  no operation moved by 1% of the time
where the time goes in v20:
time: 143 us; the launch traced here: 142 us
  blocking collectives  44.9 us (31%)
  waiting for transfers between devices  39.5 us (28%)
  local copies, waits for them, and re-layouts  18.1 us (13%)
  Pallas kernels  15.8 us (11%)
  starting transfers between devices  10.6 us (7%)
  other arithmetic  7.53 us (5%)
  matrix products  4.24 us (3%)
  between operations  1.6 us (1%)
    all_to_all x1, blocking collectives, local(): lax.all_to_all(packed.reshape(head_count * videos, 2, per_video * 3 * gro...  29.1 us
    all_to_all x1, waiting for transfers between devices, local(): lax.all_to_all(partial.reshape(head_count * tile_count, 2, per_video * mo...  20.3 us
    all_to_all x1, waiting for transfers between devices, local(): lax.all_to_all(copies, ('head', 'tile'), split_axis=0, concat_axis=0, til...  19.1 us
    all_to_all x1, blocking collectives, local(): lax.all_to_all(own_mixture.reshape(head_count * tile_count, 2, per_video...  15.8 us
    pallas_call x1, Pallas kernels, pack_projected(): pl.pallas_call(_qkv_kernel, grid=(head_count,), in_specs=[pl.BlockSpec((t...  8.22 us
    all_to_all x1, starting transfers between devices, local(): lax.all_to_all(copies, ('head', 'tile'), split_axis=0, concat_axis=0, til...  5.9 us
    pallas_call x1, Pallas kernels, cross_partial(): pl.pallas_call(_cross_kernel, in_specs=[pl.BlockSpec(memory_space=pltpu.S...  4.83 us
    all_to_all x1, starting transfers between devices, local(): lax.all_to_all(partial.reshape(head_count * tile_count, 2, per_video * mo...  4.75 us
  transfers between devices with their start and end apart: 2, of which 2 were waited for; matrix products, arithmetic and copies ran while one was open for 1% of the time, Pallas kernels for 0%

profile of v20, /device:TPU:1, one launch (start us, length us, event | category | flops | bytes accessed | tf_op | source)
XLA Modules:
  0.0 142.2 jit_solution(17998891272154433339)
XLA Ops:
  0.7 0.8 fusion.24
  2.0 1.2 slice_bitcast_fusion.1
  4.1 1.0 reshape.106.x_ref
  5.2 0.6 pad_maximum_fusion.3.gain_ref
  5.9 0.3 fusion.29
  6.2 0.7 pad_maximum_fusion.1
  6.9 8.2 %shard_map.185 = bf16[4,96,1152]{2,1,0:T(8,128)(2,1)} custom-call(bf16[96,1536]{1,0:T(8,128)(2,1)} %reshape.106.x_ref, bf16[1536,4608]{1,0:T(8,128)(2,1)} %wv_ref.1, bf16[1536,4608]{1,0:T(8,128)(2,1)} %wv_ref.1, bf16[1536,4608]{1,0:T(8,128)(2,1)} %wv_ref.1, f32[96,128]{1,0:T(8,128)} %get-tuple-element.21.cos_ref, f32[96,128]{1,0:T(8,128)} %get-tuple-element.22.sin_ref, ...), custom_call_target="tpu_custom_call" | custom-call | flops 1358954496 | bytes 15925248 | tf_op jit(solution)/shard_map/pallas_call | solution.py:195
  15.1 3.1 %reshape_reshape.3 = bf16[128,2,1728]{2,1,0:T(2,128)(2,1)S(1)} reshape(bf16[4,96,1152]{2,1,0:T(8,128)(2,1)} %shard_map.185) | data formatting | bytes 1769472 | tf_op jit(solution)/shard_map/reshape;reshape | solution.py:250
  18.2 29.1 %all_to_all.20 = bf16[128,2,1728]{2,1,0:T(2,128)(2,1)S(1)} all-to-all(bf16[128,2,1728]{2,1,0:T(2,128)(2,1)S(1)} %reshape_reshape.3), channel_id=1, replica_groups=mesh['head'=4,'tile'=32] {'head','tile'}, dimensions={0} | all-to-all | bytes 1769472 | tf_op jit(solution)/shard_map/all_to_all | solution.py:249
  47.2 2.2 %reshape.107.x_ref = bf16[384,1152]{1,0:T(8,128)(2,1)} reshape(bf16[128,2,1728]{2,1,0:T(2,128)(2,1)S(1)} %all_to_all.20) | data formatting | bytes 1769472 | tf_op jit(solution)/shard_map/reshape | solution.py:256
  49.4 2.7 %shard_map.186 = bf16[384,384]{1,0:T(8,128)(2,1)} custom-call(bf16[384,1152]{1,0:T(8,128)(2,1)} %reshape.107.x_ref), custom_call_target="tpu_custom_call" | custom-call | flops 226492416 | bytes 1179648 | tf_op jit(solution)/shard_map/pallas_call | solution.py:91
  52.2 1.4 reshape.108
  53.5 15.8 %all_to_all.21 = bf16[128,2,576]{2,1,0:T(2,128)(2,1)S(1)} all-to-all(bf16[128,2,576]{2,1,0:T(2,128)(2,1)S(1)} %reshape.108), channel_id=1, replica_groups=mesh['head'=4,'tile'=32] {'head','tile'}, dimensions={0} | all-to-all | bytes 589824 | tf_op jit(solution)/shard_map/all_to_all | solution.py:257
  69.3 0.5 reshape.109
  69.8 0.3 copy.30
  70.2 3.3 %fusion.32 = (f32[32,3]{0,1:T(4,128)S(1)}, f32[32,3,1536]{2,0,1:T(8,128)S(1)}) fusion(bf16[32,3,1536]{2,0,1:T(8,128)(2,1)S(1)} %dot_general.8, bf16[1536,1536]{1,0:T(8,128)(2,1)} %param.28, f32[32,1536]{1,0:T(8,128)S(1)} %get-tuple-element.8, bf16[32,3,1536]{2,0,1:T(8,128)(2,1)S(1)} %copy-done.4), kind=kOutput, calls=%fused_computation.65 | convolution fusion | flops 453574560 | bytes 6095232 | tf_op jit(solution)/shard_map/dot_general | solution.py:269
  74.2 0.3 broadcast_in_dim.4
  74.5 1.6 %broadcast_in_dim.5 = bf16[4,32,2,2304]{3,2,1,0:T(2,128)(2,1)} broadcast(bf16[32,2,2304]{2,1,0:T(2,128)(2,1)S(1)} %broadcast_in_dim.4), dimensions={1,2,3} | broadcast | bytes 1474560 | tf_op jit(solution)/shard_map/broadcast_in_dim | solution.py:275
  76.2 5.9 %all-to-all-start.2 = ((bf16[128,2,2304]{2,1,0:T(2,128)(2,1)}), bf16[128,2,2304]{2,1,0:T(2,128)(2,1)}, u32[]{:S(2)}, u32[]{:S(2)}) async-start(bf16[128,2,2304]{2,1,0:T(2,128)(2,1)} %bitcast.5), calls=%async_computation.2 | async-start | bytes 2359296 | tf_op jit(solution)/shard_map/all_to_all | solution.py:278
  82.1 0.6 reshape.112.gain_ref
  83.4 19.1 %all-to-all-done.2 = bf16[128,2,2304]{2,1,0:T(2,128)(2,1)} async-done(((bf16[128,2,2304]{2,1,0:T(2,128)(2,1)}), bf16[128,2,2304]{2,1,0:T(2,128)(2,1)}, u32[]{:S(2)}, u32[]{:S(2)}) %all-to-all-start.2) | async-done | bytes 1179680 | tf_op jit(solution)/shard_map/all_to_all | solution.py:278
  102.5 2.7 %reshape.111.x_ref = bf16[384,1536]{1,0:T(8,128)(2,1)} reshape(bf16[128,2,2304]{2,1,0:T(2,128)(2,1)} %all-to-all-done.2) | data formatting | bytes 2359296 | tf_op jit(solution)/shard_map/reshape | solution.py:279
  105.2 4.8 %shard_map.187 = bf16[384,1536]{1,0:T(8,128)(2,1)} custom-call(s32[1]{0:T(128)S(6)} %copy.43.length_ref, bf16[384,1536]{1,0:T(8,128)(2,1)} %reshape.111.x_ref, bf16[1536,384]{1,0:T(8,128)(2,1)} %wq_ref.3, f32[1,384]{1,0:T(1,128)} %reshape.112.gain_ref, bf16[512,384]{1,0:T(8,128)(2,1)S(1)} %bitcast.30, bf16[512,384]{1,0:T(8,128)(2,1)S(1)} %bitcast.31, ...), custom_call_target="tpu_custom_call" | custom-call | flops 1207959552 | bytes 5505024 | tf_op jit(solution)/shard_map/pallas_call | solution.py:137
  110.0 2.7 %reshape.113 = bf16[128,2,2304]{2,1,0:T(2,128)(2,1)} reshape(bf16[384,1536]{1,0:T(8,128)(2,1)} %shard_map.187) | data formatting | bytes 2359296 | tf_op jit(solution)/shard_map/reshape | solution.py:284
  112.7 4.7 %all-to-all-start.3 = ((bf16[128,2,2304]{2,1,0:T(2,128)(2,1)}), bf16[128,2,2304]{2,1,0:T(2,128)(2,1)S(1)}, u32[]{:S(2)}, u32[]{:S(2)}) async-start(bf16[128,2,2304]{2,1,0:T(2,128)(2,1)} %reshape.113), calls=%async_computation.3 | async-start | bytes 2359296 | tf_op jit(solution)/shard_map/all_to_all | solution.py:283
  117.4 0.3 fusion.31
  117.8 20.3 %all-to-all-done.3 = bf16[128,2,2304]{2,1,0:T(2,128)(2,1)S(1)} async-done(((bf16[128,2,2304]{2,1,0:T(2,128)(2,1)}), bf16[128,2,2304]{2,1,0:T(2,128)(2,1)S(1)}, u32[]{:S(2)}, u32[]{:S(2)}) %all-to-all-start.3) | async-done | bytes 1179680 | tf_op jit(solution)/shard_map/all_to_all | solution.py:283
  138.1 1.6 %reduce_sum.70 = bf16[32,2,2304]{2,1,0:T(2,128)(2,1)S(1)} reduce(bf16[4,32,2,2304]{3,2,1,0:T(2,128)(2,1)S(1)} %bitcast.32, bf16[]{:T(256)} %constant.66.clone.1), dimensions={0}, to_apply=%region_4.5 | reduce | flops 442368 | bytes 1474562 | tf_op jit(solution)/shard_map/reduce_sum | solution.py:291
  139.7 0.3 reshape.115
  140.1 0.3 fusion.28
  140.4 0.9 multiply_reduce_fusion
  141.3 0.9 fusion.8
  (51 shorter events, 2.5 us)
Async XLA Ops:
  0.6 140.6 %copy-start = (bf16[1536,64]{0,1:T(8,128)(2,1)S(1)}, bf16[1536,64]{0,1:T(8,128)(2,1)}, u32[]{:S(2)}) copy-start(bf16[1536,64]{0,1:T(8,128)(2,1)} %param.35) | copy-start | bytes 589828
  0.6 2.6 %copy-start.4 = (bf16[32,3,1536]{2,0,1:T(8,128)(2,1)S(1)}, bf16[32,3,1536]{2,0,1:T(8,128)(2,1)}, u32[]{:S(2)}) copy-start(bf16[32,3,1536]{2,0,1:T(8,128)(2,1)} %param.18) | copy-start | bytes 884740
  3.6 1.5 %copy-start.8 = (f32[1536]{0:T(1024)S(1)}, f32[1536]{0:T(1024)}, u32[]{:S(2)}) copy-start(f32[1536]{0:T(1024)} %param.27) | copy-start | bytes 18436
  3.6 1.5 %copy-start.9 = (f32[1536]{0:T(1024)S(1)}, f32[1536]{0:T(1024)}, u32[]{:S(2)}) copy-start(f32[1536]{0:T(1024)} %param.26) | copy-start | bytes 18436
  70.2 3.6 %copy-start.7 = (f32[1536]{0:T(1024)S(1)}, f32[1536]{0:T(1024)}, u32[]{:S(2)}) copy-start(f32[1536]{0:T(1024)} %param.29) | copy-start | bytes 18436
  76.2 5.9 %copy-start.10 = (f32[384]{0:T(512)S(1)}, f32[384]{0:T(512)}, u32[]{:S(2)}) copy-start(f32[384]{0:T(512)} %param.31) | copy-start | bytes 4612
  76.2 26.3 %all-to-all-start.2 = ((bf16[128,2,2304]{2,1,0:T(2,128)(2,1)}), bf16[128,2,2304]{2,1,0:T(2,128)(2,1)}, u32[]{:S(2)}, u32[]{:S(2)}) async-start(bf16[128,2,2304]{2,1,0:T(2,128)(2,1)} %bitcast.5), calls=%async_computation.2 | async-start | bytes 2359296 | tf_op jit(solution)/shard_map/all_to_all | solution.py:278
  83.3 21.8 %copy-start.1 = (bf16[384,1536]{1,0:T(8,128)(2,1)S(1)}, bf16[384,1536]{1,0:T(8,128)(2,1)}, u32[]{:S(2)}) copy-start(bf16[384,1536]{1,0:T(8,128)(2,1)} %wo_ref.1) | copy-start | bytes 3538948
  83.3 21.8 %copy-start.2 = (bf16[1,512,384]{2,1,0:T(8,128)(2,1)S(1)}, bf16[1,512,384]{2,1,0:T(8,128)(2,1)}, u32[]{:S(2)}) copy-start(bf16[1,512,384]{2,1,0:T(8,128)(2,1)} %param.32) | copy-start | bytes 1179652
  83.4 21.8 %copy-start.3 = (bf16[1,512,384]{2,1,0:T(8,128)(2,1)S(1)}, bf16[1,512,384]{2,1,0:T(8,128)(2,1)}, u32[]{:S(2)}) copy-start(bf16[1,512,384]{2,1,0:T(8,128)(2,1)} %param.33) | copy-start | bytes 1179652
  112.7 4.8 %copy-start.5 = (f32[32,2,1536]{2,1,0:T(2,128)S(1)}, f32[32,2,1536]{2,1,0:T(2,128)}, u32[]{:S(2)}) copy-start(f32[32,2,1536]{2,1,0:T(2,128)} %param.23) | copy-start | bytes 1179652
  112.7 25.5 %all-to-all-start.3 = ((bf16[128,2,2304]{2,1,0:T(2,128)(2,1)}), bf16[128,2,2304]{2,1,0:T(2,128)(2,1)S(1)}, u32[]{:S(2)}, u32[]{:S(2)}) async-start(bf16[128,2,2304]{2,1,0:T(2,128)(2,1)} %reshape.113), calls=%async_computation.3 | async-start | bytes 2359296 | tf_op jit(solution)/shard_map/all_to_all | solution.py:283
  140.1 1.2 copy-start.6
  140.1 1.2 copy-start.11
